TPU v7x, 256 devices: a whole 4x4x8 slice. The times are simulated.
256 devices in a mesh: grp: 4 (over y), ex: 8 (over x, core), tp: 8 (over z).
Axes of the slice: x: 4, y: 4, z: 8, core: 2. Of those that a mesh axis runs over, the one named last changes fastest.
Arguments:
- residual: bfloat16 [512, 2, 6144], P(('grp', 'ex'), None, 'tp'), may hold values from -34 to 34
- query_new: bfloat16 [512, 2, 6144], P(('grp', 'ex'), None, 'tp'), may hold values from -5 to 5
- key_new: bfloat16 [512, 2, 1024], P(('grp', 'ex'), None, 'tp'), may hold values from -8 to 8
- value_new: bfloat16 [512, 2, 1024], P(('grp', 'ex'), None, 'tp'), may hold values from -12 to 12
- key_cache: bfloat16 [512, 8, 512, 128], P(('grp', 'ex'), 'tp'), may hold values from -5 to 5
- value_cache: bfloat16 [512, 8, 512, 128], P(('grp', 'ex'), 'tp'), may hold values from -12 to 12
- lengths: int32 [512], P(('grp', 'ex')), may hold values from 128 to 512, as said below
- norm_gain: bfloat16 [6144], P('tp'), may hold values from 0.099609375 to 1.8984375
- router: float32 [6144, 8], P('tp'), may hold values from -0.078125 to 0.078125
- routes: int32 [512, 2, 2], P(('grp', 'ex')), may hold values from 0 to 7, all different within a row; in each aligned block of 32 rows (0 to 31, 32 to 63, ..., all dimensions but the last counted through in order) at most 16 rows name the same one
- w_gate: bfloat16 [8, 6144, 8192], P('ex', None, ('grp', 'tp')), may hold values from -0.078125 to 0.078125
- w_up: bfloat16 [8, 6144, 8192], P('ex', None, ('grp', 'tp')), may hold values from -0.078125 to 0.078125
- w_down: bfloat16 [8, 8192, 6144], P('ex', ('grp', 'tp')), may hold values from -0.125 to 0.125
Outputs:
- attended: bfloat16 [512, 2, 6144], P(('grp', 'ex'), None, 'tp')
- expert_mix: bfloat16 [512, 2, 6144], P(('grp', 'ex'), None, 'tp')
Inputs may be any that keep to these rules, and one draw needn't show every extreme that they name: `routes`: over the rows of one device (aligned blocks of 32 rows, environments then steps) no expert is named more than 16 times, and in some blocks one is named exactly 16 times; a row's two experts differ. `lengths`: some environment's cache is full.
All inputs are finite; a program needn't handle non-finite values.
Results may differ from a plain program's by a relative error of at most 0.023.
Values may be sent and summed in bfloat16 or wider, within the bound.
No kernel may reach another device: no remote copies, remote signals or barrier semaphores. Data moves between devices by JAX's collectives and lax.ppermute only.
A program may use at most 128 MiB of HBM per device.

v0:
```python
import jax
import jax.numpy as jnp
from jax import lax
from jax.sharding import PartitionSpec as P

CAP = 16


def attend(query_new, key_new, value_new, key_cache, value_cache, lengths):
    env_count, step_count, feature_count = query_new.shape
    kv_count = key_cache.shape[1]
    context = key_cache.shape[2]
    head_dim = key_cache.shape[3]
    group_size = feature_count // (kv_count * head_dim)
    queries = query_new.reshape(env_count, step_count, kv_count, group_size, head_dim)
    keys_now = key_new.reshape(env_count, step_count, kv_count, head_dim)
    values_now = value_new.reshape(env_count, step_count, kv_count, head_dim)
    score_scale = head_dim ** (-0.5)
    cached = (
        jnp.einsum("eskgd,ekcd->eskgc", queries, key_cache, preferred_element_type=jnp.float32)
        * score_scale
    )
    fresh_scores = (
        jnp.einsum("eskgd,etkd->eskgt", queries, keys_now, preferred_element_type=jnp.float32)
        * score_scale
    )
    valid_mask = (lax.broadcasted_iota(jnp.int32, (env_count, context), 1) < lengths[:, None])[
        :, None, None, None, :
    ]
    causal = (
        lax.broadcasted_iota(jnp.int32, (step_count, step_count), 1)
        <= lax.broadcasted_iota(jnp.int32, (step_count, step_count), 0)
    )[None, :, None, None, :]
    cached = jnp.where(valid_mask, cached, -1e30)
    fresh_scores = jnp.where(causal, fresh_scores, -1e30)
    row_top = jnp.maximum(jnp.max(cached, -1), jnp.max(fresh_scores, -1))[..., None]
    weight_cached = jnp.where(valid_mask, jnp.exp(cached - row_top), 0.0)
    weight_fresh = jnp.where(causal, jnp.exp(fresh_scores - row_top), 0.0)
    row_total = (jnp.sum(weight_cached, -1) + jnp.sum(weight_fresh, -1))[..., None]
    probs_cached = (weight_cached / row_total).astype(jnp.bfloat16)
    probs_fresh = (weight_fresh / row_total).astype(jnp.bfloat16)
    heads_out = jnp.einsum(
        "eskgc,ekcd->eskgd", probs_cached, value_cache, preferred_element_type=jnp.float32
    )
    heads_out = heads_out + jnp.einsum(
        "eskgt,etkd->eskgd", probs_fresh, values_now, preferred_element_type=jnp.float32
    )
    return heads_out.reshape(env_count, step_count, feature_count)


def ring_reduce_scatter(parts, axis, count, direction):
    me = lax.axis_index(axis)
    pairs = [(j, (j + direction) % count) for j in range(count)]

    def own(offset):
        chunk = (me - direction * offset) % count
        return lax.dynamic_index_in_dim(parts, chunk, 0, keepdims=False)

    total = own(1)
    for step in range(count - 1):
        arrived = lax.ppermute(total.astype(jnp.bfloat16), axis, pairs)
        total = arrived.astype(jnp.float32) + own(step + 2)
    return total


def both_ways(forward, backward, axis, joined):
    count = lax.axis_size(axis)
    return jnp.concatenate(
        [
            ring_reduce_scatter(forward, axis, count, 1),
            ring_reduce_scatter(backward, axis, count, -1),
        ],
        axis=joined,
    )


def exchange_sum(parts, axis):
    moved = lax.all_to_all(parts.astype(jnp.bfloat16), axis, 0, 0, tiled=True)
    return jnp.sum(moved.astype(jnp.float32), axis=0)


def per_device(
    residual,
    query_new,
    key_new,
    value_new,
    key_cache,
    value_cache,
    lengths,
    norm_gain,
    router,
    routes,
    w_gate,
    w_up,
    w_down,
):
    env_count, step_count, slice_width = residual.shape
    local_experts, width, hidden_local = w_gate.shape
    experts = router.shape[1]
    topk = routes.shape[2]
    group_count = lax.axis_size("grp")
    tensor_count = lax.axis_size("tp")
    owner_count = lax.axis_size("ex")
    row_count = env_count * step_count
    state = residual.astype(jnp.float32) + attend(
        query_new, key_new, value_new, key_cache, value_cache, lengths
    )
    attended = state.astype(jnp.bfloat16)
    squares = jnp.sum(state * state, -1)
    scaled = state * norm_gain.astype(jnp.float32)
    partial_logits = jnp.einsum("esd,dx->esx", scaled, router, precision=lax.Precision.HIGHEST)
    squares, logits = lax.psum((squares, partial_logits), "tp")
    root_mean = jnp.sqrt(squares / width + 1e-05)[..., None]
    logits = logits / root_mean
    normed = (scaled / root_mean).astype(jnp.bfloat16)
    expert_ids = lax.broadcasted_iota(jnp.int32, (1, 1, 1, experts), 3)
    picked_logits = jnp.sum(
        jnp.where(routes[..., None] == expert_ids, logits[:, :, None, :], 0.0), -1
    )
    first_gate = 1.0 / (1.0 + jnp.exp(picked_logits[..., 1] - picked_logits[..., 0]))
    second_gate = 1.0 - first_gate
    flat_routes = routes.reshape(row_count * topk)
    expert_hits = (flat_routes[:, None] == lax.broadcasted_iota(jnp.int32, (1, experts), 1)).astype(
        jnp.int32
    )
    earlier = jnp.cumsum(expert_hits, axis=0) - expert_hits
    slot_ids = jnp.sum(earlier * expert_hits, axis=1)
    targets = flat_routes * CAP + slot_ids
    slot_table = lax.broadcasted_iota(jnp.int32, (1, experts * CAP), 1)
    placed = (
        (targets[:, None] == slot_table)
        .astype(jnp.bfloat16)
        .reshape(row_count, topk, experts * CAP)
    )
    sender = jnp.sum(placed, axis=1)
    packed = jnp.einsum(
        "rs,rd->sd",
        sender,
        normed.reshape(row_count, slice_width),
        preferred_element_type=jnp.float32,
    )
    outgoing = packed.astype(jnp.bfloat16).reshape(experts, CAP, slice_width)
    received = lax.all_to_all(outgoing, "ex", split_axis=0, concat_axis=0, tiled=True)
    received = received.reshape(1, owner_count, local_experts, CAP, slice_width)
    pieces = lax.all_gather(received, ("grp", "tp"), axis=0, tiled=True)

    pieces = pieces.reshape(
        group_count, tensor_count, owner_count, local_experts, CAP, slice_width
    )
    gate_split = w_gate.reshape(local_experts, tensor_count, slice_width, hidden_local)
    up_split = w_up.reshape(local_experts, tensor_count, slice_width, hidden_local)
    gate_sums = jnp.einsum(
        "gtajcd,jtdf->jgacf", pieces, gate_split, preferred_element_type=jnp.float32
    )
    up_sums = jnp.einsum("gtajcd,jtdf->jgacf", pieces, up_split, preferred_element_type=jnp.float32)
    hidden = (jax.nn.silu(gate_sums) * up_sums).astype(jnp.bfloat16)
    down_split = w_down.reshape(local_experts, hidden_local, tensor_count, slice_width)
    owner_half = owner_count // 2
    group_half = group_count // 2
    tensor_half = tensor_count // 2

    def down(rows, columns, spec):
        return jnp.einsum(spec, rows, columns, preferred_element_type=jnp.float32)

    z_rows = hidden[:, :, :owner_half]
    y_rows = hidden[:, :, owner_half:]
    z_first = both_ways(
        down(z_rows[:, :group_half], down_split, "jgacf,jftd->tgajcd"),
        down(z_rows[:, group_half:], down_split, "jgacf,jftd->tgajcd"),
        "tp",
        0,
    )
    y_first = both_ways(
        down(y_rows, down_split[:, :, :tensor_half], "jgacf,jftd->gtajcd"),
        down(y_rows, down_split[:, :, tensor_half:], "jgacf,jftd->gtajcd"),
        "grp",
        0,
    )
    z_done = exchange_sum(z_first, "grp")
    y_done = exchange_sum(y_first, "tp")
    summed = jnp.concatenate([z_done, y_done], axis=0)
    returned = lax.all_to_all(
        summed.astype(jnp.bfloat16), "ex", split_axis=0, concat_axis=0, tiled=True
    )
    returned = returned.reshape(experts * CAP, slice_width)
    picked_rows = jnp.einsum("rks,sd->rkd", placed, returned, preferred_element_type=jnp.float32)
    picked_rows = picked_rows.reshape(env_count, step_count, topk, slice_width)
    expert_mix = (
        first_gate[..., None] * picked_rows[:, :, 0] + second_gate[..., None] * picked_rows[:, :, 1]
    )
    return (attended, expert_mix.astype(jnp.bfloat16))


def solution(mesh):
    return jax.shard_map(
        per_device,
        mesh=mesh,
        in_specs=(
            P(("grp", "ex"), None, "tp"),
            P(("grp", "ex"), None, "tp"),
            P(("grp", "ex"), None, "tp"),
            P(("grp", "ex"), None, "tp"),
            P(("grp", "ex"), "tp", None, None),
            P(("grp", "ex"), "tp", None, None),
            P(("grp", "ex")),
            P("tp"),
            P("tp", None),
            P(("grp", "ex"), None, None),
            P("ex", None, ("grp", "tp")),
            P("ex", None, ("grp", "tp")),
            P("ex", ("grp", "tp"), None),
        ),
        out_specs=(P(("grp", "ex"), None, "tp"), P(("grp", "ex"), None, "tp")),
        check_vma=False,
    )
```

profile of v0, /device:TPU:1, one launch (start us, length us, event | category | flops | bytes accessed | tf_op | source)
XLA Modules:
  0.0 255.1 jit_solution(11867714438750460552)
XLA Ops:
  7.2 0.9 copy.164
  8.9 0.7 iota_compare_fusion.3
  9.6 0.8 reshape.502
  10.4 2.5 fusion.84
  13.0 1.1 fusion.85
  16.0 18.3 %all-reduce = (f32[16,2]{0,1:T(2,128)S(1)}, f32[16,2,8]{0,2,1:T(8,128)}) all-reduce(f32[16,2]{0,1:T(2,128)S(1)} %multiply_reduce_fusion, f32[16,2,8]{0,2,1:T(8,128)S(1)} %fusion.66), channel_id=1, replica_groups=mesh['grp'=4,'ex'=8,'tp'=8] {'tp'}, use_global_device_ids=true, to_apply=%region_6.7 | all-reduce | flops 288 | bytes 2304 | tf_op jit(solution)/shard_map/psum | solution.py:112
  36.2 14.3 %all_to_all.20 = bf16[8,16,768]{2,1,0:T(8,128)(2,1)} all-to-all(bf16[8,16,768]{2,1,0:T(8,128)(2,1)S(1)} %bitcast.440), channel_id=1, replica_groups=mesh['grp'=4,'ex'=8,'tp'=8] {'ex'}, dimensions={0} | all-to-all | bytes 393216 | tf_op jit(solution)/shard_map/all_to_all | solution.py:143
  50.9 4.8 %copy.187 = bf16[1,256,6144]{1,2,0:T(8,128)(2,1)} copy(bf16[1,256,6144]{2,1,0:T(8,128)(2,1)} %param.25) | data formatting | bytes 6291456 | tf_op args[12]
  55.7 4.4 %copy.227 = bf16[32,8,8,768]{3,2,1,0:T(8,128)(2,1)} copy(bf16[32,8,8,768]{3,1,2,0:T(8,128)(2,1)} %bitcast.434) | data formatting | bytes 6291456
  60.2 74.4 %all-gather.3.cloned.1.call-done = bf16[256,16,768]{2,1,0:T(8,128)(2,1)} async-done(((bf16[8,16,768]{2,1,0:T(8,128)(2,1)}), bf16[256,16,768]{2,1,0:T(8,128)(2,1)}) %all-gather.3.cloned.1.call-update) | async-done | bytes 6291472 | tf_op jit(solution)/shard_map/all_gather | solution.py:145
  134.6 4.7 %convolution_bitcast_fusion.1 = f32[4,8,16,256]{3,2,1,0:T(8,128)S(1)} fusion(bf16[4,8,8,16,768]{4,3,2,1,0:T(8,128)(2,1)} %bitcast.445, bf16[8,768,256,1,1]{2,1,4,0,3:T(8,128)(2,1)S(1)} %bitcast.433), kind=kOutput, calls=%fused_computation.14 | convolution fusion | flops 1610612736 | bytes 9961472 | tf_op jit(solution)/shard_map/gtajcd,jtdf->jgacf/dot_general | solution.py:152
  139.3 0.8 copy-done.9
  140.1 1.8 fusion.24
  142.0 1.3 fusion.2
  143.3 1.3 fusion
  146.5 2.7 %collective-permute-start.7 = (bf16[2,4,1,16,768]{4,3,1,0,2:T(8,128)(2,1)S(1)}, bf16[2,4,1,16,768]{4,3,1,0,2:T(8,128)(2,1)S(1)}, u32[]{:S(2)}, u32[]{:S(2)}) collective-permute-start(bf16[2,4,1,16,768]{4,3,1,0,2:T(8,128)(2,1)S(1)} %fusion.60), channel_id=1, source_target_pairs={{0,7},{1,0},{2,1},{3,2},{4,3},{5,4},{6,5},{7,6},{8,15},{9,8},{10,9... | collective-permute-start | bytes 589832 | tf_op jit(solution)/shard_map/ppermute | solution.py:61
  149.6 2.7 %collective-permute-start.17 = (bf16[4,4,1,16,768]{4,3,0,1,2:T(8,128)(2,1)S(1)}, bf16[4,4,1,16,768]{4,3,0,1,2:T(8,128)(2,1)S(1)}, u32[]{:S(2)}, u32[]{:S(2)}) collective-permute-start(bf16[4,4,1,16,768]{4,3,0,1,2:T(8,128)(2,1)S(1)} %fusion.41), channel_id=1, source_target_pairs={{0,192},{64,0},{128,64},{192,128},{1,193},{65,1},{129,65},{193,129... | collective-permute-start | bytes 1179656 | tf_op jit(solution)/shard_map/ppermute | solution.py:61
  152.8 2.7 %collective-permute-start.8 = (bf16[2,4,1,16,768]{4,3,1,0,2:T(8,128)(2,1)S(1)}, bf16[2,4,1,16,768]{4,3,1,0,2:T(8,128)(2,1)S(1)}, u32[]{:S(2)}, u32[]{:S(2)}) collective-permute-start(bf16[2,4,1,16,768]{4,3,1,0,2:T(8,128)(2,1)S(1)} %fusion.54), channel_id=1, source_target_pairs={{0,7},{1,0},{2,1},{3,2},{4,3},{5,4},{6,5},{7,6},{8,15},{9,8},{10,9... | collective-permute-start | bytes 589832 | tf_op jit(solution)/shard_map/ppermute | solution.py:61
  155.5 3.2 %collective-permute-done.1 = bf16[2,4,1,16,768]{4,3,1,0,2:T(8,128)(2,1)S(1)} collective-permute-done((bf16[2,4,1,16,768]{4,3,1,0,2:T(8,128)(2,1)S(1)}, bf16[2,4,1,16,768]{4,3,1,0,2:T(8,128)(2,1)S(1)}, u32[]{:S(2)}, u32[]{:S(2)}) %collective-permute-start.1) | collective-permute-done | bytes 196640 | tf_op jit(solution)/shard_map/ppermute | solution.py:61
  158.9 2.7 %collective-permute-start.9 = (bf16[2,4,1,16,768]{4,3,1,0,2:T(8,128)(2,1)S(1)}, bf16[2,4,1,16,768]{4,3,1,0,2:T(8,128)(2,1)S(1)}, u32[]{:S(2)}, u32[]{:S(2)}) collective-permute-start(bf16[2,4,1,16,768]{4,3,1,0,2:T(8,128)(2,1)S(1)} %fusion.53), channel_id=1, source_target_pairs={{0,7},{1,0},{2,1},{3,2},{4,3},{5,4},{6,5},{7,6},{8,15},{9,8},{10,9... | collective-permute-start | bytes 589832 | tf_op jit(solution)/shard_map/ppermute | solution.py:61
  162.0 2.7 %collective-permute-start.18 = (bf16[4,4,1,16,768]{4,3,0,1,2:T(8,128)(2,1)S(1)}, bf16[4,4,1,16,768]{4,3,0,1,2:T(8,128)(2,1)S(1)}, u32[]{:S(2)}, u32[]{:S(2)}) collective-permute-start(bf16[4,4,1,16,768]{4,3,0,1,2:T(8,128)(2,1)S(1)} %fusion.35), channel_id=1, source_target_pairs={{0,192},{64,0},{128,64},{192,128},{1,193},{65,1},{129,65},{193,129... | collective-permute-start | bytes 1179656 | tf_op jit(solution)/shard_map/ppermute | solution.py:61
  164.9 2.7 %collective-permute-start.10 = (bf16[2,4,1,16,768]{4,3,1,0,2:T(8,128)(2,1)S(1)}, bf16[2,4,1,16,768]{4,3,1,0,2:T(8,128)(2,1)S(1)}, u32[]{:S(2)}, u32[]{:S(2)}) collective-permute-start(bf16[2,4,1,16,768]{4,3,1,0,2:T(8,128)(2,1)S(1)} %fusion.52), channel_id=1, source_target_pairs={{0,7},{1,0},{2,1},{3,2},{4,3},{5,4},{6,5},{7,6},{8,15},{9,8},{10,9... | collective-permute-start | bytes 589832 | tf_op jit(solution)/shard_map/ppermute | solution.py:61
  167.6 3.2 %collective-permute-done.3 = bf16[2,4,1,16,768]{4,3,1,0,2:T(8,128)(2,1)S(1)} collective-permute-done((bf16[2,4,1,16,768]{4,3,1,0,2:T(8,128)(2,1)S(1)}, bf16[2,4,1,16,768]{4,3,1,0,2:T(8,128)(2,1)S(1)}, u32[]{:S(2)}, u32[]{:S(2)}) %collective-permute-start.3) | collective-permute-done | bytes 196640 | tf_op jit(solution)/shard_map/ppermute | solution.py:61
  171.0 3.0 %collective-permute-start.11 = (bf16[2,4,1,16,768]{4,3,1,0,2:T(8,128)(2,1)S(1)}, bf16[2,4,1,16,768]{4,3,1,0,2:T(8,128)(2,1)S(1)}, u32[]{:S(2)}, u32[]{:S(2)}) collective-permute-start(bf16[2,4,1,16,768]{4,3,1,0,2:T(8,128)(2,1)S(1)} %fusion.51), channel_id=1, source_target_pairs={{0,7},{1,0},{2,1},{3,2},{4,3},{5,4},{6,5},{7,6},{8,15},{9,8},{10,9... | collective-permute-start | bytes 589832 | tf_op jit(solution)/shard_map/ppermute | solution.py:61
  174.2 0.9 fusion.34
  175.1 2.6 %collective-permute-start.19 = (bf16[4,4,1,16,768]{4,3,0,1,2:T(8,128)(2,1)}, bf16[4,4,1,16,768]{4,3,0,1,2:T(8,128)(2,1)}, u32[]{:S(2)}, u32[]{:S(2)}) collective-permute-start(bf16[4,4,1,16,768]{4,3,0,1,2:T(8,128)(2,1)} %fusion.34), channel_id=1, source_target_pairs={{0,192},{64,0},{128,64},{192,128},{1,193},{65,1},{129,65},{193,129... | collective-permute-start | bytes 1179656 | tf_op jit(solution)/shard_map/ppermute | solution.py:61
  178.0 3.3 %collective-permute-start.12 = (bf16[2,4,1,16,768]{4,3,1,0,2:T(8,128)(2,1)S(1)}, bf16[2,4,1,16,768]{4,3,1,0,2:T(8,128)(2,1)S(1)}, u32[]{:S(2)}, u32[]{:S(2)}) collective-permute-start(bf16[2,4,1,16,768]{4,3,1,0,2:T(8,128)(2,1)S(1)} %fusion.50), channel_id=1, source_target_pairs={{0,7},{1,0},{2,1},{3,2},{4,3},{5,4},{6,5},{7,6},{8,15},{9,8},{10,9... | collective-permute-start | bytes 589832 | tf_op jit(solution)/shard_map/ppermute | solution.py:61
  181.2 4.6 %collective-permute-done.5 = bf16[2,4,1,16,768]{4,3,1,0,2:T(8,128)(2,1)S(1)} collective-permute-done((bf16[2,4,1,16,768]{4,3,1,0,2:T(8,128)(2,1)S(1)}, bf16[2,4,1,16,768]{4,3,1,0,2:T(8,128)(2,1)S(1)}, u32[]{:S(2)}, u32[]{:S(2)}) %collective-permute-start.5) | collective-permute-done | bytes 196640 | tf_op jit(solution)/shard_map/ppermute | solution.py:61
  186.1 3.4 %collective-permute-start.13 = (bf16[2,4,1,16,768]{4,3,1,0,2:T(8,128)(2,1)S(1)}, bf16[2,4,1,16,768]{4,3,1,0,2:T(8,128)(2,1)S(1)}, u32[]{:S(2)}, u32[]{:S(2)}) collective-permute-start(bf16[2,4,1,16,768]{4,3,1,0,2:T(8,128)(2,1)S(1)} %fusion.49), channel_id=1, source_target_pairs={{0,7},{1,0},{2,1},{3,2},{4,3},{5,4},{6,5},{7,6},{8,15},{9,8},{10,9... | collective-permute-start | bytes 589832 | tf_op jit(solution)/shard_map/ppermute | solution.py:61
  189.4 0.8 fusion.36
  190.2 3.2 %collective-permute-done.6 = bf16[2,4,1,16,768]{4,3,1,0,2:T(8,128)(2,1)S(1)} collective-permute-done((bf16[2,4,1,16,768]{4,3,1,0,2:T(8,128)(2,1)S(1)}, bf16[2,4,1,16,768]{4,3,1,0,2:T(8,128)(2,1)S(1)}, u32[]{:S(2)}, u32[]{:S(2)}) %collective-permute-start.6) | collective-permute-done | bytes 196640 | tf_op jit(solution)/shard_map/ppermute | solution.py:61
  193.5 0.8 maximum_bitcast_fusion
  194.3 3.5 %all-to-all-start.1 = ((bf16[4,4,1,16,768]{4,3,1,2,0:T(8,128)(2,1)}), bf16[4,4,1,16,768]{4,3,1,2,0:T(8,128)(2,1)S(1)}, u32[]{:S(2)}, u32[]{:S(2)}) async-start(bf16[4,4,1,16,768]{4,3,1,2,0:T(8,128)(2,1)} %maximum_bitcast_fusion), calls=%async_computation.1 | async-start | bytes 786432 | tf_op jit(solution)/shard_map/all_to_all | solution.py:78
  197.8 1.3 fusion.33
  199.1 1.1 pad_maximum_fusion
  200.2 1.0 copy.190
  201.1 2.8 %all-to-all-done.1 = bf16[4,4,1,16,768]{4,3,1,2,0:T(8,128)(2,1)S(1)} async-done(((bf16[4,4,1,16,768]{4,3,1,2,0:T(8,128)(2,1)}), bf16[4,4,1,16,768]{4,3,1,2,0:T(8,128)(2,1)S(1)}, u32[]{:S(2)}, u32[]{:S(2)}) %all-to-all-start.1) | async-done | bytes 393248 | tf_op jit(solution)/shard_map/all_to_all | solution.py:78
  204.0 4.8 %all-to-all-start.2 = ((bf16[8,4,1,16,768]{4,3,1,2,0:T(8,128)(2,1)}), bf16[8,4,1,16,768]{4,3,1,2,0:T(8,128)(2,1)}, u32[]{:S(2)}, u32[]{:S(2)}) async-start(bf16[8,4,1,16,768]{4,3,1,2,0:T(8,128)(2,1)} %copy.190), calls=%async_computation.2 | async-start | bytes 1572864 | tf_op jit(solution)/shard_map/all_to_all | solution.py:78
  209.5 0.7 eq.100
  210.2 1.5 copy.193
  212.4 1.3 select_reduce_fusion.1
  213.7 0.7 reduce.7
  214.4 9.7 %all-to-all-done.2 = bf16[8,4,1,16,768]{4,3,1,2,0:T(8,128)(2,1)} async-done(((bf16[8,4,1,16,768]{4,3,1,2,0:T(8,128)(2,1)}), bf16[8,4,1,16,768]{4,3,1,2,0:T(8,128)(2,1)}, u32[]{:S(2)}, u32[]{:S(2)}) %all-to-all-start.2) | async-done | bytes 786464 | tf_op jit(solution)/shard_map/all_to_all | solution.py:78
  224.0 1.2 reduce.8
  225.3 1.6 pad_maximum_fusion.1
  226.9 14.6 %all-to-all-start.3 = ((bf16[8,1,16,768]{3,2,1,0:T(8,128)(2,1)}), bf16[8,1,16,768]{3,2,1,0:T(8,128)(2,1)S(1)}, u32[]{:S(2)}, u32[]{:S(2)}) async-start(bf16[8,1,16,768]{3,2,1,0:T(8,128)(2,1)} %pad_maximum_fusion.1), calls=%async_computation.3 | async-start | bytes 393216 | tf_op jit(solution)/shard_map/all_to_all | solution.py:182
  241.4 0.8 broadcast_subtract_fusion
  242.2 5.1 %all-to-all-done.3 = bf16[8,1,16,768]{3,2,1,0:T(8,128)(2,1)S(1)} async-done(((bf16[8,1,16,768]{3,2,1,0:T(8,128)(2,1)}), bf16[8,1,16,768]{3,2,1,0:T(8,128)(2,1)S(1)}, u32[]{:S(2)}, u32[]{:S(2)}) %all-to-all-start.3) | async-done | bytes 196640 | tf_op jit(solution)/shard_map/all_to_all | solution.py:182
  (106 shorter events, 11.1 us)
Async XLA Ops:
  7.2 127.4 %copy-start = (bf16[1,6144,256]{2,1,0:T(8,128)(2,1)S(1)}, bf16[1,6144,256]{2,1,0:T(8,128)(2,1)}, u32[]{:S(2)}) copy-start(bf16[1,6144,256]{2,1,0:T(8,128)(2,1)} %param.23) | copy-start | bytes 9437188
  7.2 7.4 %copy-start.11 = (bf16[16,2,128]{2,1,0:T(2,128)(2,1)S(1)}, bf16[16,2,128]{2,1,0:T(2,128)(2,1)}, u32[]{:S(2)}) copy-start(bf16[16,2,128]{2,1,0:T(2,128)(2,1)} %param.16) | copy-start | bytes 24580
  7.2 127.4 %all-gather.3.cloned.1.call-start = ((), (), s32[]{:S(2)}) async-start(), calls=%async_computation.4 | async-start | bytes 6488064 | tf_op jit(solution)/shard_map/all_gather | solution.py:145
  10.4 4.4 %copy-start.10 = (bf16[16,1,512,128]{3,2,1,0:T(8,128)(2,1)S(1)}, bf16[16,1,512,128]{3,2,1,0:T(8,128)(2,1)}, u32[]{:S(2)}) copy-start(bf16[16,1,512,128]{3,2,1,0:T(8,128)(2,1)} %param.18) | copy-start | bytes 6291460
  12.9 2.5 copy-start.7
  12.9 2.5 copy-start.4
  12.9 2.6 %copy-start.5 = (f32[768,8]{0,1:T(8,128)S(1)}, f32[768,8]{0,1:T(8,128)}, u32[]{:S(2)}) copy-start(f32[768,8]{0,1:T(8,128)} %param.21) | copy-start | bytes 73732
  34.3 21.4 %copy-start.6 = (f32[16,2]{0,1:T(2,128)}, f32[16,2]{0,1:T(2,128)S(1)}, u32[]{:S(2)}) copy-start(f32[16,2]{0,1:T(2,128)S(1)} %add_sqrt_fusion) | copy-start | bytes 388
  134.6 4.7 %copy-start.8 = (bf16[256,16,768]{2,1,0:T(8,128)(2,1)S(1)}, bf16[256,16,768]{2,1,0:T(8,128)(2,1)}, u32[]{:S(2)}) copy-start(bf16[256,16,768]{2,1,0:T(8,128)(2,1)} %all-gather.3.cloned.1.call-done) | copy-start | bytes 18874372
  134.6 5.5 %copy-start.9 = (bf16[1,6144,256]{2,1,0:T(8,128)(2,1)S(1)}, bf16[1,6144,256]{2,1,0:T(8,128)(2,1)}, u32[]{:S(2)}) copy-start(bf16[1,6144,256]{2,1,0:T(8,128)(2,1)} %param.24) | copy-start | bytes 9437188
  140.1 1.9 copy-start.1
  143.3 1.9 copy-start.2
  146.4 27.9 %copy-start.3 = (f32[4,4,16,4,768]{4,2,3,1,0:T(8,128)}, f32[4,4,16,4,768]{4,2,3,1,0:T(8,128)S(1)}, u32[]{:S(2)}) copy-start(f32[4,4,16,4,768]{4,2,3,1,0:T(8,128)S(1)} %fusion.8) | copy-start | bytes 9437188
  146.4 6.1 %collective-permute-start = (bf16[2,4,1,16,768]{4,3,1,0,2:T(8,128)(2,1)S(1)}, bf16[2,4,1,16,768]{4,3,1,0,2:T(8,128)(2,1)S(1)}, u32[]{:S(2)}, u32[]{:S(2)}) collective-permute-start(bf16[2,4,1,16,768]{4,3,1,0,2:T(8,128)(2,1)S(1)} %fusion.61), channel_id=1, source_target_pairs={{0,1},{1,2},{2,3},{3,4},{4,5},{5,6},{6,7},{7,0},{8,9},{9,10},{10,1... | collective-permute-start | bytes 589832 | tf_op jit(solution)/shard_map/ppermute | solution.py:61
  146.5 6.2 %collective-permute-start.7 = (bf16[2,4,1,16,768]{4,3,1,0,2:T(8,128)(2,1)S(1)}, bf16[2,4,1,16,768]{4,3,1,0,2:T(8,128)(2,1)S(1)}, u32[]{:S(2)}, u32[]{:S(2)}) collective-permute-start(bf16[2,4,1,16,768]{4,3,1,0,2:T(8,128)(2,1)S(1)} %fusion.60), channel_id=1, source_target_pairs={{0,7},{1,0},{2,1},{3,2},{4,3},{5,4},{6,5},{7,6},{8,15},{9,8},{10,9... | collective-permute-start | bytes 589832 | tf_op jit(solution)/shard_map/ppermute | solution.py:61
  149.3 12.3 %collective-permute-start.14 = (bf16[4,4,1,16,768]{4,3,0,1,2:T(8,128)(2,1)S(1)}, bf16[4,4,1,16,768]{4,3,0,1,2:T(8,128)(2,1)S(1)}, u32[]{:S(2)}, u32[]{:S(2)}) collective-permute-start(bf16[4,4,1,16,768]{4,3,0,1,2:T(8,128)(2,1)S(1)} %fusion.40), channel_id=1, source_target_pairs={{0,64},{64,128},{128,192},{192,0},{1,65},{65,129},{129,193},{193,1... | collective-permute-start | bytes 1179656 | tf_op jit(solution)/shard_map/ppermute | solution.py:61
  149.6 12.2 %collective-permute-start.17 = (bf16[4,4,1,16,768]{4,3,0,1,2:T(8,128)(2,1)S(1)}, bf16[4,4,1,16,768]{4,3,0,1,2:T(8,128)(2,1)S(1)}, u32[]{:S(2)}, u32[]{:S(2)}) collective-permute-start(bf16[4,4,1,16,768]{4,3,0,1,2:T(8,128)(2,1)S(1)} %fusion.41), channel_id=1, source_target_pairs={{0,192},{64,0},{128,64},{192,128},{1,193},{65,1},{129,65},{193,129... | collective-permute-start | bytes 1179656 | tf_op jit(solution)/shard_map/ppermute | solution.py:61
  152.6 6.1 %collective-permute-start.1 = (bf16[2,4,1,16,768]{4,3,1,0,2:T(8,128)(2,1)S(1)}, bf16[2,4,1,16,768]{4,3,1,0,2:T(8,128)(2,1)S(1)}, u32[]{:S(2)}, u32[]{:S(2)}) collective-permute-start(bf16[2,4,1,16,768]{4,3,1,0,2:T(8,128)(2,1)S(1)} %fusion.47), channel_id=1, source_target_pairs={{0,1},{1,2},{2,3},{3,4},{4,5},{5,6},{6,7},{7,0},{8,9},{9,10},{10,1... | collective-permute-start | bytes 589832 | tf_op jit(solution)/shard_map/ppermute | solution.py:61
  152.8 6.1 %collective-permute-start.8 = (bf16[2,4,1,16,768]{4,3,1,0,2:T(8,128)(2,1)S(1)}, bf16[2,4,1,16,768]{4,3,1,0,2:T(8,128)(2,1)S(1)}, u32[]{:S(2)}, u32[]{:S(2)}) collective-permute-start(bf16[2,4,1,16,768]{4,3,1,0,2:T(8,128)(2,1)S(1)} %fusion.54), channel_id=1, source_target_pairs={{0,7},{1,0},{2,1},{3,2},{4,3},{5,4},{6,5},{7,6},{8,15},{9,8},{10,9... | collective-permute-start | bytes 589832 | tf_op jit(solution)/shard_map/ppermute | solution.py:61
  158.8 5.9 %collective-permute-start.2 = (bf16[2,4,1,16,768]{4,3,1,0,2:T(8,128)(2,1)S(1)}, bf16[2,4,1,16,768]{4,3,1,0,2:T(8,128)(2,1)S(1)}, u32[]{:S(2)}, u32[]{:S(2)}) collective-permute-start(bf16[2,4,1,16,768]{4,3,1,0,2:T(8,128)(2,1)S(1)} %fusion.46), channel_id=1, source_target_pairs={{0,1},{1,2},{2,3},{3,4},{4,5},{5,6},{6,7},{7,0},{8,9},{9,10},{10,1... | collective-permute-start | bytes 589832 | tf_op jit(solution)/shard_map/ppermute | solution.py:61
  158.9 5.9 %collective-permute-start.9 = (bf16[2,4,1,16,768]{4,3,1,0,2:T(8,128)(2,1)S(1)}, bf16[2,4,1,16,768]{4,3,1,0,2:T(8,128)(2,1)S(1)}, u32[]{:S(2)}, u32[]{:S(2)}) collective-permute-start(bf16[2,4,1,16,768]{4,3,1,0,2:T(8,128)(2,1)S(1)} %fusion.53), channel_id=1, source_target_pairs={{0,7},{1,0},{2,1},{3,2},{4,3},{5,4},{6,5},{7,6},{8,15},{9,8},{10,9... | collective-permute-start | bytes 589832 | tf_op jit(solution)/shard_map/ppermute | solution.py:61
  161.7 12.3 %collective-permute-start.15 = (bf16[4,4,1,16,768]{4,3,0,1,2:T(8,128)(2,1)S(1)}, bf16[4,4,1,16,768]{4,3,0,1,2:T(8,128)(2,1)S(1)}, u32[]{:S(2)}, u32[]{:S(2)}) collective-permute-start(bf16[4,4,1,16,768]{4,3,0,1,2:T(8,128)(2,1)S(1)} %fusion.38), channel_id=1, source_target_pairs={{0,64},{64,128},{128,192},{192,0},{1,65},{65,129},{129,193},{193,1... | collective-permute-start | bytes 1179656 | tf_op jit(solution)/shard_map/ppermute | solution.py:61
  162.0 12.3 %collective-permute-start.18 = (bf16[4,4,1,16,768]{4,3,0,1,2:T(8,128)(2,1)S(1)}, bf16[4,4,1,16,768]{4,3,0,1,2:T(8,128)(2,1)S(1)}, u32[]{:S(2)}, u32[]{:S(2)}) collective-permute-start(bf16[4,4,1,16,768]{4,3,0,1,2:T(8,128)(2,1)S(1)} %fusion.35), channel_id=1, source_target_pairs={{0,192},{64,0},{128,64},{192,128},{1,193},{65,1},{129,65},{193,129... | collective-permute-start | bytes 1179656 | tf_op jit(solution)/shard_map/ppermute | solution.py:61
  164.7 6.1 %collective-permute-start.3 = (bf16[2,4,1,16,768]{4,3,1,0,2:T(8,128)(2,1)S(1)}, bf16[2,4,1,16,768]{4,3,1,0,2:T(8,128)(2,1)S(1)}, u32[]{:S(2)}, u32[]{:S(2)}) collective-permute-start(bf16[2,4,1,16,768]{4,3,1,0,2:T(8,128)(2,1)S(1)} %fusion.45), channel_id=1, source_target_pairs={{0,1},{1,2},{2,3},{3,4},{4,5},{5,6},{6,7},{7,0},{8,9},{9,10},{10,1... | collective-permute-start | bytes 589832 | tf_op jit(solution)/shard_map/ppermute | solution.py:61
  164.9 6.1 %collective-permute-start.10 = (bf16[2,4,1,16,768]{4,3,1,0,2:T(8,128)(2,1)S(1)}, bf16[2,4,1,16,768]{4,3,1,0,2:T(8,128)(2,1)S(1)}, u32[]{:S(2)}, u32[]{:S(2)}) collective-permute-start(bf16[2,4,1,16,768]{4,3,1,0,2:T(8,128)(2,1)S(1)} %fusion.52), channel_id=1, source_target_pairs={{0,7},{1,0},{2,1},{3,2},{4,3},{5,4},{6,5},{7,6},{8,15},{9,8},{10,9... | collective-permute-start | bytes 589832 | tf_op jit(solution)/shard_map/ppermute | solution.py:61
  170.9 6.9 %collective-permute-start.4 = (bf16[2,4,1,16,768]{4,3,1,0,2:T(8,128)(2,1)S(1)}, bf16[2,4,1,16,768]{4,3,1,0,2:T(8,128)(2,1)S(1)}, u32[]{:S(2)}, u32[]{:S(2)}) collective-permute-start(bf16[2,4,1,16,768]{4,3,1,0,2:T(8,128)(2,1)S(1)} %fusion.44), channel_id=1, source_target_pairs={{0,1},{1,2},{2,3},{3,4},{4,5},{5,6},{6,7},{7,0},{8,9},{9,10},{10,1... | collective-permute-start | bytes 589832 | tf_op jit(solution)/shard_map/ppermute | solution.py:61
  171.0 6.9 %collective-permute-start.11 = (bf16[2,4,1,16,768]{4,3,1,0,2:T(8,128)(2,1)S(1)}, bf16[2,4,1,16,768]{4,3,1,0,2:T(8,128)(2,1)S(1)}, u32[]{:S(2)}, u32[]{:S(2)}) collective-permute-start(bf16[2,4,1,16,768]{4,3,1,0,2:T(8,128)(2,1)S(1)} %fusion.51), channel_id=1, source_target_pairs={{0,7},{1,0},{2,1},{3,2},{4,3},{5,4},{6,5},{7,6},{8,15},{9,8},{10,9... | collective-permute-start | bytes 589832 | tf_op jit(solution)/shard_map/ppermute | solution.py:61
  174.1 15.3 %collective-permute-start.16 = (bf16[4,4,1,16,768]{4,3,0,1,2:T(8,128)(2,1)S(1)}, bf16[4,4,1,16,768]{4,3,0,1,2:T(8,128)(2,1)S(1)}, u32[]{:S(2)}, u32[]{:S(2)}) collective-permute-start(bf16[4,4,1,16,768]{4,3,0,1,2:T(8,128)(2,1)S(1)} %fusion.37), channel_id=1, source_target_pairs={{0,64},{64,128},{128,192},{192,0},{1,65},{65,129},{129,193},{193,1... | collective-permute-start | bytes 1179656 | tf_op jit(solution)/shard_map/ppermute | solution.py:61
  175.1 22.7 %collective-permute-start.19 = (bf16[4,4,1,16,768]{4,3,0,1,2:T(8,128)(2,1)}, bf16[4,4,1,16,768]{4,3,0,1,2:T(8,128)(2,1)}, u32[]{:S(2)}, u32[]{:S(2)}) collective-permute-start(bf16[4,4,1,16,768]{4,3,0,1,2:T(8,128)(2,1)} %fusion.34), channel_id=1, source_target_pairs={{0,192},{64,0},{128,64},{192,128},{1,193},{65,1},{129,65},{193,129... | collective-permute-start | bytes 1179656 | tf_op jit(solution)/shard_map/ppermute | solution.py:61
  177.8 8.0 %collective-permute-start.5 = (bf16[2,4,1,16,768]{4,3,1,0,2:T(8,128)(2,1)S(1)}, bf16[2,4,1,16,768]{4,3,1,0,2:T(8,128)(2,1)S(1)}, u32[]{:S(2)}, u32[]{:S(2)}) collective-permute-start(bf16[2,4,1,16,768]{4,3,1,0,2:T(8,128)(2,1)S(1)} %fusion.43), channel_id=1, source_target_pairs={{0,1},{1,2},{2,3},{3,4},{4,5},{5,6},{6,7},{7,0},{8,9},{9,10},{10,1... | collective-permute-start | bytes 589832 | tf_op jit(solution)/shard_map/ppermute | solution.py:61
  178.0 8.0 %collective-permute-start.12 = (bf16[2,4,1,16,768]{4,3,1,0,2:T(8,128)(2,1)S(1)}, bf16[2,4,1,16,768]{4,3,1,0,2:T(8,128)(2,1)S(1)}, u32[]{:S(2)}, u32[]{:S(2)}) collective-permute-start(bf16[2,4,1,16,768]{4,3,1,0,2:T(8,128)(2,1)S(1)} %fusion.50), channel_id=1, source_target_pairs={{0,7},{1,0},{2,1},{3,2},{4,3},{5,4},{6,5},{7,6},{8,15},{9,8},{10,9... | collective-permute-start | bytes 589832 | tf_op jit(solution)/shard_map/ppermute | solution.py:61
  185.9 7.5 %collective-permute-start.6 = (bf16[2,4,1,16,768]{4,3,1,0,2:T(8,128)(2,1)S(1)}, bf16[2,4,1,16,768]{4,3,1,0,2:T(8,128)(2,1)S(1)}, u32[]{:S(2)}, u32[]{:S(2)}) collective-permute-start(bf16[2,4,1,16,768]{4,3,1,0,2:T(8,128)(2,1)S(1)} %fusion.42), channel_id=1, source_target_pairs={{0,1},{1,2},{2,3},{3,4},{4,5},{5,6},{6,7},{7,0},{8,9},{9,10},{10,1... | collective-permute-start | bytes 589832 | tf_op jit(solution)/shard_map/ppermute | solution.py:61
  186.1 7.4 %collective-permute-start.13 = (bf16[2,4,1,16,768]{4,3,1,0,2:T(8,128)(2,1)S(1)}, bf16[2,4,1,16,768]{4,3,1,0,2:T(8,128)(2,1)S(1)}, u32[]{:S(2)}, u32[]{:S(2)}) collective-permute-start(bf16[2,4,1,16,768]{4,3,1,0,2:T(8,128)(2,1)S(1)} %fusion.49), channel_id=1, source_target_pairs={{0,7},{1,0},{2,1},{3,2},{4,3},{5,4},{6,5},{7,6},{8,15},{9,8},{10,9... | collective-permute-start | bytes 589832 | tf_op jit(solution)/shard_map/ppermute | solution.py:61
  194.3 9.7 %all-to-all-start.1 = ((bf16[4,4,1,16,768]{4,3,1,2,0:T(8,128)(2,1)}), bf16[4,4,1,16,768]{4,3,1,2,0:T(8,128)(2,1)S(1)}, u32[]{:S(2)}, u32[]{:S(2)}) async-start(bf16[4,4,1,16,768]{4,3,1,2,0:T(8,128)(2,1)} %maximum_bitcast_fusion), calls=%async_computation.1 | async-start | bytes 786432 | tf_op jit(solution)/shard_map/all_to_all | solution.py:78
  204.0 20.1 %all-to-all-start.2 = ((bf16[8,4,1,16,768]{4,3,1,2,0:T(8,128)(2,1)}), bf16[8,4,1,16,768]{4,3,1,2,0:T(8,128)(2,1)}, u32[]{:S(2)}, u32[]{:S(2)}) async-start(bf16[8,4,1,16,768]{4,3,1,2,0:T(8,128)(2,1)} %copy.190), calls=%async_computation.2 | async-start | bytes 1572864 | tf_op jit(solution)/shard_map/all_to_all | solution.py:78
  226.9 20.4 %all-to-all-start.3 = ((bf16[8,1,16,768]{3,2,1,0:T(8,128)(2,1)}), bf16[8,1,16,768]{3,2,1,0:T(8,128)(2,1)S(1)}, u32[]{:S(2)}, u32[]{:S(2)}) async-start(bf16[8,1,16,768]{3,2,1,0:T(8,128)(2,1)} %pad_maximum_fusion.1), calls=%async_computation.3 | async-start | bytes 393216 | tf_op jit(solution)/shard_map/all_to_all | solution.py:182
Sparse Core Ops, SparseCore 0:
  50.7 83.8 all-gather.2
where the time goes:
time: 256 us; the launch traced here: 255 us
  waiting for transfers between devices  106 us (41%)
  starting transfers between devices  52.5 us (21%)
  blocking collectives  32.6 us (13%)
  local copies, waits for them, and re-layouts  17.1 us (7%)
  other arithmetic  15.9 us (6%)
  matrix products  15.5 us (6%)
  between operations  15 us (6%)
    all_gather x1, waiting for transfers between devices, per_device(): pieces = lax.all_gather(received, ('grp', 'tp'), axis=0, tiled=True)  74.4 us
    ppermute x20, starting transfers between devices, ring_reduce_scatter(): arrived = lax.ppermute(total.astype(jnp.bfloat16), axis, pairs)  29.6 us
    psum x1, blocking collectives, per_device(): squares, logits = lax.psum((squares, partial_logits), 'tp')  18.3 us
    all_to_all x1, starting transfers between devices, per_device(): lax.all_to_all(summed.astype(jnp.bfloat16), 'ex', split_axis=0, concat_ax...  14.6 us
    ppermute x20, waiting for transfers between devices, ring_reduce_scatter(): arrived = lax.ppermute(total.astype(jnp.bfloat16), axis, pairs)  14.5 us
    all_to_all x1, blocking collectives, per_device(): lax.all_to_all(outgoing, 'ex', split_axis=0, concat_axis=0, tiled=True)  14.3 us
    unnamed x29, local copies, waits for them, and re-layouts  13.8 us
    all_to_all x2, waiting for transfers between devices, exchange_sum(): moved = lax.all_to_all(parts.astype(jnp.bfloat16), axis, 0, 0, tiled=True)  12.5 us
  transfers between devices with their start and end apart: 24, of which 9 were waited for; matrix products, arithmetic and copies ran while one was open for 9% of the time, Pallas kernels for 0%

commit v1 on v0

--- a/solution.py
+++ b/solution.py
@@ -157,7 +157,6 @@
     down_split = w_down.reshape(local_experts, hidden_local, tensor_count, slice_width)
     owner_half = owner_count // 2
     group_half = group_count // 2
-    tensor_half = tensor_count // 2
 
     def down(rows, columns, spec):
         return jnp.einsum(spec, rows, columns, preferred_element_type=jnp.float32)
@@ -170,12 +169,7 @@
         "tp",
         0,
     )
-    y_first = both_ways(
-        down(y_rows, down_split[:, :, :tensor_half], "jgacf,jftd->gtajcd"),
-        down(y_rows, down_split[:, :, tensor_half:], "jgacf,jftd->gtajcd"),
-        "grp",
-        0,
-    )
+    y_first = exchange_sum(down(y_rows, down_split, "jgacf,jftd->gtajcd"), "grp")
     z_done = exchange_sum(z_first, "grp")
     y_done = exchange_sum(y_first, "tp")
     summed = jnp.concatenate([z_done, y_done], axis=0)

time: 256 us -> 266 us (1.039)
  waiting for transfers between devices: 106 us -> 115 us
  other arithmetic: 15.9 us -> 23 us
  starting transfers between devices: 52.5 us -> 48.6 us
  local copies, waits for them, and re-layouts: 17.1 us -> 13.5 us
    ppermute x20 -> x14, starting transfers between devices: 29.6 us -> 18.4 us  [ring_reduce_scatter(): arrived = lax.ppermute(total.astype(jnp.bfloat16), axis, pairs)]
    convert_element_type x16 -> x12, other arithmetic: 1.71 us -> 8.75 us  [ring_reduce_scatter(): arrived = lax.ppermute(total.astype(jnp.bfloat16), axis, pairs)]
    all_to_all x2 -> x3, starting transfers between devices: 8.31 us -> 14.6 us  [exchange_sum(): moved = lax.all_to_all(parts.astype(jnp.bfloat16), axis, 0, 0, tiled=True)]
    all_gather x1, waiting for transfers between devices: 74.4 us -> 79.2 us  [per_device(): pieces = lax.all_gather(received, ('grp', 'tp'), axis=0, tiled=True)]
    ppermute x20 -> x14, waiting for transfers between devices: 14.5 us -> 18.1 us  [ring_reduce_scatter(): arrived = lax.ppermute(total.astype(jnp.bfloat16), axis, pairs)]
    unnamed x29 -> x30, local copies, waits for them, and re-layouts: 13.8 us -> 10.3 us
    dot_general x4 -> x3, matrix products: 3.72 us -> 5.63 us  [down(): return jnp.einsum(spec, rows, columns, preferred_element_type=jnp.float32)]
    all_to_all x2 -> x3, waiting for transfers between devices: 12.5 us -> 12.4 us  [exchange_sum(): moved = lax.all_to_all(parts.astype(jnp.bfloat16), axis, 0, 0, tiled=True)]
  transfers between devices with their start and end apart: 24 -> 19, of which waited for: 9 -> 10; matrix products, arithmetic and copies ran while one was open for 9% -> 11% of each run, Pallas kernels for 0% -> 0%
where the time goes in v1:
time: 266 us; the launch traced here: 265 us
  waiting for transfers between devices  115 us (43%)
  starting transfers between devices  48.6 us (18%)
  blocking collectives  32.6 us (12%)
  other arithmetic  23 us (9%)
  matrix products  17.4 us (7%)
  between operations  14.8 us (6%)
  local copies, waits for them, and re-layouts  13.5 us (5%)
    all_gather x1, waiting for transfers between devices, per_device(): pieces = lax.all_gather(received, ('grp', 'tp'), axis=0, tiled=True)  79.2 us
    ppermute x14, starting transfers between devices, ring_reduce_scatter(): arrived = lax.ppermute(total.astype(jnp.bfloat16), axis, pairs)  18.4 us
    psum x1, blocking collectives, per_device(): squares, logits = lax.psum((squares, partial_logits), 'tp')  18.3 us
    ppermute x14, waiting for transfers between devices, ring_reduce_scatter(): arrived = lax.ppermute(total.astype(jnp.bfloat16), axis, pairs)  18.1 us
    all_to_all x1, starting transfers between devices, per_device(): lax.all_to_all(summed.astype(jnp.bfloat16), 'ex', split_axis=0, concat_ax...  15.5 us
    all_to_all x3, starting transfers between devices, exchange_sum(): moved = lax.all_to_all(parts.astype(jnp.bfloat16), axis, 0, 0, tiled=True)  14.6 us
    all_to_all x1, blocking collectives, per_device(): lax.all_to_all(outgoing, 'ex', split_axis=0, concat_axis=0, tiled=True)  14.3 us
    all_to_all x3, waiting for transfers between devices, exchange_sum(): moved = lax.all_to_all(parts.astype(jnp.bfloat16), axis, 0, 0, tiled=True)  12.4 us
  transfers between devices with their start and end apart: 19, of which 10 were waited for; matrix products, arithmetic and copies ran while one was open for 11% of the time, Pallas kernels for 0%

profile of v1, /device:TPU:1, one launch (start us, length us, event | category | flops | bytes accessed | tf_op | source)
XLA Modules:
  0.0 264.7 jit_solution(8483767270113815134)
XLA Ops:
  7.2 0.9 copy.161
  10.4 2.5 fusion.78
  13.0 1.1 fusion.79
  16.0 18.3 %all-reduce = (f32[16,2]{0,1:T(2,128)S(1)}, f32[16,2,8]{0,2,1:T(8,128)}) all-reduce(f32[16,2]{0,1:T(2,128)S(1)} %multiply_reduce_fusion, f32[16,2,8]{0,2,1:T(8,128)S(1)} %fusion.60), channel_id=1, replica_groups=mesh['grp'=4,'ex'=8,'tp'=8] {'tp'}, use_global_device_ids=true, to_apply=%region_6.7 | all-reduce | flops 288 | bytes 2304 | tf_op jit(solution)/shard_map/psum | solution.py:112
  36.2 14.3 %all_to_all.25 = bf16[8,16,768]{2,1,0:T(8,128)(2,1)} all-to-all(bf16[8,16,768]{2,1,0:T(8,128)(2,1)S(1)} %bitcast.358), channel_id=1, replica_groups=mesh['grp'=4,'ex'=8,'tp'=8] {'ex'}, dimensions={0} | all-to-all | bytes 393216 | tf_op jit(solution)/shard_map/all_to_all | solution.py:143
  50.8 4.5 %copy.223 = bf16[32,8,8,768]{3,2,1,0:T(8,128)(2,1)} copy(bf16[32,8,8,768]{3,1,2,0:T(8,128)(2,1)} %bitcast.355) | data formatting | bytes 6291456
  55.3 79.2 %all-gather.3.cloned.1.call-done = bf16[256,16,768]{2,1,0:T(8,128)(2,1)} async-done(((bf16[8,16,768]{2,1,0:T(8,128)(2,1)}), bf16[256,16,768]{2,1,0:T(8,128)(2,1)}) %all-gather.3.cloned.1.call-update) | async-done | bytes 6291472 | tf_op jit(solution)/shard_map/all_gather | solution.py:145
  134.6 4.7 %convolution_bitcast_fusion.1 = f32[4,8,16,256]{3,2,1,0:T(8,128)S(1)} fusion(bf16[4,8,8,16,768]{4,3,2,1,0:T(8,128)(2,1)} %bitcast.363, bf16[8,768,256,1,1]{2,1,4,0,3:T(8,128)(2,1)S(1)} %bitcast.351), kind=kOutput, calls=%fused_computation.14 | convolution fusion | flops 1610612736 | bytes 9961472 | tf_op jit(solution)/shard_map/gtajcd,jtdf->jgacf/dot_general | solution.py:152
  140.1 1.8 fusion.26
  142.0 1.3 fusion.4
  143.3 1.3 fusion
  145.0 1.5 copy-done.2
  146.5 1.2 collective-permute-start.7
  147.8 3.1 %convert_bitcast_fusion = bf16[4,8,4,1,16,768]{5,4,1,2,3,0:T(8,128)(2,1)} fusion(bf16[256,8,768,1,1]{2,1,0,4,3:T(8,128)(2,1)S(1)} %bitcast.354, bf16[1,4,8,16,256]{4,3,2,1,0:T(8,128)(2,1)S(1)} %fusion.26), kind=kOutput, calls=%fused_computation.3 | convolution fusion | flops 806879232 | bytes 6422528 | tf_op jit(solution)/shard_map/jgacf,jftd->gtajcd/dot_general | solution.py:162
  150.9 4.6 %all-to-all-start.2 = ((bf16[4,8,4,1,16,768]{5,4,1,2,3,0:T(8,128)(2,1)}), bf16[4,8,4,1,16,768]{5,4,1,2,3,0:T(8,128)(2,1)}, u32[]{:S(2)}, u32[]{:S(2)}) async-start(bf16[4,8,4,1,16,768]{5,4,1,2,3,0:T(8,128)(2,1)} %convert_bitcast_fusion), calls=%async_computation.2 | async-start | bytes 6291456 | tf_op jit(solution)/shard_map/all_to_all | solution.py:78
  155.5 1.2 fusion.41
  157.3 1.1 fusion.48
  158.4 2.5 collective-permute-start.8
  160.9 2.3 collective-permute-done.1
  163.2 1.0 fusion.40
  164.3 1.0 fusion.47
  165.4 2.8 %collective-permute-start.9 = (bf16[2,4,1,16,768]{4,3,1,0,2:T(8,128)(2,1)S(1)}, bf16[2,4,1,16,768]{4,3,1,0,2:T(8,128)(2,1)S(1)}, u32[]{:S(2)}, u32[]{:S(2)}) collective-permute-start(bf16[2,4,1,16,768]{4,3,1,0,2:T(8,128)(2,1)S(1)} %fusion.47), channel_id=1, source_target_pairs={{0,7},{1,0},{2,1},{3,2},{4,3},{5,4},{6,5},{7,6},{8,15},{9,8},{10,9... | collective-permute-start | bytes 589832 | tf_op jit(solution)/shard_map/ppermute | solution.py:61
  168.1 2.3 collective-permute-done.2
  170.4 1.0 fusion.39
  171.6 2.8 %collective-permute-start.10 = (bf16[2,4,1,16,768]{4,3,1,0,2:T(8,128)(2,1)S(1)}, bf16[2,4,1,16,768]{4,3,1,0,2:T(8,128)(2,1)S(1)}, u32[]{:S(2)}, u32[]{:S(2)}) collective-permute-start(bf16[2,4,1,16,768]{4,3,1,0,2:T(8,128)(2,1)S(1)} %fusion.46), channel_id=1, source_target_pairs={{0,7},{1,0},{2,1},{3,2},{4,3},{5,4},{6,5},{7,6},{8,15},{9,8},{10,9... | collective-permute-start | bytes 589832 | tf_op jit(solution)/shard_map/ppermute | solution.py:61
  174.4 3.3 %collective-permute-done.3 = bf16[2,4,1,16,768]{4,3,1,0,2:T(8,128)(2,1)S(1)} collective-permute-done((bf16[2,4,1,16,768]{4,3,1,0,2:T(8,128)(2,1)S(1)}, bf16[2,4,1,16,768]{4,3,1,0,2:T(8,128)(2,1)S(1)}, u32[]{:S(2)}, u32[]{:S(2)}) %collective-permute-start.3) | collective-permute-done | bytes 196640 | tf_op jit(solution)/shard_map/ppermute | solution.py:61
  177.7 1.0 fusion.38
  178.9 2.7 %collective-permute-start.11 = (bf16[2,4,1,16,768]{4,3,1,0,2:T(8,128)(2,1)S(1)}, bf16[2,4,1,16,768]{4,3,1,0,2:T(8,128)(2,1)S(1)}, u32[]{:S(2)}, u32[]{:S(2)}) collective-permute-start(bf16[2,4,1,16,768]{4,3,1,0,2:T(8,128)(2,1)S(1)} %fusion.45), channel_id=1, source_target_pairs={{0,7},{1,0},{2,1},{3,2},{4,3},{5,4},{6,5},{7,6},{8,15},{9,8},{10,9... | collective-permute-start | bytes 589832 | tf_op jit(solution)/shard_map/ppermute | solution.py:61
  181.6 3.3 %collective-permute-done.4 = bf16[2,4,1,16,768]{4,3,1,0,2:T(8,128)(2,1)S(1)} collective-permute-done((bf16[2,4,1,16,768]{4,3,1,0,2:T(8,128)(2,1)S(1)}, bf16[2,4,1,16,768]{4,3,1,0,2:T(8,128)(2,1)S(1)}, u32[]{:S(2)}, u32[]{:S(2)}) %collective-permute-start.4) | collective-permute-done | bytes 196640 | tf_op jit(solution)/shard_map/ppermute | solution.py:61
  184.9 1.0 fusion.37
  186.1 2.7 %collective-permute-start.12 = (bf16[2,4,1,16,768]{4,3,1,0,2:T(8,128)(2,1)S(1)}, bf16[2,4,1,16,768]{4,3,1,0,2:T(8,128)(2,1)S(1)}, u32[]{:S(2)}, u32[]{:S(2)}) collective-permute-start(bf16[2,4,1,16,768]{4,3,1,0,2:T(8,128)(2,1)S(1)} %fusion.44), channel_id=1, source_target_pairs={{0,7},{1,0},{2,1},{3,2},{4,3},{5,4},{6,5},{7,6},{8,15},{9,8},{10,9... | collective-permute-start | bytes 589832 | tf_op jit(solution)/shard_map/ppermute | solution.py:61
  188.9 3.3 %collective-permute-done.5 = bf16[2,4,1,16,768]{4,3,1,0,2:T(8,128)(2,1)S(1)} collective-permute-done((bf16[2,4,1,16,768]{4,3,1,0,2:T(8,128)(2,1)S(1)}, bf16[2,4,1,16,768]{4,3,1,0,2:T(8,128)(2,1)S(1)}, u32[]{:S(2)}, u32[]{:S(2)}) %collective-permute-start.5) | collective-permute-done | bytes 196640 | tf_op jit(solution)/shard_map/ppermute | solution.py:61
  192.2 1.0 fusion.36
  193.4 2.7 %collective-permute-start.13 = (bf16[2,4,1,16,768]{4,3,1,0,2:T(8,128)(2,1)S(1)}, bf16[2,4,1,16,768]{4,3,1,0,2:T(8,128)(2,1)S(1)}, u32[]{:S(2)}, u32[]{:S(2)}) collective-permute-start(bf16[2,4,1,16,768]{4,3,1,0,2:T(8,128)(2,1)S(1)} %fusion.43), channel_id=1, source_target_pairs={{0,7},{1,0},{2,1},{3,2},{4,3},{5,4},{6,5},{7,6},{8,15},{9,8},{10,9... | collective-permute-start | bytes 589832 | tf_op jit(solution)/shard_map/ppermute | solution.py:61
  196.1 3.5 %collective-permute-done.6 = bf16[2,4,1,16,768]{4,3,1,0,2:T(8,128)(2,1)S(1)} collective-permute-done((bf16[2,4,1,16,768]{4,3,1,0,2:T(8,128)(2,1)S(1)}, bf16[2,4,1,16,768]{4,3,1,0,2:T(8,128)(2,1)S(1)}, u32[]{:S(2)}, u32[]{:S(2)}) %collective-permute-start.6) | collective-permute-done | bytes 196640 | tf_op jit(solution)/shard_map/ppermute | solution.py:61
  199.7 1.0 fusion.49
  201.6 5.7 %all-to-all-start.1 = ((bf16[4,4,1,16,768]{4,3,1,2,0:T(8,128)(2,1)}), bf16[4,4,1,16,768]{4,3,1,2,0:T(8,128)(2,1)S(1)}, u32[]{:S(2)}, u32[]{:S(2)}) async-start(bf16[4,4,1,16,768]{4,3,1,2,0:T(8,128)(2,1)} %maximum_bitcast_fusion), calls=%async_computation.1 | async-start | bytes 786432 | tf_op jit(solution)/shard_map/all_to_all | solution.py:78
  207.3 2.3 bitcast_reduce_fusion
  209.6 1.0 copy.187
  210.6 2.9 %all-to-all-done.1 = bf16[4,4,1,16,768]{4,3,1,2,0:T(8,128)(2,1)S(1)} async-done(((bf16[4,4,1,16,768]{4,3,1,2,0:T(8,128)(2,1)}), bf16[4,4,1,16,768]{4,3,1,2,0:T(8,128)(2,1)S(1)}, u32[]{:S(2)}, u32[]{:S(2)}) %all-to-all-start.1) | async-done | bytes 393248 | tf_op jit(solution)/shard_map/all_to_all | solution.py:78
  213.5 4.2 %all-to-all-start.3 = ((bf16[8,4,1,16,768]{4,3,1,2,0:T(8,128)(2,1)}), bf16[8,4,1,16,768]{4,3,1,2,0:T(8,128)(2,1)}, u32[]{:S(2)}, u32[]{:S(2)}) async-start(bf16[8,4,1,16,768]{4,3,1,2,0:T(8,128)(2,1)} %copy.187), calls=%async_computation.3 | async-start | bytes 1572864 | tf_op jit(solution)/shard_map/all_to_all | solution.py:78
  219.1 1.5 copy.190
  221.3 1.3 select_reduce_fusion.1
  223.3 9.5 %all-to-all-done.3 = bf16[8,4,1,16,768]{4,3,1,2,0:T(8,128)(2,1)} async-done(((bf16[8,4,1,16,768]{4,3,1,2,0:T(8,128)(2,1)}), bf16[8,4,1,16,768]{4,3,1,2,0:T(8,128)(2,1)}, u32[]{:S(2)}, u32[]{:S(2)}) %all-to-all-start.3) | async-done | bytes 786464 | tf_op jit(solution)/shard_map/all_to_all | solution.py:78
  232.7 1.2 reduce.10
  234.0 1.6 pad_maximum_fusion
  235.6 15.5 %all-to-all-start.4 = ((bf16[8,1,16,768]{3,2,1,0:T(8,128)(2,1)}), bf16[8,1,16,768]{3,2,1,0:T(8,128)(2,1)S(1)}, u32[]{:S(2)}, u32[]{:S(2)}) async-start(bf16[8,1,16,768]{3,2,1,0:T(8,128)(2,1)} %pad_maximum_fusion), calls=%async_computation.4 | async-start | bytes 393216 | tf_op jit(solution)/shard_map/all_to_all | solution.py:176
  251.9 5.1 %all-to-all-done.4 = bf16[8,1,16,768]{3,2,1,0:T(8,128)(2,1)S(1)} async-done(((bf16[8,1,16,768]{3,2,1,0:T(8,128)(2,1)}), bf16[8,1,16,768]{3,2,1,0:T(8,128)(2,1)S(1)}, u32[]{:S(2)}, u32[]{:S(2)}) %all-to-all-start.4) | async-done | bytes 196640 | tf_op jit(solution)/shard_map/all_to_all | solution.py:176
  (88 shorter events, 13.9 us)
Async XLA Ops:
  7.2 127.4 %copy-start = (bf16[1,6144,256]{2,1,0:T(8,128)(2,1)S(1)}, bf16[1,6144,256]{2,1,0:T(8,128)(2,1)}, u32[]{:S(2)}) copy-start(bf16[1,6144,256]{2,1,0:T(8,128)(2,1)} %param.23) | copy-start | bytes 9437188
  7.2 7.4 %copy-start.12 = (bf16[16,2,128]{2,1,0:T(2,128)(2,1)S(1)}, bf16[16,2,128]{2,1,0:T(2,128)(2,1)}, u32[]{:S(2)}) copy-start(bf16[16,2,128]{2,1,0:T(2,128)(2,1)} %param.16) | copy-start | bytes 24580
  7.2 127.4 %all-gather.3.cloned.1.call-start = ((), (), s32[]{:S(2)}) async-start(), calls=%async_computation.5 | async-start | bytes 6488064 | tf_op jit(solution)/shard_map/all_gather | solution.py:145
  10.4 4.4 %copy-start.11 = (bf16[16,1,512,128]{3,2,1,0:T(8,128)(2,1)S(1)}, bf16[16,1,512,128]{3,2,1,0:T(8,128)(2,1)}, u32[]{:S(2)}) copy-start(bf16[16,1,512,128]{3,2,1,0:T(8,128)(2,1)} %param.18) | copy-start | bytes 6291460
  12.9 2.5 copy-start.8
  12.9 2.5 copy-start.5
  12.9 2.6 copy-start.6
  34.3 21.0 %copy-start.7 = (f32[16,2]{0,1:T(2,128)}, f32[16,2]{0,1:T(2,128)S(1)}, u32[]{:S(2)}) copy-start(f32[16,2]{0,1:T(2,128)S(1)} %add_sqrt_fusion) | copy-start | bytes 388
  134.6 4.7 %copy-start.9 = (bf16[256,16,768]{2,1,0:T(8,128)(2,1)S(1)}, bf16[256,16,768]{2,1,0:T(8,128)(2,1)}, u32[]{:S(2)}) copy-start(bf16[256,16,768]{2,1,0:T(8,128)(2,1)} %all-gather.3.cloned.1.call-done) | copy-start | bytes 18874372
  134.6 5.5 %copy-start.10 = (bf16[1,6144,256]{2,1,0:T(8,128)(2,1)S(1)}, bf16[1,6144,256]{2,1,0:T(8,128)(2,1)}, u32[]{:S(2)}) copy-start(bf16[1,6144,256]{2,1,0:T(8,128)(2,1)} %param.24) | copy-start | bytes 9437188
  140.1 1.9 copy-start.1
  143.2 1.6 copy-start.4
  144.9 1.6 copy-start.2
  144.9 10.6 %collective-permute-start = (bf16[2,4,1,16,768]{4,3,1,0,2:T(8,128)(2,1)S(1)}, bf16[2,4,1,16,768]{4,3,1,0,2:T(8,128)(2,1)}, u32[]{:S(2)}, u32[]{:S(2)}) collective-permute-start(bf16[2,4,1,16,768]{4,3,1,0,2:T(8,128)(2,1)S(1)} %fusion.55), channel_id=1, source_target_pairs={{0,1},{1,2},{2,3},{3,4},{4,5},{5,6},{6,7},{7,0},{8,9},{9,10},{10,1... | collective-permute-start | bytes 589832 | tf_op jit(solution)/shard_map/ppermute | solution.py:61
  146.5 10.8 %collective-permute-start.7 = (bf16[2,4,1,16,768]{4,3,1,0,2:T(8,128)(2,1)S(1)}, bf16[2,4,1,16,768]{4,3,1,0,2:T(8,128)(2,1)}, u32[]{:S(2)}, u32[]{:S(2)}) collective-permute-start(bf16[2,4,1,16,768]{4,3,1,0,2:T(8,128)(2,1)S(1)} %fusion.54), channel_id=1, source_target_pairs={{0,7},{1,0},{2,1},{3,2},{4,3},{5,4},{6,5},{7,6},{8,15},{9,8},{10,9... | collective-permute-start | bytes 589832 | tf_op jit(solution)/shard_map/ppermute | solution.py:61
  150.9 50.7 %all-to-all-start.2 = ((bf16[4,8,4,1,16,768]{5,4,1,2,3,0:T(8,128)(2,1)}), bf16[4,8,4,1,16,768]{5,4,1,2,3,0:T(8,128)(2,1)}, u32[]{:S(2)}, u32[]{:S(2)}) async-start(bf16[4,8,4,1,16,768]{5,4,1,2,3,0:T(8,128)(2,1)} %convert_bitcast_fusion), calls=%async_computation.2 | async-start | bytes 6291456 | tf_op jit(solution)/shard_map/all_to_all | solution.py:78
  155.5 16.1 %copy-start.3 = (f32[2,4,16,8,768]{4,2,1,0,3:T(8,128)S(1)}, f32[2,4,16,8,768]{4,2,1,0,3:T(8,128)}, u32[]{:S(2)}) copy-start(f32[2,4,16,8,768]{4,2,1,0,3:T(8,128)} %copy-done.2) | copy-start | bytes 9437188
  156.8 6.4 %collective-permute-start.1 = (bf16[2,4,1,16,768]{4,3,1,0,2:T(8,128)(2,1)S(1)}, bf16[2,4,1,16,768]{4,3,1,0,2:T(8,128)(2,1)S(1)}, u32[]{:S(2)}, u32[]{:S(2)}) collective-permute-start(bf16[2,4,1,16,768]{4,3,1,0,2:T(8,128)(2,1)S(1)} %fusion.41), channel_id=1, source_target_pairs={{0,1},{1,2},{2,3},{3,4},{4,5},{5,6},{6,7},{7,0},{8,9},{9,10},{10,1... | collective-permute-start | bytes 589832 | tf_op jit(solution)/shard_map/ppermute | solution.py:61
  158.4 5.9 %collective-permute-start.8 = (bf16[2,4,1,16,768]{4,3,1,0,2:T(8,128)(2,1)S(1)}, bf16[2,4,1,16,768]{4,3,1,0,2:T(8,128)(2,1)S(1)}, u32[]{:S(2)}, u32[]{:S(2)}) collective-permute-start(bf16[2,4,1,16,768]{4,3,1,0,2:T(8,128)(2,1)S(1)} %fusion.48), channel_id=1, source_target_pairs={{0,7},{1,0},{2,1},{3,2},{4,3},{5,4},{6,5},{7,6},{8,15},{9,8},{10,9... | collective-permute-start | bytes 589832 | tf_op jit(solution)/shard_map/ppermute | solution.py:61
  164.2 6.2 %collective-permute-start.2 = (bf16[2,4,1,16,768]{4,3,1,0,2:T(8,128)(2,1)S(1)}, bf16[2,4,1,16,768]{4,3,1,0,2:T(8,128)(2,1)S(1)}, u32[]{:S(2)}, u32[]{:S(2)}) collective-permute-start(bf16[2,4,1,16,768]{4,3,1,0,2:T(8,128)(2,1)S(1)} %fusion.40), channel_id=1, source_target_pairs={{0,1},{1,2},{2,3},{3,4},{4,5},{5,6},{6,7},{7,0},{8,9},{9,10},{10,1... | collective-permute-start | bytes 589832 | tf_op jit(solution)/shard_map/ppermute | solution.py:61
  165.4 6.2 %collective-permute-start.9 = (bf16[2,4,1,16,768]{4,3,1,0,2:T(8,128)(2,1)S(1)}, bf16[2,4,1,16,768]{4,3,1,0,2:T(8,128)(2,1)S(1)}, u32[]{:S(2)}, u32[]{:S(2)}) collective-permute-start(bf16[2,4,1,16,768]{4,3,1,0,2:T(8,128)(2,1)S(1)} %fusion.47), channel_id=1, source_target_pairs={{0,7},{1,0},{2,1},{3,2},{4,3},{5,4},{6,5},{7,6},{8,15},{9,8},{10,9... | collective-permute-start | bytes 589832 | tf_op jit(solution)/shard_map/ppermute | solution.py:61
  171.5 6.2 %collective-permute-start.3 = (bf16[2,4,1,16,768]{4,3,1,0,2:T(8,128)(2,1)S(1)}, bf16[2,4,1,16,768]{4,3,1,0,2:T(8,128)(2,1)S(1)}, u32[]{:S(2)}, u32[]{:S(2)}) collective-permute-start(bf16[2,4,1,16,768]{4,3,1,0,2:T(8,128)(2,1)S(1)} %fusion.39), channel_id=1, source_target_pairs={{0,1},{1,2},{2,3},{3,4},{4,5},{5,6},{6,7},{7,0},{8,9},{9,10},{10,1... | collective-permute-start | bytes 589832 | tf_op jit(solution)/shard_map/ppermute | solution.py:61
  171.6 7.2 %collective-permute-start.10 = (bf16[2,4,1,16,768]{4,3,1,0,2:T(8,128)(2,1)S(1)}, bf16[2,4,1,16,768]{4,3,1,0,2:T(8,128)(2,1)S(1)}, u32[]{:S(2)}, u32[]{:S(2)}) collective-permute-start(bf16[2,4,1,16,768]{4,3,1,0,2:T(8,128)(2,1)S(1)} %fusion.46), channel_id=1, source_target_pairs={{0,7},{1,0},{2,1},{3,2},{4,3},{5,4},{6,5},{7,6},{8,15},{9,8},{10,9... | collective-permute-start | bytes 589832 | tf_op jit(solution)/shard_map/ppermute | solution.py:61
  178.7 6.2 %collective-permute-start.4 = (bf16[2,4,1,16,768]{4,3,1,0,2:T(8,128)(2,1)S(1)}, bf16[2,4,1,16,768]{4,3,1,0,2:T(8,128)(2,1)S(1)}, u32[]{:S(2)}, u32[]{:S(2)}) collective-permute-start(bf16[2,4,1,16,768]{4,3,1,0,2:T(8,128)(2,1)S(1)} %fusion.38), channel_id=1, source_target_pairs={{0,1},{1,2},{2,3},{3,4},{4,5},{5,6},{6,7},{7,0},{8,9},{9,10},{10,1... | collective-permute-start | bytes 589832 | tf_op jit(solution)/shard_map/ppermute | solution.py:61
  178.9 7.2 %collective-permute-start.11 = (bf16[2,4,1,16,768]{4,3,1,0,2:T(8,128)(2,1)S(1)}, bf16[2,4,1,16,768]{4,3,1,0,2:T(8,128)(2,1)S(1)}, u32[]{:S(2)}, u32[]{:S(2)}) collective-permute-start(bf16[2,4,1,16,768]{4,3,1,0,2:T(8,128)(2,1)S(1)} %fusion.45), channel_id=1, source_target_pairs={{0,7},{1,0},{2,1},{3,2},{4,3},{5,4},{6,5},{7,6},{8,15},{9,8},{10,9... | collective-permute-start | bytes 589832 | tf_op jit(solution)/shard_map/ppermute | solution.py:61
  186.0 6.2 %collective-permute-start.5 = (bf16[2,4,1,16,768]{4,3,1,0,2:T(8,128)(2,1)S(1)}, bf16[2,4,1,16,768]{4,3,1,0,2:T(8,128)(2,1)S(1)}, u32[]{:S(2)}, u32[]{:S(2)}) collective-permute-start(bf16[2,4,1,16,768]{4,3,1,0,2:T(8,128)(2,1)S(1)} %fusion.37), channel_id=1, source_target_pairs={{0,1},{1,2},{2,3},{3,4},{4,5},{5,6},{6,7},{7,0},{8,9},{9,10},{10,1... | collective-permute-start | bytes 589832 | tf_op jit(solution)/shard_map/ppermute | solution.py:61
  186.1 7.2 %collective-permute-start.12 = (bf16[2,4,1,16,768]{4,3,1,0,2:T(8,128)(2,1)S(1)}, bf16[2,4,1,16,768]{4,3,1,0,2:T(8,128)(2,1)S(1)}, u32[]{:S(2)}, u32[]{:S(2)}) collective-permute-start(bf16[2,4,1,16,768]{4,3,1,0,2:T(8,128)(2,1)S(1)} %fusion.44), channel_id=1, source_target_pairs={{0,7},{1,0},{2,1},{3,2},{4,3},{5,4},{6,5},{7,6},{8,15},{9,8},{10,9... | collective-permute-start | bytes 589832 | tf_op jit(solution)/shard_map/ppermute | solution.py:61
  193.2 6.4 %collective-permute-start.6 = (bf16[2,4,1,16,768]{4,3,1,0,2:T(8,128)(2,1)S(1)}, bf16[2,4,1,16,768]{4,3,1,0,2:T(8,128)(2,1)S(1)}, u32[]{:S(2)}, u32[]{:S(2)}) collective-permute-start(bf16[2,4,1,16,768]{4,3,1,0,2:T(8,128)(2,1)S(1)} %fusion.36), channel_id=1, source_target_pairs={{0,1},{1,2},{2,3},{3,4},{4,5},{5,6},{6,7},{7,0},{8,9},{9,10},{10,1... | collective-permute-start | bytes 589832 | tf_op jit(solution)/shard_map/ppermute | solution.py:61
  193.4 7.3 %collective-permute-start.13 = (bf16[2,4,1,16,768]{4,3,1,0,2:T(8,128)(2,1)S(1)}, bf16[2,4,1,16,768]{4,3,1,0,2:T(8,128)(2,1)S(1)}, u32[]{:S(2)}, u32[]{:S(2)}) collective-permute-start(bf16[2,4,1,16,768]{4,3,1,0,2:T(8,128)(2,1)S(1)} %fusion.43), channel_id=1, source_target_pairs={{0,7},{1,0},{2,1},{3,2},{4,3},{5,4},{6,5},{7,6},{8,15},{9,8},{10,9... | collective-permute-start | bytes 589832 | tf_op jit(solution)/shard_map/ppermute | solution.py:61
  201.6 12.0 %all-to-all-start.1 = ((bf16[4,4,1,16,768]{4,3,1,2,0:T(8,128)(2,1)}), bf16[4,4,1,16,768]{4,3,1,2,0:T(8,128)(2,1)S(1)}, u32[]{:S(2)}, u32[]{:S(2)}) async-start(bf16[4,4,1,16,768]{4,3,1,2,0:T(8,128)(2,1)} %maximum_bitcast_fusion), calls=%async_computation.1 | async-start | bytes 786432 | tf_op jit(solution)/shard_map/all_to_all | solution.py:78
  213.5 19.2 %all-to-all-start.3 = ((bf16[8,4,1,16,768]{4,3,1,2,0:T(8,128)(2,1)}), bf16[8,4,1,16,768]{4,3,1,2,0:T(8,128)(2,1)}, u32[]{:S(2)}, u32[]{:S(2)}) async-start(bf16[8,4,1,16,768]{4,3,1,2,0:T(8,128)(2,1)} %copy.187), calls=%async_computation.3 | async-start | bytes 1572864 | tf_op jit(solution)/shard_map/all_to_all | solution.py:78
  235.6 21.4 %all-to-all-start.4 = ((bf16[8,1,16,768]{3,2,1,0:T(8,128)(2,1)}), bf16[8,1,16,768]{3,2,1,0:T(8,128)(2,1)S(1)}, u32[]{:S(2)}, u32[]{:S(2)}) async-start(bf16[8,1,16,768]{3,2,1,0:T(8,128)(2,1)} %pad_maximum_fusion), calls=%async_computation.4 | async-start | bytes 393216 | tf_op jit(solution)/shard_map/all_to_all | solution.py:176
Sparse Core Ops, SparseCore 0:
  50.7 83.8 all-gather.2

commit v2 on v0

--- a/solution.py
+++ b/solution.py
@@ -112,7 +112,6 @@
     squares, logits = lax.psum((squares, partial_logits), "tp")
     root_mean = jnp.sqrt(squares / width + 1e-05)[..., None]
     logits = logits / root_mean
-    normed = (scaled / root_mean).astype(jnp.bfloat16)
     expert_ids = lax.broadcasted_iota(jnp.int32, (1, 1, 1, experts), 3)
     picked_logits = jnp.sum(
         jnp.where(routes[..., None] == expert_ids, logits[:, :, None, :], 0.0), -1
@@ -136,7 +135,7 @@
     packed = jnp.einsum(
         "rs,rd->sd",
         sender,
-        normed.reshape(row_count, slice_width),
+        attended.reshape(row_count, slice_width),
         preferred_element_type=jnp.float32,
     )
     outgoing = packed.astype(jnp.bfloat16).reshape(experts, CAP, slice_width)
@@ -146,7 +145,13 @@
 
     pieces = pieces.reshape(
         group_count, tensor_count, owner_count, local_experts, CAP, slice_width
-    )
+    ).astype(jnp.float32)
+    gains = lax.all_gather(norm_gain, "tp", axis=0, tiled=True).astype(jnp.float32)
+    slot_squares = jnp.sum(pieces * pieces, axis=(1, 5), keepdims=True)
+    pieces = (pieces * gains.reshape(1, tensor_count, 1, 1, 1, slice_width)) / jnp.sqrt(
+        slot_squares / width + 1e-05
+    )
+    pieces = pieces.astype(jnp.bfloat16)
     gate_split = w_gate.reshape(local_experts, tensor_count, slice_width, hidden_local)
     up_split = w_up.reshape(local_experts, tensor_count, slice_width, hidden_local)
     gate_sums = jnp.einsum(

time: 256 us -> 258 us (level)
  waiting for transfers between devices: 106 us -> 81.5 us
  blocking collectives: 32.6 us -> 53.1 us
  other arithmetic: 15.9 us -> 25.8 us
    all_gather x0 -> x1, blocking collectives: none -> 21.5 us  [per_device(): lax.all_gather(norm_gain, 'tp', axis=0, tiled=True).astype(jnp.float32)]
    all_gather x1, waiting for transfers between devices: 74.4 us -> 57.3 us  [per_device(): pieces = lax.all_gather(received, ('grp', 'tp'), axis=0, tiled=True)]
    all_to_all x2, waiting for transfers between devices: 12.5 us -> 2.83 us  [exchange_sum(): moved = lax.all_to_all(parts.astype(jnp.bfloat16), axis, 0, 0, tiled=True)]
    reduce_sum x0 -> x2, other arithmetic: none -> 4.09 us  [per_device(): slot_squares = jnp.sum(pieces * pieces, axis=(1, 5), keepdims=True)]
    convert_element_type x1, other arithmetic: 0.64 us -> 4.61 us  [per_device(): pieces = pieces.astype(jnp.bfloat16)]
    dot_general x1, matrix products: 4.72 us -> 1.79 us  [per_device(): jnp.einsum('gtajcd,jtdf->jgacf', pieces, gate_split, preferred_element_ty...]
  transfers between devices with their start and end apart: 24 -> 24, of which waited for: 9 -> 12; matrix products, arithmetic and copies ran while one was open for 9% -> 9% of each run, Pallas kernels for 0% -> 0%
where the time goes in v2:
time: 258 us; the launch traced here: 257 us
  waiting for transfers between devices  81.5 us (32%)
  blocking collectives  53.1 us (21%)
  starting transfers between devices  52.4 us (20%)
  other arithmetic  25.8 us (10%)
  between operations  14.9 us (6%)
  local copies, waits for them, and re-layouts  14.8 us (6%)
  matrix products  14.1 us (5%)
    all_gather x1, waiting for transfers between devices, per_device(): pieces = lax.all_gather(received, ('grp', 'tp'), axis=0, tiled=True)  57.3 us
    ppermute x20, starting transfers between devices, ring_reduce_scatter(): arrived = lax.ppermute(total.astype(jnp.bfloat16), axis, pairs)  29.5 us
    all_gather x1, blocking collectives, per_device(): lax.all_gather(norm_gain, 'tp', axis=0, tiled=True).astype(jnp.float32)  21.5 us
    psum x1, blocking collectives, per_device(): squares, logits = lax.psum((squares, partial_logits), 'tp')  19.5 us
    ppermute x20, waiting for transfers between devices, ring_reduce_scatter(): arrived = lax.ppermute(total.astype(jnp.bfloat16), axis, pairs)  16.2 us
    all_to_all x1, starting transfers between devices, per_device(): lax.all_to_all(summed.astype(jnp.bfloat16), 'ex', split_axis=0, concat_ax...  13.9 us
    all_to_all x1, blocking collectives, per_device(): lax.all_to_all(outgoing, 'ex', split_axis=0, concat_axis=0, tiled=True)  12.1 us
    unnamed x29, local copies, waits for them, and re-layouts  11.5 us
  transfers between devices with their start and end apart: 24, of which 12 were waited for; matrix products, arithmetic and copies ran while one was open for 9% of the time, Pallas kernels for 0%

profile of v2, /device:TPU:1, one launch (start us, length us, event | category | flops | bytes accessed | tf_op | source)
XLA Modules:
  0.0 256.6 jit_solution(5859815401846571486)
XLA Ops:
  7.2 0.8 broadcast_multiply_fusion
  8.1 0.8 copy.163
  10.6 0.9 reshape.542
  11.4 1.3 fusion.85
  12.7 2.3 fusion.84
  17.4 12.1 %all_to_all.20 = bf16[8,16,768]{2,1,0:T(8,128)(2,1)} all-to-all(bf16[8,16,768]{2,1,0:T(8,128)(2,1)S(1)} %bitcast.446), channel_id=1, replica_groups=mesh['grp'=4,'ex'=8,'tp'=8] {'ex'}, dimensions={0} | all-to-all | bytes 393216 | tf_op jit(solution)/shard_map/all_to_all | solution.py:142
  30.0 21.5 %all-gather.1 = bf16[8,1,768]{2,1,0:T(2,128)(2,1)S(1)} all-gather(bf16[1,1,768]{2,1,0:T(2,128)(2,1)S(1)} %reshape.520), channel_id=1, replica_groups=mesh['grp'=4,'ex'=8,'tp'=8] {'tp'}, dimensions={0}, use_global_device_ids=true | all-gather | bytes 13824 | tf_op jit(solution)/shard_map/all_gather | solution.py:149
  51.4 4.7 %copy.186 = bf16[1,256,6144]{1,2,0:T(8,128)(2,1)} copy(bf16[1,256,6144]{2,1,0:T(8,128)(2,1)} %param.25) | data formatting | bytes 6291456 | tf_op args[12]
  56.1 4.4 %copy.227 = bf16[32,8,8,768]{3,2,1,0:T(8,128)(2,1)} copy(bf16[32,8,8,768]{3,1,2,0:T(8,128)(2,1)} %bitcast.440) | data formatting | bytes 6291456
  60.6 57.3 %all-gather.4.cloned.1.call-done = bf16[256,16,768]{2,1,0:T(8,128)(2,1)} async-done(((bf16[8,16,768]{2,1,0:T(8,128)(2,1)}), bf16[256,16,768]{2,1,0:T(8,128)(2,1)}) %all-gather.4.cloned.1.call-update) | async-done | bytes 6291472 | tf_op jit(solution)/shard_map/all_gather | solution.py:144
  117.9 4.1 %multiply_reduce_fusion = f32[256,16]{1,0:T(8,128)S(1)} fusion(bf16[256,16,768]{2,1,0:T(8,128)(2,1)} %all-gather.4.cloned.1.call-done), kind=kLoop, calls=%fused_computation | loop fusion | flops 9433088 | bytes 6307840 | tf_op jit(solution)/shard_map/reduce_sum | solution.py:150
  122.0 4.6 %divide_convert_fusion = bf16[4,8,8,16,768]{4,3,2,1,0:T(8,128)(2,1)S(1)} fusion(f32[4,8,16]{2,1,0:T(8,128)S(1)} %add_sqrt_fusion, f32[8,768]{1,0:T(8,128)S(1)} %bitcast.450, bf16[4,8,8,16,768]{4,3,2,1,0:T(8,128)(2,1)} %bitcast.439), kind=kLoop, calls=%fused_computation.1 | loop fusion | flops 12582912 | bytes 12609536 | tf_op jit(solution)/shard_map/convert_element_type | solution.py:154
  126.6 1.8 convolution_bitcast_fusion.1
  128.5 1.8 fusion.24
  130.4 1.3 fusion
  131.7 1.3 fusion.2
  134.8 1.2 collective-permute-start.7
  136.9 2.7 %collective-permute-start.17 = (bf16[4,4,1,16,768]{4,3,0,1,2:T(8,128)(2,1)S(1)}, bf16[4,4,1,16,768]{4,3,0,1,2:T(8,128)(2,1)S(1)}, u32[]{:S(2)}, u32[]{:S(2)}) collective-permute-start(bf16[4,4,1,16,768]{4,3,0,1,2:T(8,128)(2,1)S(1)} %fusion.41), channel_id=1, source_target_pairs={{0,192},{64,0},{128,64},{192,128},{1,193},{65,1},{129,65},{193,129... | collective-permute-start | bytes 1179656 | tf_op jit(solution)/shard_map/ppermute | solution.py:61
  139.8 2.2 collective-permute-start.8
  142.2 2.5 collective-permute-done.8
  144.8 3.4 %collective-permute-start.9 = (bf16[2,4,1,16,768]{4,3,1,0,2:T(8,128)(2,1)S(1)}, bf16[2,4,1,16,768]{4,3,1,0,2:T(8,128)(2,1)S(1)}, u32[]{:S(2)}, u32[]{:S(2)}) collective-permute-start(bf16[2,4,1,16,768]{4,3,1,0,2:T(8,128)(2,1)S(1)} %fusion.53), channel_id=1, source_target_pairs={{0,7},{1,0},{2,1},{3,2},{4,3},{5,4},{6,5},{7,6},{8,15},{9,8},{10,9... | collective-permute-start | bytes 589832 | tf_op jit(solution)/shard_map/ppermute | solution.py:61
  148.6 2.7 %collective-permute-start.18 = (bf16[4,4,1,16,768]{4,3,0,1,2:T(8,128)(2,1)S(1)}, bf16[4,4,1,16,768]{4,3,0,1,2:T(8,128)(2,1)S(1)}, u32[]{:S(2)}, u32[]{:S(2)}) collective-permute-start(bf16[4,4,1,16,768]{4,3,0,1,2:T(8,128)(2,1)S(1)} %fusion.35), channel_id=1, source_target_pairs={{0,192},{64,0},{128,64},{192,128},{1,193},{65,1},{129,65},{193,129... | collective-permute-start | bytes 1179656 | tf_op jit(solution)/shard_map/ppermute | solution.py:61
  151.4 2.7 %collective-permute-start.10 = (bf16[2,4,1,16,768]{4,3,1,0,2:T(8,128)(2,1)S(1)}, bf16[2,4,1,16,768]{4,3,1,0,2:T(8,128)(2,1)S(1)}, u32[]{:S(2)}, u32[]{:S(2)}) collective-permute-start(bf16[2,4,1,16,768]{4,3,1,0,2:T(8,128)(2,1)S(1)} %fusion.52), channel_id=1, source_target_pairs={{0,7},{1,0},{2,1},{3,2},{4,3},{5,4},{6,5},{7,6},{8,15},{9,8},{10,9... | collective-permute-start | bytes 589832 | tf_op jit(solution)/shard_map/ppermute | solution.py:61
  154.3 3.2 %collective-permute-done.10 = bf16[2,4,1,16,768]{4,3,1,0,2:T(8,128)(2,1)S(1)} collective-permute-done((bf16[2,4,1,16,768]{4,3,1,0,2:T(8,128)(2,1)S(1)}, bf16[2,4,1,16,768]{4,3,1,0,2:T(8,128)(2,1)S(1)}, u32[]{:S(2)}, u32[]{:S(2)}) %collective-permute-start.10) | collective-permute-done | bytes 196640 | tf_op jit(solution)/shard_map/ppermute | solution.py:61
  157.5 3.5 %collective-permute-start.11 = (bf16[2,4,1,16,768]{4,3,1,0,2:T(8,128)(2,1)S(1)}, bf16[2,4,1,16,768]{4,3,1,0,2:T(8,128)(2,1)S(1)}, u32[]{:S(2)}, u32[]{:S(2)}) collective-permute-start(bf16[2,4,1,16,768]{4,3,1,0,2:T(8,128)(2,1)S(1)} %fusion.51), channel_id=1, source_target_pairs={{0,7},{1,0},{2,1},{3,2},{4,3},{5,4},{6,5},{7,6},{8,15},{9,8},{10,9... | collective-permute-start | bytes 589832 | tf_op jit(solution)/shard_map/ppermute | solution.py:61
  161.6 0.8 fusion.34
  162.5 2.6 %collective-permute-start.19 = (bf16[4,4,1,16,768]{4,3,0,1,2:T(8,128)(2,1)}, bf16[4,4,1,16,768]{4,3,0,1,2:T(8,128)(2,1)}, u32[]{:S(2)}, u32[]{:S(2)}) collective-permute-start(bf16[4,4,1,16,768]{4,3,0,1,2:T(8,128)(2,1)} %fusion.34), channel_id=1, source_target_pairs={{0,192},{64,0},{128,64},{192,128},{1,193},{65,1},{129,65},{193,129... | collective-permute-start | bytes 1179656 | tf_op jit(solution)/shard_map/ppermute | solution.py:61
  165.2 3.2 %collective-permute-start.12 = (bf16[2,4,1,16,768]{4,3,1,0,2:T(8,128)(2,1)S(1)}, bf16[2,4,1,16,768]{4,3,1,0,2:T(8,128)(2,1)S(1)}, u32[]{:S(2)}, u32[]{:S(2)}) collective-permute-start(bf16[2,4,1,16,768]{4,3,1,0,2:T(8,128)(2,1)S(1)} %fusion.50), channel_id=1, source_target_pairs={{0,7},{1,0},{2,1},{3,2},{4,3},{5,4},{6,5},{7,6},{8,15},{9,8},{10,9... | collective-permute-start | bytes 589832 | tf_op jit(solution)/shard_map/ppermute | solution.py:61
  169.4 3.2 %collective-permute-done.12 = bf16[2,4,1,16,768]{4,3,1,0,2:T(8,128)(2,1)S(1)} collective-permute-done((bf16[2,4,1,16,768]{4,3,1,0,2:T(8,128)(2,1)S(1)}, bf16[2,4,1,16,768]{4,3,1,0,2:T(8,128)(2,1)S(1)}, u32[]{:S(2)}, u32[]{:S(2)}) %collective-permute-start.12) | collective-permute-done | bytes 196640 | tf_op jit(solution)/shard_map/ppermute | solution.py:61
  172.6 3.5 %collective-permute-start.13 = (bf16[2,4,1,16,768]{4,3,1,0,2:T(8,128)(2,1)S(1)}, bf16[2,4,1,16,768]{4,3,1,0,2:T(8,128)(2,1)S(1)}, u32[]{:S(2)}, u32[]{:S(2)}) collective-permute-start(bf16[2,4,1,16,768]{4,3,1,0,2:T(8,128)(2,1)S(1)} %fusion.49), channel_id=1, source_target_pairs={{0,7},{1,0},{2,1},{3,2},{4,3},{5,4},{6,5},{7,6},{8,15},{9,8},{10,9... | collective-permute-start | bytes 589832 | tf_op jit(solution)/shard_map/ppermute | solution.py:61
  176.1 0.8 collective-permute-done.5
  177.0 0.8 fusion.36
  177.9 1.5 collective-permute-done.13
  179.4 4.0 %collective-permute-done.6 = bf16[2,4,1,16,768]{4,3,1,0,2:T(8,128)(2,1)S(1)} collective-permute-done((bf16[2,4,1,16,768]{4,3,1,0,2:T(8,128)(2,1)S(1)}, bf16[2,4,1,16,768]{4,3,1,0,2:T(8,128)(2,1)S(1)}, u32[]{:S(2)}, u32[]{:S(2)}) %collective-permute-start.6) | collective-permute-done | bytes 196640 | tf_op jit(solution)/shard_map/ppermute | solution.py:61
  183.5 0.8 maximum_bitcast_fusion
  184.3 3.5 %all-to-all-start.1 = ((bf16[4,4,1,16,768]{4,3,1,2,0:T(8,128)(2,1)}), bf16[4,4,1,16,768]{4,3,1,2,0:T(8,128)(2,1)S(1)}, u32[]{:S(2)}, u32[]{:S(2)}) async-start(bf16[4,4,1,16,768]{4,3,1,2,0:T(8,128)(2,1)} %maximum_bitcast_fusion), calls=%async_computation.1 | async-start | bytes 786432 | tf_op jit(solution)/shard_map/all_to_all | solution.py:78
  187.7 1.3 fusion.33
  189.1 1.1 pad_maximum_fusion
  190.1 1.0 copy.189
  191.1 2.8 %all-to-all-done.1 = bf16[4,4,1,16,768]{4,3,1,2,0:T(8,128)(2,1)S(1)} async-done(((bf16[4,4,1,16,768]{4,3,1,2,0:T(8,128)(2,1)}), bf16[4,4,1,16,768]{4,3,1,2,0:T(8,128)(2,1)S(1)}, u32[]{:S(2)}, u32[]{:S(2)}) %all-to-all-start.1) | async-done | bytes 393248 | tf_op jit(solution)/shard_map/all_to_all | solution.py:78
  193.9 5.4 %all-to-all-start.2 = ((bf16[8,4,1,16,768]{4,3,1,2,0:T(8,128)(2,1)}), bf16[8,4,1,16,768]{4,3,1,2,0:T(8,128)(2,1)}, u32[]{:S(2)}, u32[]{:S(2)}) async-start(bf16[8,4,1,16,768]{4,3,1,2,0:T(8,128)(2,1)} %copy.189), calls=%async_computation.2 | async-start | bytes 1572864 | tf_op jit(solution)/shard_map/all_to_all | solution.py:78
  201.3 2.0 fusion.66
  203.3 19.5 %all-reduce = (f32[16,2,8]{0,2,1:T(8,128)}, f32[16,2]{0,1:T(2,128)}) all-reduce(f32[16,2,8]{0,2,1:T(8,128)} %fusion.66, f32[16,2]{0,1:T(2,128)} %get-tuple-element.16), channel_id=1, replica_groups=mesh['grp'=4,'ex'=8,'tp'=8] {'tp'}, use_global_device_ids=true, to_apply=%region_4.5 | all-reduce | flops 288 | bytes 2304 | tf_op jit(solution)/shard_map/psum | solution.py:112
  224.2 1.3 select_reduce_fusion.1
  226.2 1.2 reduce.12
  227.4 1.6 pad_maximum_fusion.1
  229.0 13.9 %all-to-all-start.3 = ((bf16[8,1,16,768]{3,2,1,0:T(8,128)(2,1)}), bf16[8,1,16,768]{3,2,1,0:T(8,128)(2,1)S(1)}, u32[]{:S(2)}, u32[]{:S(2)}) async-start(bf16[8,1,16,768]{3,2,1,0:T(8,128)(2,1)} %pad_maximum_fusion.1), calls=%async_computation.3 | async-start | bytes 393216 | tf_op jit(solution)/shard_map/all_to_all | solution.py:187
  243.7 5.1 %all-to-all-done.3 = bf16[8,1,16,768]{3,2,1,0:T(8,128)(2,1)S(1)} async-done(((bf16[8,1,16,768]{3,2,1,0:T(8,128)(2,1)}), bf16[8,1,16,768]{3,2,1,0:T(8,128)(2,1)S(1)}, u32[]{:S(2)}, u32[]{:S(2)}) %all-to-all-start.3) | async-done | bytes 196640 | tf_op jit(solution)/shard_map/all_to_all | solution.py:187
  (109 shorter events, 15.5 us)
Async XLA Ops:
  7.2 119.5 %copy-start = (bf16[1,6144,256]{2,1,0:T(8,128)(2,1)S(1)}, bf16[1,6144,256]{2,1,0:T(8,128)(2,1)}, u32[]{:S(2)}) copy-start(bf16[1,6144,256]{2,1,0:T(8,128)(2,1)} %param.23) | copy-start | bytes 9437188
  7.2 8.3 %copy-start.10 = (bf16[16,2,128]{2,1,0:T(2,128)(2,1)S(1)}, bf16[16,2,128]{2,1,0:T(2,128)(2,1)}, u32[]{:S(2)}) copy-start(bf16[16,2,128]{2,1,0:T(2,128)(2,1)} %param.16) | copy-start | bytes 24580
  7.2 110.7 %all-gather.4.cloned.1.call-start = ((), (), s32[]{:S(2)}) async-start(), calls=%async_computation.4 | async-start | bytes 6488064 | tf_op jit(solution)/shard_map/all_gather | solution.py:144
  11.4 4.4 %copy-start.9 = (bf16[16,1,512,128]{3,2,1,0:T(8,128)(2,1)S(1)}, bf16[16,1,512,128]{3,2,1,0:T(8,128)(2,1)}, u32[]{:S(2)}) copy-start(bf16[16,1,512,128]{3,2,1,0:T(8,128)(2,1)} %param.18) | copy-start | bytes 6291460
  15.1 1.4 copy-start.6
  15.8 14.1 %copy-start.7 = (bf16[768]{0:T(1024)(128)(2,1)S(1)}, bf16[768]{0:T(1024)(128)(2,1)}, u32[]{:S(2)}) copy-start(bf16[768]{0:T(1024)(128)(2,1)} %param.20) | copy-start | bytes 4612
  16.4 39.7 %copy-start.4 = (f32[16,2,768]{2,1,0:T(2,128)}, f32[16,2,768]{2,1,0:T(2,128)S(1)}, u32[]{:S(2)}) copy-start(f32[16,2,768]{2,1,0:T(2,128)S(1)} %reshape.541) | copy-start | bytes 294916
  17.1 39.0 %copy-start.5 = (bf16[16,2,768]{2,1,0:T(2,128)(2,1)}, bf16[16,2,768]{2,1,0:T(2,128)(2,1)S(1)}, u32[]{:S(2)}) copy-start(bf16[16,2,768]{2,1,0:T(2,128)(2,1)S(1)} %copy.192) | copy-start | bytes 147460
  126.6 1.9 copy-start.8
  128.5 1.9 copy-start.1
  131.7 1.9 copy-start.2
  134.8 26.8 %copy-start.3 = (f32[4,4,16,4,768]{4,2,3,1,0:T(8,128)}, f32[4,4,16,4,768]{4,2,3,1,0:T(8,128)S(1)}, u32[]{:S(2)}) copy-start(f32[4,4,16,4,768]{4,2,3,1,0:T(8,128)S(1)} %fusion.8) | copy-start | bytes 9437188
  134.8 4.9 %collective-permute-start.7 = (bf16[2,4,1,16,768]{4,3,1,0,2:T(8,128)(2,1)S(1)}, bf16[2,4,1,16,768]{4,3,1,0,2:T(8,128)(2,1)S(1)}, u32[]{:S(2)}, u32[]{:S(2)}) collective-permute-start(bf16[2,4,1,16,768]{4,3,1,0,2:T(8,128)(2,1)S(1)} %fusion.60), channel_id=1, source_target_pairs={{0,7},{1,0},{2,1},{3,2},{4,3},{5,4},{6,5},{7,6},{8,15},{9,8},{10,9... | collective-permute-start | bytes 589832 | tf_op jit(solution)/shard_map/ppermute | solution.py:61
  136.0 6.0 %collective-permute-start = (bf16[2,4,1,16,768]{4,3,1,0,2:T(8,128)(2,1)S(1)}, bf16[2,4,1,16,768]{4,3,1,0,2:T(8,128)(2,1)S(1)}, u32[]{:S(2)}, u32[]{:S(2)}) collective-permute-start(bf16[2,4,1,16,768]{4,3,1,0,2:T(8,128)(2,1)S(1)} %fusion.61), channel_id=1, source_target_pairs={{0,1},{1,2},{2,3},{3,4},{4,5},{5,6},{6,7},{7,0},{8,9},{9,10},{10,1... | collective-permute-start | bytes 589832 | tf_op jit(solution)/shard_map/ppermute | solution.py:61
  136.5 11.8 %collective-permute-start.14 = (bf16[4,4,1,16,768]{4,3,0,1,2:T(8,128)(2,1)S(1)}, bf16[4,4,1,16,768]{4,3,0,1,2:T(8,128)(2,1)S(1)}, u32[]{:S(2)}, u32[]{:S(2)}) collective-permute-start(bf16[4,4,1,16,768]{4,3,0,1,2:T(8,128)(2,1)S(1)} %fusion.40), channel_id=1, source_target_pairs={{0,64},{64,128},{128,192},{192,0},{1,65},{65,129},{129,193},{193,1... | collective-permute-start | bytes 1179656 | tf_op jit(solution)/shard_map/ppermute | solution.py:61
  136.9 11.6 %collective-permute-start.17 = (bf16[4,4,1,16,768]{4,3,0,1,2:T(8,128)(2,1)S(1)}, bf16[4,4,1,16,768]{4,3,0,1,2:T(8,128)(2,1)S(1)}, u32[]{:S(2)}, u32[]{:S(2)}) collective-permute-start(bf16[4,4,1,16,768]{4,3,0,1,2:T(8,128)(2,1)S(1)} %fusion.41), channel_id=1, source_target_pairs={{0,192},{64,0},{128,64},{192,128},{1,193},{65,1},{129,65},{193,129... | collective-permute-start | bytes 1179656 | tf_op jit(solution)/shard_map/ppermute | solution.py:61
  139.8 4.9 %collective-permute-start.8 = (bf16[2,4,1,16,768]{4,3,1,0,2:T(8,128)(2,1)S(1)}, bf16[2,4,1,16,768]{4,3,1,0,2:T(8,128)(2,1)S(1)}, u32[]{:S(2)}, u32[]{:S(2)}) collective-permute-start(bf16[2,4,1,16,768]{4,3,1,0,2:T(8,128)(2,1)S(1)} %fusion.54), channel_id=1, source_target_pairs={{0,7},{1,0},{2,1},{3,2},{4,3},{5,4},{6,5},{7,6},{8,15},{9,8},{10,9... | collective-permute-start | bytes 589832 | tf_op jit(solution)/shard_map/ppermute | solution.py:61
  142.1 6.1 %collective-permute-start.1 = (bf16[2,4,1,16,768]{4,3,1,0,2:T(8,128)(2,1)S(1)}, bf16[2,4,1,16,768]{4,3,1,0,2:T(8,128)(2,1)S(1)}, u32[]{:S(2)}, u32[]{:S(2)}) collective-permute-start(bf16[2,4,1,16,768]{4,3,1,0,2:T(8,128)(2,1)S(1)} %fusion.47), channel_id=1, source_target_pairs={{0,1},{1,2},{2,3},{3,4},{4,5},{5,6},{6,7},{7,0},{8,9},{9,10},{10,1... | collective-permute-start | bytes 589832 | tf_op jit(solution)/shard_map/ppermute | solution.py:61
  144.8 6.6 %collective-permute-start.9 = (bf16[2,4,1,16,768]{4,3,1,0,2:T(8,128)(2,1)S(1)}, bf16[2,4,1,16,768]{4,3,1,0,2:T(8,128)(2,1)S(1)}, u32[]{:S(2)}, u32[]{:S(2)}) collective-permute-start(bf16[2,4,1,16,768]{4,3,1,0,2:T(8,128)(2,1)S(1)} %fusion.53), channel_id=1, source_target_pairs={{0,7},{1,0},{2,1},{3,2},{4,3},{5,4},{6,5},{7,6},{8,15},{9,8},{10,9... | collective-permute-start | bytes 589832 | tf_op jit(solution)/shard_map/ppermute | solution.py:61
  148.2 5.9 %collective-permute-start.2 = (bf16[2,4,1,16,768]{4,3,1,0,2:T(8,128)(2,1)S(1)}, bf16[2,4,1,16,768]{4,3,1,0,2:T(8,128)(2,1)S(1)}, u32[]{:S(2)}, u32[]{:S(2)}) collective-permute-start(bf16[2,4,1,16,768]{4,3,1,0,2:T(8,128)(2,1)S(1)} %fusion.46), channel_id=1, source_target_pairs={{0,1},{1,2},{2,3},{3,4},{4,5},{5,6},{6,7},{7,0},{8,9},{9,10},{10,1... | collective-permute-start | bytes 589832 | tf_op jit(solution)/shard_map/ppermute | solution.py:61
  148.4 13.0 %collective-permute-start.15 = (bf16[4,4,1,16,768]{4,3,0,1,2:T(8,128)(2,1)S(1)}, bf16[4,4,1,16,768]{4,3,0,1,2:T(8,128)(2,1)S(1)}, u32[]{:S(2)}, u32[]{:S(2)}) collective-permute-start(bf16[4,4,1,16,768]{4,3,0,1,2:T(8,128)(2,1)S(1)} %fusion.38), channel_id=1, source_target_pairs={{0,64},{64,128},{128,192},{192,0},{1,65},{65,129},{129,193},{193,1... | collective-permute-start | bytes 1179656 | tf_op jit(solution)/shard_map/ppermute | solution.py:61
  148.6 13.0 %collective-permute-start.18 = (bf16[4,4,1,16,768]{4,3,0,1,2:T(8,128)(2,1)S(1)}, bf16[4,4,1,16,768]{4,3,0,1,2:T(8,128)(2,1)S(1)}, u32[]{:S(2)}, u32[]{:S(2)}) collective-permute-start(bf16[4,4,1,16,768]{4,3,0,1,2:T(8,128)(2,1)S(1)} %fusion.35), channel_id=1, source_target_pairs={{0,192},{64,0},{128,64},{192,128},{1,193},{65,1},{129,65},{193,129... | collective-permute-start | bytes 1179656 | tf_op jit(solution)/shard_map/ppermute | solution.py:61
  151.4 6.0 %collective-permute-start.10 = (bf16[2,4,1,16,768]{4,3,1,0,2:T(8,128)(2,1)S(1)}, bf16[2,4,1,16,768]{4,3,1,0,2:T(8,128)(2,1)S(1)}, u32[]{:S(2)}, u32[]{:S(2)}) collective-permute-start(bf16[2,4,1,16,768]{4,3,1,0,2:T(8,128)(2,1)S(1)} %fusion.52), channel_id=1, source_target_pairs={{0,7},{1,0},{2,1},{3,2},{4,3},{5,4},{6,5},{7,6},{8,15},{9,8},{10,9... | collective-permute-start | bytes 589832 | tf_op jit(solution)/shard_map/ppermute | solution.py:61
  154.2 7.1 %collective-permute-start.3 = (bf16[2,4,1,16,768]{4,3,1,0,2:T(8,128)(2,1)S(1)}, bf16[2,4,1,16,768]{4,3,1,0,2:T(8,128)(2,1)S(1)}, u32[]{:S(2)}, u32[]{:S(2)}) collective-permute-start(bf16[2,4,1,16,768]{4,3,1,0,2:T(8,128)(2,1)S(1)} %fusion.45), channel_id=1, source_target_pairs={{0,1},{1,2},{2,3},{3,4},{4,5},{5,6},{6,7},{7,0},{8,9},{9,10},{10,1... | collective-permute-start | bytes 589832 | tf_op jit(solution)/shard_map/ppermute | solution.py:61
  157.5 7.6 %collective-permute-start.11 = (bf16[2,4,1,16,768]{4,3,1,0,2:T(8,128)(2,1)S(1)}, bf16[2,4,1,16,768]{4,3,1,0,2:T(8,128)(2,1)S(1)}, u32[]{:S(2)}, u32[]{:S(2)}) collective-permute-start(bf16[2,4,1,16,768]{4,3,1,0,2:T(8,128)(2,1)S(1)} %fusion.51), channel_id=1, source_target_pairs={{0,7},{1,0},{2,1},{3,2},{4,3},{5,4},{6,5},{7,6},{8,15},{9,8},{10,9... | collective-permute-start | bytes 589832 | tf_op jit(solution)/shard_map/ppermute | solution.py:61
  161.3 7.6 %collective-permute-start.4 = (bf16[2,4,1,16,768]{4,3,1,0,2:T(8,128)(2,1)S(1)}, bf16[2,4,1,16,768]{4,3,1,0,2:T(8,128)(2,1)S(1)}, u32[]{:S(2)}, u32[]{:S(2)}) collective-permute-start(bf16[2,4,1,16,768]{4,3,1,0,2:T(8,128)(2,1)S(1)} %fusion.44), channel_id=1, source_target_pairs={{0,1},{1,2},{2,3},{3,4},{4,5},{5,6},{6,7},{7,0},{8,9},{9,10},{10,1... | collective-permute-start | bytes 589832 | tf_op jit(solution)/shard_map/ppermute | solution.py:61
  161.5 15.5 %collective-permute-start.16 = (bf16[4,4,1,16,768]{4,3,0,1,2:T(8,128)(2,1)S(1)}, bf16[4,4,1,16,768]{4,3,0,1,2:T(8,128)(2,1)S(1)}, u32[]{:S(2)}, u32[]{:S(2)}) collective-permute-start(bf16[4,4,1,16,768]{4,3,0,1,2:T(8,128)(2,1)S(1)} %fusion.37), channel_id=1, source_target_pairs={{0,64},{64,128},{128,192},{192,0},{1,65},{65,129},{129,193},{193,1... | collective-permute-start | bytes 1179656 | tf_op jit(solution)/shard_map/ppermute | solution.py:61
  162.5 25.2 %collective-permute-start.19 = (bf16[4,4,1,16,768]{4,3,0,1,2:T(8,128)(2,1)}, bf16[4,4,1,16,768]{4,3,0,1,2:T(8,128)(2,1)}, u32[]{:S(2)}, u32[]{:S(2)}) collective-permute-start(bf16[4,4,1,16,768]{4,3,0,1,2:T(8,128)(2,1)} %fusion.34), channel_id=1, source_target_pairs={{0,192},{64,0},{128,64},{192,128},{1,193},{65,1},{129,65},{193,129... | collective-permute-start | bytes 1179656 | tf_op jit(solution)/shard_map/ppermute | solution.py:61
  165.2 7.3 %collective-permute-start.12 = (bf16[2,4,1,16,768]{4,3,1,0,2:T(8,128)(2,1)S(1)}, bf16[2,4,1,16,768]{4,3,1,0,2:T(8,128)(2,1)S(1)}, u32[]{:S(2)}, u32[]{:S(2)}) collective-permute-start(bf16[2,4,1,16,768]{4,3,1,0,2:T(8,128)(2,1)S(1)} %fusion.50), channel_id=1, source_target_pairs={{0,7},{1,0},{2,1},{3,2},{4,3},{5,4},{6,5},{7,6},{8,15},{9,8},{10,9... | collective-permute-start | bytes 589832 | tf_op jit(solution)/shard_map/ppermute | solution.py:61
  169.0 7.9 %collective-permute-start.5 = (bf16[2,4,1,16,768]{4,3,1,0,2:T(8,128)(2,1)S(1)}, bf16[2,4,1,16,768]{4,3,1,0,2:T(8,128)(2,1)S(1)}, u32[]{:S(2)}, u32[]{:S(2)}) collective-permute-start(bf16[2,4,1,16,768]{4,3,1,0,2:T(8,128)(2,1)S(1)} %fusion.43), channel_id=1, source_target_pairs={{0,1},{1,2},{2,3},{3,4},{4,5},{5,6},{6,7},{7,0},{8,9},{9,10},{10,1... | collective-permute-start | bytes 589832 | tf_op jit(solution)/shard_map/ppermute | solution.py:61
  172.6 6.8 %collective-permute-start.13 = (bf16[2,4,1,16,768]{4,3,1,0,2:T(8,128)(2,1)S(1)}, bf16[2,4,1,16,768]{4,3,1,0,2:T(8,128)(2,1)S(1)}, u32[]{:S(2)}, u32[]{:S(2)}) collective-permute-start(bf16[2,4,1,16,768]{4,3,1,0,2:T(8,128)(2,1)S(1)} %fusion.49), channel_id=1, source_target_pairs={{0,7},{1,0},{2,1},{3,2},{4,3},{5,4},{6,5},{7,6},{8,15},{9,8},{10,9... | collective-permute-start | bytes 589832 | tf_op jit(solution)/shard_map/ppermute | solution.py:61
  176.9 6.5 %collective-permute-start.6 = (bf16[2,4,1,16,768]{4,3,1,0,2:T(8,128)(2,1)S(1)}, bf16[2,4,1,16,768]{4,3,1,0,2:T(8,128)(2,1)S(1)}, u32[]{:S(2)}, u32[]{:S(2)}) collective-permute-start(bf16[2,4,1,16,768]{4,3,1,0,2:T(8,128)(2,1)S(1)} %fusion.42), channel_id=1, source_target_pairs={{0,1},{1,2},{2,3},{3,4},{4,5},{5,6},{6,7},{7,0},{8,9},{9,10},{10,1... | collective-permute-start | bytes 589832 | tf_op jit(solution)/shard_map/ppermute | solution.py:61
  184.3 9.7 %all-to-all-start.1 = ((bf16[4,4,1,16,768]{4,3,1,2,0:T(8,128)(2,1)}), bf16[4,4,1,16,768]{4,3,1,2,0:T(8,128)(2,1)S(1)}, u32[]{:S(2)}, u32[]{:S(2)}) async-start(bf16[4,4,1,16,768]{4,3,1,2,0:T(8,128)(2,1)} %maximum_bitcast_fusion), calls=%async_computation.1 | async-start | bytes 786432 | tf_op jit(solution)/shard_map/all_to_all | solution.py:78
  193.9 32.3 %all-to-all-start.2 = ((bf16[8,4,1,16,768]{4,3,1,2,0:T(8,128)(2,1)}), bf16[8,4,1,16,768]{4,3,1,2,0:T(8,128)(2,1)}, u32[]{:S(2)}, u32[]{:S(2)}) async-start(bf16[8,4,1,16,768]{4,3,1,2,0:T(8,128)(2,1)} %copy.189), calls=%async_computation.2 | async-start | bytes 1572864 | tf_op jit(solution)/shard_map/all_to_all | solution.py:78
  229.0 19.8 %all-to-all-start.3 = ((bf16[8,1,16,768]{3,2,1,0:T(8,128)(2,1)}), bf16[8,1,16,768]{3,2,1,0:T(8,128)(2,1)S(1)}, u32[]{:S(2)}, u32[]{:S(2)}) async-start(bf16[8,1,16,768]{3,2,1,0:T(8,128)(2,1)} %pad_maximum_fusion.1), calls=%async_computation.3 | async-start | bytes 393216 | tf_op jit(solution)/shard_map/all_to_all | solution.py:187
Sparse Core Ops, SparseCore 0:
  29.7 88.1 all-gather.3

commit v3 on v2

--- a/solution.py
+++ b/solution.py
@@ -109,15 +109,14 @@
     squares = jnp.sum(state * state, -1)
     scaled = state * norm_gain.astype(jnp.float32)
     partial_logits = jnp.einsum("esd,dx->esx", scaled, router, precision=lax.Precision.HIGHEST)
-    squares, logits = lax.psum((squares, partial_logits), "tp")
-    root_mean = jnp.sqrt(squares / width + 1e-05)[..., None]
-    logits = logits / root_mean
-    expert_ids = lax.broadcasted_iota(jnp.int32, (1, 1, 1, experts), 3)
-    picked_logits = jnp.sum(
-        jnp.where(routes[..., None] == expert_ids, logits[:, :, None, :], 0.0), -1
-    )
-    first_gate = 1.0 / (1.0 + jnp.exp(picked_logits[..., 1] - picked_logits[..., 0]))
-    second_gate = 1.0 - first_gate
+    stats = jnp.concatenate([squares[..., None], partial_logits], axis=-1)
+    stats_high = stats.astype(jnp.bfloat16)
+    stats_low = (stats - stats_high.astype(jnp.float32)).astype(jnp.bfloat16)
+    stat_count = stats.size
+    extras = jnp.zeros((2, slice_width), jnp.bfloat16)
+    extras = extras.at[0].set(norm_gain)
+    extras = extras.at[1, :stat_count].set(stats_high.reshape(stat_count))
+    extras = extras.at[1, stat_count : 2 * stat_count].set(stats_low.reshape(stat_count))
     flat_routes = routes.reshape(row_count * topk)
     expert_hits = (flat_routes[:, None] == lax.broadcasted_iota(jnp.int32, (1, experts), 1)).astype(
         jnp.int32
@@ -140,13 +139,30 @@
     )
     outgoing = packed.astype(jnp.bfloat16).reshape(experts, CAP, slice_width)
     received = lax.all_to_all(outgoing, "ex", split_axis=0, concat_axis=0, tiled=True)
-    received = received.reshape(1, owner_count, local_experts, CAP, slice_width)
-    pieces = lax.all_gather(received, ("grp", "tp"), axis=0, tiled=True)
+    block_rows = owner_count * local_experts * CAP
+    payload = jnp.concatenate([received.reshape(block_rows, slice_width), extras], axis=0)
+    gathered = lax.all_gather(payload[None], ("grp", "tp"), axis=0, tiled=True)
+    pieces = gathered[:, :block_rows]
+    gain_rows = gathered[:, block_rows]
+    stat_rows = gathered[:, block_rows + 1].reshape(group_count, tensor_count, slice_width)
+    stat_rows = lax.dynamic_index_in_dim(stat_rows, lax.axis_index("grp"), 0, keepdims=False)
+    stat_rows = stat_rows.astype(jnp.float32)
+    stats = jnp.sum(stat_rows[:, :stat_count] + stat_rows[:, stat_count : 2 * stat_count], 0)
+    stats = stats.reshape(env_count, step_count, experts + 1)
+    squares, logits = stats[..., 0], stats[..., 1:]
+    root_mean = jnp.sqrt(squares / width + 1e-05)[..., None]
+    logits = logits / root_mean
+    expert_ids = lax.broadcasted_iota(jnp.int32, (1, 1, 1, experts), 3)
+    picked_logits = jnp.sum(
+        jnp.where(routes[..., None] == expert_ids, logits[:, :, None, :], 0.0), -1
+    )
+    first_gate = 1.0 / (1.0 + jnp.exp(picked_logits[..., 1] - picked_logits[..., 0]))
+    second_gate = 1.0 - first_gate
 
     pieces = pieces.reshape(
         group_count, tensor_count, owner_count, local_experts, CAP, slice_width
     ).astype(jnp.float32)
-    gains = lax.all_gather(norm_gain, "tp", axis=0, tiled=True).astype(jnp.float32)
+    gains = gain_rows.reshape(group_count, width)[0].astype(jnp.float32)
     slot_squares = jnp.sum(pieces * pieces, axis=(1, 5), keepdims=True)
     pieces = (pieces * gains.reshape(1, tensor_count, 1, 1, 1, slice_width)) / jnp.sqrt(
         slot_squares / width + 1e-05

time: 258 us -> 267 us (1.035)
  blocking collectives: 53.1 us -> 0 us
  waiting for transfers between devices: 81.5 us -> 114 us
  other arithmetic: 25.8 us -> 39.9 us
  local copies, waits for them, and re-layouts: 14.8 us -> 21.1 us
  starting transfers between devices: 52.4 us -> 58.1 us
  matrix products: 14.1 us -> 16.9 us
    all_gather x1, waiting for transfers between devices: 57.3 us -> 80.8 us  [per_device(): gathered = lax.all_gather(payload[None], ('grp', 'tp'), axis=0, tiled=True)]
    all_gather x1 -> x0, blocking collectives: 21.5 us -> none  [per_device(): lax.all_gather(norm_gain, 'tp', axis=0, tiled=True).astype(jnp.float32)]
    psum x1 -> x0, blocking collectives: 19.5 us -> none  [per_device(): squares, logits = lax.psum((squares, partial_logits), 'tp')]
    all_to_all x1 -> x0, blocking collectives: 12.1 us -> none  [per_device(): lax.all_to_all(outgoing, 'ex', split_axis=0, concat_axis=0, tiled=True)]
    convert_element_type x0 -> x4, other arithmetic: none -> 9.84 us  [the longest x1 8.91 us: per_device(): pieces = pieces.reshape(group_count, tensor_count, owner_count, local_exp...]
    all_to_all x0 -> x1, starting transfers between devices: none -> 6.49 us  [per_device(): lax.all_to_all(outgoing, 'ex', split_axis=0, concat_axis=0, tiled=True)]
    all_to_all x2, waiting for transfers between devices: 2.83 us -> 7.96 us  [exchange_sum(): moved = lax.all_to_all(parts.astype(jnp.bfloat16), axis, 0, 0, tiled=True)]
    convert_element_type x1, other arithmetic: 4.61 us -> 9.42 us  [per_device(): pieces = pieces.astype(jnp.bfloat16)]
  transfers between devices with their start and end apart: 24 -> 25, of which waited for: 12 -> 10; matrix products, arithmetic and copies ran while one was open for 9% -> 10% of each run, Pallas kernels for 0% -> 0%
where the time goes in v3:
time: 267 us; the launch traced here: 265 us
  waiting for transfers between devices  114 us (43%)
  starting transfers between devices  58.1 us (22%)
  other arithmetic  39.9 us (15%)
  local copies, waits for them, and re-layouts  21.1 us (8%)
  matrix products  16.9 us (6%)
  between operations  15.1 us (6%)
    all_gather x1, waiting for transfers between devices, per_device(): gathered = lax.all_gather(payload[None], ('grp', 'tp'), axis=0, tiled=True)  80.8 us
    ppermute x20, starting transfers between devices, ring_reduce_scatter(): arrived = lax.ppermute(total.astype(jnp.bfloat16), axis, pairs)  29.1 us
    ppermute x20, waiting for transfers between devices, ring_reduce_scatter(): arrived = lax.ppermute(total.astype(jnp.bfloat16), axis, pairs)  15.1 us
    all_to_all x1, starting transfers between devices, per_device(): lax.all_to_all(summed.astype(jnp.bfloat16), 'ex', split_axis=0, concat_ax...  14.1 us
    unnamed x32, local copies, waits for them, and re-layouts  13.1 us
    convert_element_type x1, other arithmetic, per_device(): pieces = pieces.astype(jnp.bfloat16)  9.42 us
    convert_element_type x1, other arithmetic, per_device(): pieces = pieces.reshape(group_count, tensor_count, owner_count, local_exp...  8.91 us
    all_to_all x2, starting transfers between devices, exchange_sum(): moved = lax.all_to_all(parts.astype(jnp.bfloat16), axis, 0, 0, tiled=True)  8.47 us
  transfers between devices with their start and end apart: 25, of which 10 were waited for; matrix products, arithmetic and copies ran while one was open for 10% of the time, Pallas kernels for 0%

profile of v3, /device:TPU:1, one launch (start us, length us, event | category | flops | bytes accessed | tf_op | source)
XLA Modules:
  0.0 265.3 jit_solution(2073772445635283197)
XLA Ops:
  7.2 0.9 copy.217
  10.4 2.5 fusion.85
  12.9 1.1 fusion.86
  16.6 0.9 convolution_convert_fusion
  17.5 6.5 %all-to-all-start = ((bf16[8,16,768]{2,1,0:T(8,128)(2,1)}), bf16[8,16,768]{2,1,0:T(8,128)(2,1)S(1)}, u32[]{:S(2)}, u32[]{:S(2)}) async-start(bf16[8,16,768]{2,1,0:T(8,128)(2,1)} %bitcast.460), calls=%async_computation | async-start | bytes 393216 | tf_op jit(solution)/shard_map/all_to_all | solution.py:141
  25.3 4.6 %all-to-all-done = bf16[8,16,768]{2,1,0:T(8,128)(2,1)S(1)} async-done(((bf16[8,16,768]{2,1,0:T(8,128)(2,1)}), bf16[8,16,768]{2,1,0:T(8,128)(2,1)S(1)}, u32[]{:S(2)}, u32[]{:S(2)}) %all-to-all-start) | async-done | bytes 196640 | tf_op jit(solution)/shard_map/all_to_all | solution.py:141
  30.9 4.7 %copy.246 = bf16[1,256,6144]{1,2,0:T(8,128)(2,1)} copy(bf16[1,256,6144]{2,1,0:T(8,128)(2,1)} %param.31) | data formatting | bytes 6291456 | tf_op args[12]
  35.7 4.5 %copy.289 = bf16[32,8,8,768]{3,2,1,0:T(8,128)(2,1)} copy(bf16[32,8,8,768]{3,1,2,0:T(8,128)(2,1)} %bitcast.453) | data formatting | bytes 6291456
  40.2 80.8 %all-gather.4.cloned.1.call-done = bf16[32,130,768]{2,1,0:T(8,128)(2,1)} async-done(((bf16[1,130,768]{2,1,0:T(8,128)(2,1)}), bf16[32,130,768]{2,1,0:T(8,128)(2,1)}) %all-gather.4.cloned.1.call-update) | async-done | bytes 6389776 | tf_op jit(solution)/shard_map/all_gather | solution.py:144
  120.9 4.1 %multiply_reduce_fusion = f32[32,128]{1,0:T(8,128)S(1)} fusion(bf16[32,130,768]{2,1,0:T(8,128)(2,1)} %all-gather.4.cloned.1.call-done), kind=kLoop, calls=%fused_computation.1 | loop fusion | flops 9433088 | bytes 6307840 | tf_op jit(solution)/shard_map/reduce_sum | solution.py:166
  125.2 0.9 slice_convert_fusion.1
  126.1 8.9 %slice_convert_fusion = f32[32,128,768]{2,1,0:T(8,128)} fusion(bf16[32,130,768]{2,1,0:T(8,128)(2,1)} %all-gather.4.cloned.1.call-done), kind=kLoop, calls=%fused_computation.2 | loop fusion | flops 3145728 | bytes 18874368 | tf_op jit(solution)/shard_map/convert_element_type | solution.py:164
  135.0 9.4 %divide_convert_fusion = bf16[4,8,8,16,768]{4,3,2,1,0:T(8,128)(2,1)} fusion(f32[4,8,8,16,768]{4,3,2,1,0:T(8,128)} %bitcast.452, f32[4,8,16]{2,1,0:T(8,128)S(1)} %add_sqrt_fusion, f32[8,768]{1,0:T(8,128)S(1)} %bitcast.464), kind=kLoop, calls=%fused_computation | loop fusion | flops 9437184 | bytes 18900992 | tf_op jit(solution)/shard_map/convert_element_type | solution.py:170
  144.4 4.7 %convolution_bitcast_fusion.1 = f32[4,8,16,256]{3,2,1,0:T(8,128)S(1)} fusion(bf16[4,8,8,16,768]{4,3,2,1,0:T(8,128)(2,1)} %divide_convert_fusion, bf16[8,768,256,1,1]{2,1,4,0,3:T(8,128)(2,1)S(1)} %bitcast.451), kind=kOutput, calls=%fused_computation.17 | convolution fusion | flops 1610612736 | bytes 9961472 | tf_op jit(solution)/shard_map/gtajcd,jtdf->jgacf/dot_general | solution.py:173
  150.0 1.8 fusion.24
  151.8 1.3 fusion.2
  153.1 1.3 fusion
  156.4 2.9 %collective-permute-start.7 = (bf16[2,4,1,16,768]{4,3,1,0,2:T(8,128)(2,1)S(1)}, bf16[2,4,1,16,768]{4,3,1,0,2:T(8,128)(2,1)S(1)}, u32[]{:S(2)}, u32[]{:S(2)}) collective-permute-start(bf16[2,4,1,16,768]{4,3,1,0,2:T(8,128)(2,1)S(1)} %fusion.60), channel_id=1, source_target_pairs={{0,7},{1,0},{2,1},{3,2},{4,3},{5,4},{6,5},{7,6},{8,15},{9,8},{10,9... | collective-permute-start | bytes 589832 | tf_op jit(solution)/shard_map/ppermute | solution.py:61
  159.5 2.7 %collective-permute-start.17 = (bf16[4,4,1,16,768]{4,3,0,1,2:T(8,128)(2,1)S(1)}, bf16[4,4,1,16,768]{4,3,0,1,2:T(8,128)(2,1)S(1)}, u32[]{:S(2)}, u32[]{:S(2)}) collective-permute-start(bf16[4,4,1,16,768]{4,3,0,1,2:T(8,128)(2,1)S(1)} %fusion.41), channel_id=1, source_target_pairs={{0,192},{64,0},{128,64},{192,128},{1,193},{65,1},{129,65},{193,129... | collective-permute-start | bytes 1179656 | tf_op jit(solution)/shard_map/ppermute | solution.py:61
  163.1 2.7 %collective-permute-start.8 = (bf16[2,4,1,16,768]{4,3,1,0,2:T(8,128)(2,1)S(1)}, bf16[2,4,1,16,768]{4,3,1,0,2:T(8,128)(2,1)S(1)}, u32[]{:S(2)}, u32[]{:S(2)}) collective-permute-start(bf16[2,4,1,16,768]{4,3,1,0,2:T(8,128)(2,1)S(1)} %fusion.54), channel_id=1, source_target_pairs={{0,7},{1,0},{2,1},{3,2},{4,3},{5,4},{6,5},{7,6},{8,15},{9,8},{10,9... | collective-permute-start | bytes 589832 | tf_op jit(solution)/shard_map/ppermute | solution.py:61
  165.8 3.2 %collective-permute-done.1 = bf16[2,4,1,16,768]{4,3,1,0,2:T(8,128)(2,1)S(1)} collective-permute-done((bf16[2,4,1,16,768]{4,3,1,0,2:T(8,128)(2,1)S(1)}, bf16[2,4,1,16,768]{4,3,1,0,2:T(8,128)(2,1)S(1)}, u32[]{:S(2)}, u32[]{:S(2)}) %collective-permute-start.1) | collective-permute-done | bytes 196640 | tf_op jit(solution)/shard_map/ppermute | solution.py:61
  169.2 2.7 %collective-permute-start.9 = (bf16[2,4,1,16,768]{4,3,1,0,2:T(8,128)(2,1)S(1)}, bf16[2,4,1,16,768]{4,3,1,0,2:T(8,128)(2,1)S(1)}, u32[]{:S(2)}, u32[]{:S(2)}) collective-permute-start(bf16[2,4,1,16,768]{4,3,1,0,2:T(8,128)(2,1)S(1)} %fusion.53), channel_id=1, source_target_pairs={{0,7},{1,0},{2,1},{3,2},{4,3},{5,4},{6,5},{7,6},{8,15},{9,8},{10,9... | collective-permute-start | bytes 589832 | tf_op jit(solution)/shard_map/ppermute | solution.py:61
  172.3 2.7 %collective-permute-start.18 = (bf16[4,4,1,16,768]{4,3,0,1,2:T(8,128)(2,1)S(1)}, bf16[4,4,1,16,768]{4,3,0,1,2:T(8,128)(2,1)S(1)}, u32[]{:S(2)}, u32[]{:S(2)}) collective-permute-start(bf16[4,4,1,16,768]{4,3,0,1,2:T(8,128)(2,1)S(1)} %fusion.35), channel_id=1, source_target_pairs={{0,192},{64,0},{128,64},{192,128},{1,193},{65,1},{129,65},{193,129... | collective-permute-start | bytes 1179656 | tf_op jit(solution)/shard_map/ppermute | solution.py:61
  175.2 2.7 %collective-permute-start.10 = (bf16[2,4,1,16,768]{4,3,1,0,2:T(8,128)(2,1)S(1)}, bf16[2,4,1,16,768]{4,3,1,0,2:T(8,128)(2,1)S(1)}, u32[]{:S(2)}, u32[]{:S(2)}) collective-permute-start(bf16[2,4,1,16,768]{4,3,1,0,2:T(8,128)(2,1)S(1)} %fusion.52), channel_id=1, source_target_pairs={{0,7},{1,0},{2,1},{3,2},{4,3},{5,4},{6,5},{7,6},{8,15},{9,8},{10,9... | collective-permute-start | bytes 589832 | tf_op jit(solution)/shard_map/ppermute | solution.py:61
  177.9 3.2 %collective-permute-done.3 = bf16[2,4,1,16,768]{4,3,1,0,2:T(8,128)(2,1)S(1)} collective-permute-done((bf16[2,4,1,16,768]{4,3,1,0,2:T(8,128)(2,1)S(1)}, bf16[2,4,1,16,768]{4,3,1,0,2:T(8,128)(2,1)S(1)}, u32[]{:S(2)}, u32[]{:S(2)}) %collective-permute-start.3) | collective-permute-done | bytes 196640 | tf_op jit(solution)/shard_map/ppermute | solution.py:61
  181.4 2.7 %collective-permute-start.11 = (bf16[2,4,1,16,768]{4,3,1,0,2:T(8,128)(2,1)S(1)}, bf16[2,4,1,16,768]{4,3,1,0,2:T(8,128)(2,1)S(1)}, u32[]{:S(2)}, u32[]{:S(2)}) collective-permute-start(bf16[2,4,1,16,768]{4,3,1,0,2:T(8,128)(2,1)S(1)} %fusion.51), channel_id=1, source_target_pairs={{0,7},{1,0},{2,1},{3,2},{4,3},{5,4},{6,5},{7,6},{8,15},{9,8},{10,9... | collective-permute-start | bytes 589832 | tf_op jit(solution)/shard_map/ppermute | solution.py:61
  184.3 0.9 fusion.34
  185.1 2.7 collective-permute-start.19
  188.3 2.7 %collective-permute-start.12 = (bf16[2,4,1,16,768]{4,3,1,0,2:T(8,128)(2,1)S(1)}, bf16[2,4,1,16,768]{4,3,1,0,2:T(8,128)(2,1)S(1)}, u32[]{:S(2)}, u32[]{:S(2)}) collective-permute-start(bf16[2,4,1,16,768]{4,3,1,0,2:T(8,128)(2,1)S(1)} %fusion.50), channel_id=1, source_target_pairs={{0,7},{1,0},{2,1},{3,2},{4,3},{5,4},{6,5},{7,6},{8,15},{9,8},{10,9... | collective-permute-start | bytes 589832 | tf_op jit(solution)/shard_map/ppermute | solution.py:61
  191.0 4.0 %collective-permute-done.5 = bf16[2,4,1,16,768]{4,3,1,0,2:T(8,128)(2,1)S(1)} collective-permute-done((bf16[2,4,1,16,768]{4,3,1,0,2:T(8,128)(2,1)S(1)}, bf16[2,4,1,16,768]{4,3,1,0,2:T(8,128)(2,1)S(1)}, u32[]{:S(2)}, u32[]{:S(2)}) %collective-permute-start.5) | collective-permute-done | bytes 196640 | tf_op jit(solution)/shard_map/ppermute | solution.py:61
  195.2 3.3 %collective-permute-start.13 = (bf16[2,4,1,16,768]{4,3,1,0,2:T(8,128)(2,1)S(1)}, bf16[2,4,1,16,768]{4,3,1,0,2:T(8,128)(2,1)S(1)}, u32[]{:S(2)}, u32[]{:S(2)}) collective-permute-start(bf16[2,4,1,16,768]{4,3,1,0,2:T(8,128)(2,1)S(1)} %fusion.49), channel_id=1, source_target_pairs={{0,7},{1,0},{2,1},{3,2},{4,3},{5,4},{6,5},{7,6},{8,15},{9,8},{10,9... | collective-permute-start | bytes 589832 | tf_op jit(solution)/shard_map/ppermute | solution.py:61
  199.3 3.9 %collective-permute-done.6 = bf16[2,4,1,16,768]{4,3,1,0,2:T(8,128)(2,1)S(1)} collective-permute-done((bf16[2,4,1,16,768]{4,3,1,0,2:T(8,128)(2,1)S(1)}, bf16[2,4,1,16,768]{4,3,1,0,2:T(8,128)(2,1)S(1)}, u32[]{:S(2)}, u32[]{:S(2)}) %collective-permute-start.6) | collective-permute-done | bytes 196640 | tf_op jit(solution)/shard_map/ppermute | solution.py:61
  204.1 3.5 %all-to-all-start.1 = ((bf16[4,4,1,16,768]{4,3,1,2,0:T(8,128)(2,1)}), bf16[4,4,1,16,768]{4,3,1,2,0:T(8,128)(2,1)S(1)}, u32[]{:S(2)}, u32[]{:S(2)}) async-start(bf16[4,4,1,16,768]{4,3,1,2,0:T(8,128)(2,1)} %maximum_bitcast_fusion), calls=%async_computation.1 | async-start | bytes 786432 | tf_op jit(solution)/shard_map/all_to_all | solution.py:78
  207.6 1.1 fusion.33
  208.7 1.2 pad_maximum_fusion
  209.9 1.0 copy.249
  210.9 2.9 %all-to-all-done.1 = bf16[4,4,1,16,768]{4,3,1,2,0:T(8,128)(2,1)S(1)} async-done(((bf16[4,4,1,16,768]{4,3,1,2,0:T(8,128)(2,1)}), bf16[4,4,1,16,768]{4,3,1,2,0:T(8,128)(2,1)S(1)}, u32[]{:S(2)}, u32[]{:S(2)}) %all-to-all-start.1) | async-done | bytes 393248 | tf_op jit(solution)/shard_map/all_to_all | solution.py:78
  213.8 5.0 %all-to-all-start.2 = ((bf16[8,4,1,16,768]{4,3,1,2,0:T(8,128)(2,1)}), bf16[8,4,1,16,768]{4,3,1,2,0:T(8,128)(2,1)}, u32[]{:S(2)}, u32[]{:S(2)}) async-start(bf16[8,4,1,16,768]{4,3,1,2,0:T(8,128)(2,1)} %copy.249), calls=%async_computation.2 | async-start | bytes 1572864 | tf_op jit(solution)/shard_map/all_to_all | solution.py:78
  219.5 1.1 slice.122
  222.8 1.2 sqrt_bitcast_fusion
  224.0 1.3 copy.224
  225.4 1.4 slice_divide_fusion
  229.0 5.1 %all-to-all-done.2 = bf16[8,4,1,16,768]{4,3,1,2,0:T(8,128)(2,1)} async-done(((bf16[8,4,1,16,768]{4,3,1,2,0:T(8,128)(2,1)}), bf16[8,4,1,16,768]{4,3,1,2,0:T(8,128)(2,1)}, u32[]{:S(2)}, u32[]{:S(2)}) %all-to-all-start.2) | async-done | bytes 786464 | tf_op jit(solution)/shard_map/all_to_all | solution.py:78
  234.0 1.2 reduce.17
  235.3 1.6 pad_maximum_fusion.1
  236.8 14.1 %all-to-all-start.3 = ((bf16[8,1,16,768]{3,2,1,0:T(8,128)(2,1)}), bf16[8,1,16,768]{3,2,1,0:T(8,128)(2,1)S(1)}, u32[]{:S(2)}, u32[]{:S(2)}) async-start(bf16[8,1,16,768]{3,2,1,0:T(8,128)(2,1)} %pad_maximum_fusion.1), calls=%async_computation.3 | async-start | bytes 393216 | tf_op jit(solution)/shard_map/all_to_all | solution.py:203
  250.9 5.8 %all-to-all-done.3 = bf16[8,1,16,768]{3,2,1,0:T(8,128)(2,1)S(1)} async-done(((bf16[8,1,16,768]{3,2,1,0:T(8,128)(2,1)}), bf16[8,1,16,768]{3,2,1,0:T(8,128)(2,1)S(1)}, u32[]{:S(2)}, u32[]{:S(2)}) %all-to-all-start.3) | async-done | bytes 196640 | tf_op jit(solution)/shard_map/all_to_all | solution.py:203
  256.8 0.9 fusion.71
  (129 shorter events, 19.7 us)
Async XLA Ops:
  7.2 137.3 %copy-start = (bf16[1,6144,256]{2,1,0:T(8,128)(2,1)S(1)}, bf16[1,6144,256]{2,1,0:T(8,128)(2,1)}, u32[]{:S(2)}) copy-start(bf16[1,6144,256]{2,1,0:T(8,128)(2,1)} %param.29) | copy-start | bytes 9437188
  7.2 7.4 %copy-start.11 = (bf16[16,2,128]{2,1,0:T(2,128)(2,1)S(1)}, bf16[16,2,128]{2,1,0:T(2,128)(2,1)}, u32[]{:S(2)}) copy-start(bf16[16,2,128]{2,1,0:T(2,128)(2,1)} %param.22) | copy-start | bytes 24580
  10.4 4.4 %copy-start.10 = (bf16[16,1,512,128]{3,2,1,0:T(8,128)(2,1)S(1)}, bf16[16,1,512,128]{3,2,1,0:T(8,128)(2,1)}, u32[]{:S(2)}) copy-start(bf16[16,1,512,128]{3,2,1,0:T(8,128)(2,1)} %param.24) | copy-start | bytes 6291460
  12.9 2.5 copy-start.6
  14.5 9.5 %copy-start.8 = (bf16[768]{0:T(1024)(128)(2,1)S(1)}, bf16[768]{0:T(1024)(128)(2,1)}, u32[]{:S(2)}) copy-start(bf16[768]{0:T(1024)(128)(2,1)} %param.26) | copy-start | bytes 4612
  14.5 9.5 %copy-start.7 = (f32[768,8]{0,1:T(8,128)S(1)}, f32[768,8]{0,1:T(8,128)}, u32[]{:S(2)}) copy-start(f32[768,8]{0,1:T(8,128)} %param.27) | copy-start | bytes 73732
  15.6 1.9 copy-start.5
  17.5 12.4 %all-to-all-start = ((bf16[8,16,768]{2,1,0:T(8,128)(2,1)}), bf16[8,16,768]{2,1,0:T(8,128)(2,1)S(1)}, u32[]{:S(2)}, u32[]{:S(2)}) async-start(bf16[8,16,768]{2,1,0:T(8,128)(2,1)} %bitcast.460), calls=%async_computation | async-start | bytes 393216 | tf_op jit(solution)/shard_map/all_to_all | solution.py:141
  24.0 97.0 %all-gather.4.cloned.1.call-start = ((), (), s32[]{:S(2)}) async-start(), calls=%async_computation.4 | async-start | bytes 6893568 | tf_op jit(solution)/shard_map/all_gather | solution.py:144
  144.4 4.7 %copy-start.4 = (bf16[4,8,8,16,768]{4,3,2,1,0:T(8,128)(2,1)S(1)}, bf16[4,8,8,16,768]{4,3,2,1,0:T(8,128)(2,1)}, u32[]{:S(2)}) copy-start(bf16[4,8,8,16,768]{4,3,2,1,0:T(8,128)(2,1)} %divide_convert_fusion) | copy-start | bytes 18874372
  144.4 5.5 %copy-start.9 = (bf16[1,6144,256]{2,1,0:T(8,128)(2,1)S(1)}, bf16[1,6144,256]{2,1,0:T(8,128)(2,1)}, u32[]{:S(2)}) copy-start(bf16[1,6144,256]{2,1,0:T(8,128)(2,1)} %param.30) | copy-start | bytes 9437188
  150.0 1.9 copy-start.2
  153.1 1.9 copy-start.3
  156.3 6.6 %collective-permute-start = (bf16[2,4,1,16,768]{4,3,1,0,2:T(8,128)(2,1)S(1)}, bf16[2,4,1,16,768]{4,3,1,0,2:T(8,128)(2,1)S(1)}, u32[]{:S(2)}, u32[]{:S(2)}) collective-permute-start(bf16[2,4,1,16,768]{4,3,1,0,2:T(8,128)(2,1)S(1)} %fusion.61), channel_id=1, source_target_pairs={{0,1},{1,2},{2,3},{3,4},{4,5},{5,6},{6,7},{7,0},{8,9},{9,10},{10,1... | collective-permute-start | bytes 589832 | tf_op jit(solution)/shard_map/ppermute | solution.py:61
  156.4 6.7 %collective-permute-start.7 = (bf16[2,4,1,16,768]{4,3,1,0,2:T(8,128)(2,1)S(1)}, bf16[2,4,1,16,768]{4,3,1,0,2:T(8,128)(2,1)S(1)}, u32[]{:S(2)}, u32[]{:S(2)}) collective-permute-start(bf16[2,4,1,16,768]{4,3,1,0,2:T(8,128)(2,1)S(1)} %fusion.60), channel_id=1, source_target_pairs={{0,7},{1,0},{2,1},{3,2},{4,3},{5,4},{6,5},{7,6},{8,15},{9,8},{10,9... | collective-permute-start | bytes 589832 | tf_op jit(solution)/shard_map/ppermute | solution.py:61
  159.4 12.6 %collective-permute-start.14 = (bf16[4,4,1,16,768]{4,3,0,1,2:T(8,128)(2,1)S(1)}, bf16[4,4,1,16,768]{4,3,0,1,2:T(8,128)(2,1)S(1)}, u32[]{:S(2)}, u32[]{:S(2)}) collective-permute-start(bf16[4,4,1,16,768]{4,3,0,1,2:T(8,128)(2,1)S(1)} %fusion.40), channel_id=1, source_target_pairs={{0,64},{64,128},{128,192},{192,0},{1,65},{65,129},{129,193},{193,1... | collective-permute-start | bytes 1179656 | tf_op jit(solution)/shard_map/ppermute | solution.py:61
  159.5 12.6 %collective-permute-start.17 = (bf16[4,4,1,16,768]{4,3,0,1,2:T(8,128)(2,1)S(1)}, bf16[4,4,1,16,768]{4,3,0,1,2:T(8,128)(2,1)S(1)}, u32[]{:S(2)}, u32[]{:S(2)}) collective-permute-start(bf16[4,4,1,16,768]{4,3,0,1,2:T(8,128)(2,1)S(1)} %fusion.41), channel_id=1, source_target_pairs={{0,192},{64,0},{128,64},{192,128},{1,193},{65,1},{129,65},{193,129... | collective-permute-start | bytes 1179656 | tf_op jit(solution)/shard_map/ppermute | solution.py:61
  162.9 6.1 %collective-permute-start.1 = (bf16[2,4,1,16,768]{4,3,1,0,2:T(8,128)(2,1)S(1)}, bf16[2,4,1,16,768]{4,3,1,0,2:T(8,128)(2,1)S(1)}, u32[]{:S(2)}, u32[]{:S(2)}) collective-permute-start(bf16[2,4,1,16,768]{4,3,1,0,2:T(8,128)(2,1)S(1)} %fusion.47), channel_id=1, source_target_pairs={{0,1},{1,2},{2,3},{3,4},{4,5},{5,6},{6,7},{7,0},{8,9},{9,10},{10,1... | collective-permute-start | bytes 589832 | tf_op jit(solution)/shard_map/ppermute | solution.py:61
  163.1 6.1 %collective-permute-start.8 = (bf16[2,4,1,16,768]{4,3,1,0,2:T(8,128)(2,1)S(1)}, bf16[2,4,1,16,768]{4,3,1,0,2:T(8,128)(2,1)S(1)}, u32[]{:S(2)}, u32[]{:S(2)}) collective-permute-start(bf16[2,4,1,16,768]{4,3,1,0,2:T(8,128)(2,1)S(1)} %fusion.54), channel_id=1, source_target_pairs={{0,7},{1,0},{2,1},{3,2},{4,3},{5,4},{6,5},{7,6},{8,15},{9,8},{10,9... | collective-permute-start | bytes 589832 | tf_op jit(solution)/shard_map/ppermute | solution.py:61
  169.1 5.9 %collective-permute-start.2 = (bf16[2,4,1,16,768]{4,3,1,0,2:T(8,128)(2,1)S(1)}, bf16[2,4,1,16,768]{4,3,1,0,2:T(8,128)(2,1)S(1)}, u32[]{:S(2)}, u32[]{:S(2)}) collective-permute-start(bf16[2,4,1,16,768]{4,3,1,0,2:T(8,128)(2,1)S(1)} %fusion.46), channel_id=1, source_target_pairs={{0,1},{1,2},{2,3},{3,4},{4,5},{5,6},{6,7},{7,0},{8,9},{9,10},{10,1... | collective-permute-start | bytes 589832 | tf_op jit(solution)/shard_map/ppermute | solution.py:61
  169.2 5.9 %collective-permute-start.9 = (bf16[2,4,1,16,768]{4,3,1,0,2:T(8,128)(2,1)S(1)}, bf16[2,4,1,16,768]{4,3,1,0,2:T(8,128)(2,1)S(1)}, u32[]{:S(2)}, u32[]{:S(2)}) collective-permute-start(bf16[2,4,1,16,768]{4,3,1,0,2:T(8,128)(2,1)S(1)} %fusion.53), channel_id=1, source_target_pairs={{0,7},{1,0},{2,1},{3,2},{4,3},{5,4},{6,5},{7,6},{8,15},{9,8},{10,9... | collective-permute-start | bytes 589832 | tf_op jit(solution)/shard_map/ppermute | solution.py:61
  172.1 12.0 %collective-permute-start.15 = (bf16[4,4,1,16,768]{4,3,0,1,2:T(8,128)(2,1)S(1)}, bf16[4,4,1,16,768]{4,3,0,1,2:T(8,128)(2,1)S(1)}, u32[]{:S(2)}, u32[]{:S(2)}) collective-permute-start(bf16[4,4,1,16,768]{4,3,0,1,2:T(8,128)(2,1)S(1)} %fusion.38), channel_id=1, source_target_pairs={{0,64},{64,128},{128,192},{192,0},{1,65},{65,129},{129,193},{193,1... | collective-permute-start | bytes 1179656 | tf_op jit(solution)/shard_map/ppermute | solution.py:61
  172.3 12.0 %collective-permute-start.18 = (bf16[4,4,1,16,768]{4,3,0,1,2:T(8,128)(2,1)S(1)}, bf16[4,4,1,16,768]{4,3,0,1,2:T(8,128)(2,1)S(1)}, u32[]{:S(2)}, u32[]{:S(2)}) collective-permute-start(bf16[4,4,1,16,768]{4,3,0,1,2:T(8,128)(2,1)S(1)} %fusion.35), channel_id=1, source_target_pairs={{0,192},{64,0},{128,64},{192,128},{1,193},{65,1},{129,65},{193,129... | collective-permute-start | bytes 1179656 | tf_op jit(solution)/shard_map/ppermute | solution.py:61
  175.1 6.1 %collective-permute-start.3 = (bf16[2,4,1,16,768]{4,3,1,0,2:T(8,128)(2,1)S(1)}, bf16[2,4,1,16,768]{4,3,1,0,2:T(8,128)(2,1)S(1)}, u32[]{:S(2)}, u32[]{:S(2)}) collective-permute-start(bf16[2,4,1,16,768]{4,3,1,0,2:T(8,128)(2,1)S(1)} %fusion.45), channel_id=1, source_target_pairs={{0,1},{1,2},{2,3},{3,4},{4,5},{5,6},{6,7},{7,0},{8,9},{9,10},{10,1... | collective-permute-start | bytes 589832 | tf_op jit(solution)/shard_map/ppermute | solution.py:61
  175.2 6.1 %collective-permute-start.10 = (bf16[2,4,1,16,768]{4,3,1,0,2:T(8,128)(2,1)S(1)}, bf16[2,4,1,16,768]{4,3,1,0,2:T(8,128)(2,1)S(1)}, u32[]{:S(2)}, u32[]{:S(2)}) collective-permute-start(bf16[2,4,1,16,768]{4,3,1,0,2:T(8,128)(2,1)S(1)} %fusion.52), channel_id=1, source_target_pairs={{0,7},{1,0},{2,1},{3,2},{4,3},{5,4},{6,5},{7,6},{8,15},{9,8},{10,9... | collective-permute-start | bytes 589832 | tf_op jit(solution)/shard_map/ppermute | solution.py:61
  181.2 6.6 %collective-permute-start.4 = (bf16[2,4,1,16,768]{4,3,1,0,2:T(8,128)(2,1)S(1)}, bf16[2,4,1,16,768]{4,3,1,0,2:T(8,128)(2,1)S(1)}, u32[]{:S(2)}, u32[]{:S(2)}) collective-permute-start(bf16[2,4,1,16,768]{4,3,1,0,2:T(8,128)(2,1)S(1)} %fusion.44), channel_id=1, source_target_pairs={{0,1},{1,2},{2,3},{3,4},{4,5},{5,6},{6,7},{7,0},{8,9},{9,10},{10,1... | collective-permute-start | bytes 589832 | tf_op jit(solution)/shard_map/ppermute | solution.py:61
  181.4 6.8 %collective-permute-start.11 = (bf16[2,4,1,16,768]{4,3,1,0,2:T(8,128)(2,1)S(1)}, bf16[2,4,1,16,768]{4,3,1,0,2:T(8,128)(2,1)S(1)}, u32[]{:S(2)}, u32[]{:S(2)}) collective-permute-start(bf16[2,4,1,16,768]{4,3,1,0,2:T(8,128)(2,1)S(1)} %fusion.51), channel_id=1, source_target_pairs={{0,7},{1,0},{2,1},{3,2},{4,3},{5,4},{6,5},{7,6},{8,15},{9,8},{10,9... | collective-permute-start | bytes 589832 | tf_op jit(solution)/shard_map/ppermute | solution.py:61
  184.2 14.3 %collective-permute-start.16 = (bf16[4,4,1,16,768]{4,3,0,1,2:T(8,128)(2,1)S(1)}, bf16[4,4,1,16,768]{4,3,0,1,2:T(8,128)(2,1)S(1)}, u32[]{:S(2)}, u32[]{:S(2)}) collective-permute-start(bf16[4,4,1,16,768]{4,3,0,1,2:T(8,128)(2,1)S(1)} %fusion.37), channel_id=1, source_target_pairs={{0,64},{64,128},{128,192},{192,0},{1,65},{65,129},{129,193},{193,1... | collective-permute-start | bytes 1179656 | tf_op jit(solution)/shard_map/ppermute | solution.py:61
  185.1 22.5 %collective-permute-start.19 = (bf16[4,4,1,16,768]{4,3,0,1,2:T(8,128)(2,1)}, bf16[4,4,1,16,768]{4,3,0,1,2:T(8,128)(2,1)}, u32[]{:S(2)}, u32[]{:S(2)}) collective-permute-start(bf16[4,4,1,16,768]{4,3,0,1,2:T(8,128)(2,1)} %fusion.34), channel_id=1, source_target_pairs={{0,192},{64,0},{128,64},{192,128},{1,193},{65,1},{129,65},{193,129... | collective-permute-start | bytes 1179656 | tf_op jit(solution)/shard_map/ppermute | solution.py:61
  187.8 7.2 %collective-permute-start.5 = (bf16[2,4,1,16,768]{4,3,1,0,2:T(8,128)(2,1)S(1)}, bf16[2,4,1,16,768]{4,3,1,0,2:T(8,128)(2,1)S(1)}, u32[]{:S(2)}, u32[]{:S(2)}) collective-permute-start(bf16[2,4,1,16,768]{4,3,1,0,2:T(8,128)(2,1)S(1)} %fusion.43), channel_id=1, source_target_pairs={{0,1},{1,2},{2,3},{3,4},{4,5},{5,6},{6,7},{7,0},{8,9},{9,10},{10,1... | collective-permute-start | bytes 589832 | tf_op jit(solution)/shard_map/ppermute | solution.py:61
  188.3 6.9 %collective-permute-start.12 = (bf16[2,4,1,16,768]{4,3,1,0,2:T(8,128)(2,1)S(1)}, bf16[2,4,1,16,768]{4,3,1,0,2:T(8,128)(2,1)S(1)}, u32[]{:S(2)}, u32[]{:S(2)}) collective-permute-start(bf16[2,4,1,16,768]{4,3,1,0,2:T(8,128)(2,1)S(1)} %fusion.50), channel_id=1, source_target_pairs={{0,7},{1,0},{2,1},{3,2},{4,3},{5,4},{6,5},{7,6},{8,15},{9,8},{10,9... | collective-permute-start | bytes 589832 | tf_op jit(solution)/shard_map/ppermute | solution.py:61
  195.1 8.2 %collective-permute-start.6 = (bf16[2,4,1,16,768]{4,3,1,0,2:T(8,128)(2,1)S(1)}, bf16[2,4,1,16,768]{4,3,1,0,2:T(8,128)(2,1)S(1)}, u32[]{:S(2)}, u32[]{:S(2)}) collective-permute-start(bf16[2,4,1,16,768]{4,3,1,0,2:T(8,128)(2,1)S(1)} %fusion.42), channel_id=1, source_target_pairs={{0,1},{1,2},{2,3},{3,4},{4,5},{5,6},{6,7},{7,0},{8,9},{9,10},{10,1... | collective-permute-start | bytes 589832 | tf_op jit(solution)/shard_map/ppermute | solution.py:61
  195.2 8.1 %collective-permute-start.13 = (bf16[2,4,1,16,768]{4,3,1,0,2:T(8,128)(2,1)S(1)}, bf16[2,4,1,16,768]{4,3,1,0,2:T(8,128)(2,1)S(1)}, u32[]{:S(2)}, u32[]{:S(2)}) collective-permute-start(bf16[2,4,1,16,768]{4,3,1,0,2:T(8,128)(2,1)S(1)} %fusion.49), channel_id=1, source_target_pairs={{0,7},{1,0},{2,1},{3,2},{4,3},{5,4},{6,5},{7,6},{8,15},{9,8},{10,9... | collective-permute-start | bytes 589832 | tf_op jit(solution)/shard_map/ppermute | solution.py:61
  204.1 9.7 %all-to-all-start.1 = ((bf16[4,4,1,16,768]{4,3,1,2,0:T(8,128)(2,1)}), bf16[4,4,1,16,768]{4,3,1,2,0:T(8,128)(2,1)S(1)}, u32[]{:S(2)}, u32[]{:S(2)}) async-start(bf16[4,4,1,16,768]{4,3,1,2,0:T(8,128)(2,1)} %maximum_bitcast_fusion), calls=%async_computation.1 | async-start | bytes 786432 | tf_op jit(solution)/shard_map/all_to_all | solution.py:78
  208.7 49.7 %copy-start.1 = (bf16[1,6144,256]{2,1,0:T(8,128)(2,1)S(1)}, bf16[1,6144,256]{2,1,0:T(8,128)(2,1)}, u32[]{:S(2)}) copy-start(bf16[1,6144,256]{2,1,0:T(8,128)(2,1)} %param.29) | copy-start | bytes 9437188
  213.8 20.2 %all-to-all-start.2 = ((bf16[8,4,1,16,768]{4,3,1,2,0:T(8,128)(2,1)}), bf16[8,4,1,16,768]{4,3,1,2,0:T(8,128)(2,1)}, u32[]{:S(2)}, u32[]{:S(2)}) async-start(bf16[8,4,1,16,768]{4,3,1,2,0:T(8,128)(2,1)} %copy.249), calls=%async_computation.2 | async-start | bytes 1572864 | tf_op jit(solution)/shard_map/all_to_all | solution.py:78
  236.8 19.9 %all-to-all-start.3 = ((bf16[8,1,16,768]{3,2,1,0:T(8,128)(2,1)}), bf16[8,1,16,768]{3,2,1,0:T(8,128)(2,1)S(1)}, u32[]{:S(2)}, u32[]{:S(2)}) async-start(bf16[8,1,16,768]{3,2,1,0:T(8,128)(2,1)} %pad_maximum_fusion.1), calls=%async_computation.3 | async-start | bytes 393216 | tf_op jit(solution)/shard_map/all_to_all | solution.py:203
Sparse Core Ops, SparseCore 0:
  30.7 90.1 all-gather.3

commit v4 on v3

--- a/solution.py
+++ b/solution.py
@@ -142,8 +142,6 @@
     block_rows = owner_count * local_experts * CAP
     payload = jnp.concatenate([received.reshape(block_rows, slice_width), extras], axis=0)
     gathered = lax.all_gather(payload[None], ("grp", "tp"), axis=0, tiled=True)
-    pieces = gathered[:, :block_rows]
-    gain_rows = gathered[:, block_rows]
     stat_rows = gathered[:, block_rows + 1].reshape(group_count, tensor_count, slice_width)
     stat_rows = lax.dynamic_index_in_dim(stat_rows, lax.axis_index("grp"), 0, keepdims=False)
     stat_rows = stat_rows.astype(jnp.float32)
@@ -159,21 +157,20 @@
     first_gate = 1.0 / (1.0 + jnp.exp(picked_logits[..., 1] - picked_logits[..., 0]))
     second_gate = 1.0 - first_gate
 
-    pieces = pieces.reshape(
-        group_count, tensor_count, owner_count, local_experts, CAP, slice_width
-    ).astype(jnp.float32)
-    gains = gain_rows.reshape(group_count, width)[0].astype(jnp.float32)
-    slot_squares = jnp.sum(pieces * pieces, axis=(1, 5), keepdims=True)
-    pieces = (pieces * gains.reshape(1, tensor_count, 1, 1, 1, slice_width)) / jnp.sqrt(
-        slot_squares / width + 1e-05
-    )
-    pieces = pieces.astype(jnp.bfloat16)
-    gate_split = w_gate.reshape(local_experts, tensor_count, slice_width, hidden_local)
-    up_split = w_up.reshape(local_experts, tensor_count, slice_width, hidden_local)
-    gate_sums = jnp.einsum(
-        "gtajcd,jtdf->jgacf", pieces, gate_split, preferred_element_type=jnp.float32
-    )
-    up_sums = jnp.einsum("gtajcd,jtdf->jgacf", pieces, up_split, preferred_element_type=jnp.float32)
+    rows = gathered.reshape(group_count, tensor_count, block_rows + 2, slice_width)
+    gains = rows[0, :, block_rows].astype(jnp.float32)
+    wide = rows.astype(jnp.float32)
+    slot_scale = jnp.sqrt(jnp.sum(wide * wide, axis=(1, 3)) / width + 1e-05)[..., None]
+    scaled_rows = (wide * gains[None, :, None, :]).astype(jnp.bfloat16)
+
+    def expert_in(weights):
+        split = weights.reshape(tensor_count, slice_width, hidden_local)
+        sums = jnp.einsum("gtrd,tdf->grf", scaled_rows, split, preferred_element_type=jnp.float32)
+        sums = (sums / slot_scale)[:, :block_rows]
+        return sums.reshape(local_experts, group_count, owner_count, CAP, hidden_local)
+
+    gate_sums = expert_in(w_gate)
+    up_sums = expert_in(w_up)
     hidden = (jax.nn.silu(gate_sums) * up_sums).astype(jnp.bfloat16)
     down_split = w_down.reshape(local_experts, hidden_local, tensor_count, slice_width)
     owner_half = owner_count // 2

time: 267 us -> 249 us (0.933)
  other arithmetic: 39.9 us -> 22.4 us
  matrix products: 16.9 us -> 14.2 us
    convert_element_type x3 -> x1, other arithmetic: 19.2 us -> 0.15 us  [per_device(): hidden = (jax.nn.silu(gate_sums) * up_sums).astype(jnp.bfloat16)]
    dot_general x2, matrix products: 6.5 us -> 3.77 us  [expert_in(): jnp.einsum('gtrd,tdf->grf', scaled_rows, split, preferred_element_type=jn...]
    unnamed x32 -> x34, local copies, waits for them, and re-layouts: 13.1 us -> 13.8 us
  transfers between devices with their start and end apart: 25 -> 25, of which waited for: 10 -> 13; matrix products, arithmetic and copies ran while one was open for 10% -> 11% of each run, Pallas kernels for 0% -> 0%
where the time goes in v4:
time: 249 us; the launch traced here: 248 us
  waiting for transfers between devices  116 us (47%)
  starting transfers between devices  57.9 us (23%)
  other arithmetic  22.4 us (9%)
  local copies, waits for them, and re-layouts  21.7 us (9%)
  between operations  15.1 us (6%)
  matrix products  14.2 us (6%)
    all_gather x1, waiting for transfers between devices, per_device(): gathered = lax.all_gather(payload[None], ('grp', 'tp'), axis=0, tiled=True)  80.8 us
    ppermute x20, starting transfers between devices, ring_reduce_scatter(): arrived = lax.ppermute(total.astype(jnp.bfloat16), axis, pairs)  28.5 us
    ppermute x20, waiting for transfers between devices, ring_reduce_scatter(): arrived = lax.ppermute(total.astype(jnp.bfloat16), axis, pairs)  17.2 us
    all_to_all x1, starting transfers between devices, per_device(): lax.all_to_all(summed.astype(jnp.bfloat16), 'ex', split_axis=0, concat_ax...  15 us
    unnamed x34, local copies, waits for them, and re-layouts  13.8 us
    all_to_all x2, waiting for transfers between devices, exchange_sum(): moved = lax.all_to_all(parts.astype(jnp.bfloat16), axis, 0, 0, tiled=True)  7.93 us
    all_to_all x2, starting transfers between devices, exchange_sum(): moved = lax.all_to_all(parts.astype(jnp.bfloat16), axis, 0, 0, tiled=True)  7.91 us
    all_to_all x1, starting transfers between devices, per_device(): lax.all_to_all(outgoing, 'ex', split_axis=0, concat_axis=0, tiled=True)  6.49 us
  transfers between devices with their start and end apart: 25, of which 13 were waited for; matrix products, arithmetic and copies ran while one was open for 11% of the time, Pallas kernels for 0%

profile of v4, /device:TPU:1, one launch (start us, length us, event | category | flops | bytes accessed | tf_op | source)
XLA Modules:
  0.0 247.6 jit_solution(3583333379681728132)
XLA Ops:
  8.0 0.9 copy.210
  11.4 1.3 fusion.87
  12.7 2.3 fusion.86
  16.6 0.9 convolution_convert_fusion
  17.6 6.5 %all-to-all-start = ((bf16[8,16,768]{2,1,0:T(8,128)(2,1)}), bf16[8,16,768]{2,1,0:T(8,128)(2,1)S(1)}, u32[]{:S(2)}, u32[]{:S(2)}) async-start(bf16[8,16,768]{2,1,0:T(8,128)(2,1)} %bitcast.446), calls=%async_computation | async-start | bytes 393216 | tf_op jit(solution)/shard_map/all_to_all | solution.py:141
  25.4 4.6 %all-to-all-done = bf16[8,16,768]{2,1,0:T(8,128)(2,1)S(1)} async-done(((bf16[8,16,768]{2,1,0:T(8,128)(2,1)}), bf16[8,16,768]{2,1,0:T(8,128)(2,1)S(1)}, u32[]{:S(2)}, u32[]{:S(2)}) %all-to-all-start) | async-done | bytes 196640 | tf_op jit(solution)/shard_map/all_to_all | solution.py:141
  31.0 4.7 %copy.237 = bf16[1,256,6144]{1,2,0:T(8,128)(2,1)} copy(bf16[1,256,6144]{2,1,0:T(8,128)(2,1)} %param.31) | data formatting | bytes 6291456 | tf_op args[12]
  35.7 4.5 %copy.278 = bf16[32,8,8,768]{3,2,1,0:T(8,128)(2,1)} copy(bf16[32,8,8,768]{3,1,2,0:T(8,128)(2,1)} %bitcast.434) | data formatting | bytes 6291456
  40.2 80.8 %all-gather.4.cloned.1.call-done = bf16[32,130,768]{2,1,0:T(8,128)(2,1)} async-done(((bf16[1,130,768]{2,1,0:T(8,128)(2,1)}), bf16[32,130,768]{2,1,0:T(8,128)(2,1)}) %all-gather.4.cloned.1.call-update) | async-done | bytes 6389776 | tf_op jit(solution)/shard_map/all_gather | solution.py:144
  121.0 0.9 slice_convert_fusion
  122.0 4.5 %multiply_reduce_fusion = f32[32,130]{1,0:T(8,128)S(1)} fusion(bf16[32,130,768]{2,1,0:T(8,128)(2,1)} %all-gather.4.cloned.1.call-done), kind=kLoop, calls=%fused_computation | loop fusion | flops 9580480 | bytes 6406400 | tf_op jit(solution)/shard_map/reduce_sum | solution.py:163
  126.8 1.9 fusion.13
  128.7 1.9 fusion.12
  130.9 1.6 copy-done.1
  132.5 1.3 fusion.2
  133.8 1.3 fusion.4
  136.9 1.4 collective-permute-start.7
  139.0 2.7 %collective-permute-start.17 = (bf16[4,4,1,16,768]{4,3,0,1,2:T(8,128)(2,1)S(1)}, bf16[4,4,1,16,768]{4,3,0,1,2:T(8,128)(2,1)S(1)}, u32[]{:S(2)}, u32[]{:S(2)}) collective-permute-start(bf16[4,4,1,16,768]{4,3,0,1,2:T(8,128)(2,1)S(1)} %fusion.42), channel_id=1, source_target_pairs={{0,192},{64,0},{128,64},{192,128},{1,193},{65,1},{129,65},{193,129... | collective-permute-start | bytes 1179656 | tf_op jit(solution)/shard_map/ppermute | solution.py:61
  141.7 0.9 collective-permute-done.7
  142.6 2.1 collective-permute-start.8
  144.8 2.7 %collective-permute-done.8 = bf16[2,4,1,16,768]{4,3,1,0,2:T(8,128)(2,1)S(1)} collective-permute-done((bf16[2,4,1,16,768]{4,3,1,0,2:T(8,128)(2,1)S(1)}, bf16[2,4,1,16,768]{4,3,1,0,2:T(8,128)(2,1)S(1)}, u32[]{:S(2)}, u32[]{:S(2)}) %collective-permute-start.8) | collective-permute-done | bytes 196640 | tf_op jit(solution)/shard_map/ppermute | solution.py:61
  147.5 3.3 %collective-permute-start.9 = (bf16[2,4,1,16,768]{4,3,1,0,2:T(8,128)(2,1)S(1)}, bf16[2,4,1,16,768]{4,3,1,0,2:T(8,128)(2,1)S(1)}, u32[]{:S(2)}, u32[]{:S(2)}) collective-permute-start(bf16[2,4,1,16,768]{4,3,1,0,2:T(8,128)(2,1)S(1)} %fusion.54), channel_id=1, source_target_pairs={{0,7},{1,0},{2,1},{3,2},{4,3},{5,4},{6,5},{7,6},{8,15},{9,8},{10,9... | collective-permute-start | bytes 589832 | tf_op jit(solution)/shard_map/ppermute | solution.py:61
  151.3 2.7 %collective-permute-start.18 = (bf16[4,4,1,16,768]{4,3,0,1,2:T(8,128)(2,1)S(1)}, bf16[4,4,1,16,768]{4,3,0,1,2:T(8,128)(2,1)S(1)}, u32[]{:S(2)}, u32[]{:S(2)}) collective-permute-start(bf16[4,4,1,16,768]{4,3,0,1,2:T(8,128)(2,1)S(1)} %fusion.36), channel_id=1, source_target_pairs={{0,192},{64,0},{128,64},{192,128},{1,193},{65,1},{129,65},{193,129... | collective-permute-start | bytes 1179656 | tf_op jit(solution)/shard_map/ppermute | solution.py:61
  154.0 2.7 %collective-permute-start.10 = (bf16[2,4,1,16,768]{4,3,1,0,2:T(8,128)(2,1)S(1)}, bf16[2,4,1,16,768]{4,3,1,0,2:T(8,128)(2,1)S(1)}, u32[]{:S(2)}, u32[]{:S(2)}) collective-permute-start(bf16[2,4,1,16,768]{4,3,1,0,2:T(8,128)(2,1)S(1)} %fusion.53), channel_id=1, source_target_pairs={{0,7},{1,0},{2,1},{3,2},{4,3},{5,4},{6,5},{7,6},{8,15},{9,8},{10,9... | collective-permute-start | bytes 589832 | tf_op jit(solution)/shard_map/ppermute | solution.py:61
  156.9 2.5 collective-permute-done.10
  159.4 3.5 %collective-permute-start.11 = (bf16[2,4,1,16,768]{4,3,1,0,2:T(8,128)(2,1)S(1)}, bf16[2,4,1,16,768]{4,3,1,0,2:T(8,128)(2,1)S(1)}, u32[]{:S(2)}, u32[]{:S(2)}) collective-permute-start(bf16[2,4,1,16,768]{4,3,1,0,2:T(8,128)(2,1)S(1)} %fusion.52), channel_id=1, source_target_pairs={{0,7},{1,0},{2,1},{3,2},{4,3},{5,4},{6,5},{7,6},{8,15},{9,8},{10,9... | collective-permute-start | bytes 589832 | tf_op jit(solution)/shard_map/ppermute | solution.py:61
  164.1 2.6 %collective-permute-start.19 = (bf16[4,4,1,16,768]{4,3,0,1,2:T(8,128)(2,1)}, bf16[4,4,1,16,768]{4,3,0,1,2:T(8,128)(2,1)}, u32[]{:S(2)}, u32[]{:S(2)}) collective-permute-start(bf16[4,4,1,16,768]{4,3,0,1,2:T(8,128)(2,1)} %fusion.35), channel_id=1, source_target_pairs={{0,192},{64,0},{128,64},{192,128},{1,193},{65,1},{129,65},{193,129... | collective-permute-start | bytes 1179656 | tf_op jit(solution)/shard_map/ppermute | solution.py:61
  166.8 2.7 %collective-permute-start.12 = (bf16[2,4,1,16,768]{4,3,1,0,2:T(8,128)(2,1)S(1)}, bf16[2,4,1,16,768]{4,3,1,0,2:T(8,128)(2,1)S(1)}, u32[]{:S(2)}, u32[]{:S(2)}) collective-permute-start(bf16[2,4,1,16,768]{4,3,1,0,2:T(8,128)(2,1)S(1)} %fusion.51), channel_id=1, source_target_pairs={{0,7},{1,0},{2,1},{3,2},{4,3},{5,4},{6,5},{7,6},{8,15},{9,8},{10,9... | collective-permute-start | bytes 589832 | tf_op jit(solution)/shard_map/ppermute | solution.py:61
  169.9 4.0 %collective-permute-done.12 = bf16[2,4,1,16,768]{4,3,1,0,2:T(8,128)(2,1)S(1)} collective-permute-done((bf16[2,4,1,16,768]{4,3,1,0,2:T(8,128)(2,1)S(1)}, bf16[2,4,1,16,768]{4,3,1,0,2:T(8,128)(2,1)S(1)}, u32[]{:S(2)}, u32[]{:S(2)}) %collective-permute-start.12) | collective-permute-done | bytes 196640 | tf_op jit(solution)/shard_map/ppermute | solution.py:61
  173.9 3.5 %collective-permute-start.13 = (bf16[2,4,1,16,768]{4,3,1,0,2:T(8,128)(2,1)S(1)}, bf16[2,4,1,16,768]{4,3,1,0,2:T(8,128)(2,1)S(1)}, u32[]{:S(2)}, u32[]{:S(2)}) collective-permute-start(bf16[2,4,1,16,768]{4,3,1,0,2:T(8,128)(2,1)S(1)} %fusion.50), channel_id=1, source_target_pairs={{0,7},{1,0},{2,1},{3,2},{4,3},{5,4},{6,5},{7,6},{8,15},{9,8},{10,9... | collective-permute-start | bytes 589832 | tf_op jit(solution)/shard_map/ppermute | solution.py:61
  178.9 2.8 %collective-permute-done.13 = bf16[2,4,1,16,768]{4,3,1,0,2:T(8,128)(2,1)S(1)} collective-permute-done((bf16[2,4,1,16,768]{4,3,1,0,2:T(8,128)(2,1)S(1)}, bf16[2,4,1,16,768]{4,3,1,0,2:T(8,128)(2,1)S(1)}, u32[]{:S(2)}, u32[]{:S(2)}) %collective-permute-start.13) | collective-permute-done | bytes 196640 | tf_op jit(solution)/shard_map/ppermute | solution.py:61
  181.7 3.6 %collective-permute-done.6 = bf16[2,4,1,16,768]{4,3,1,0,2:T(8,128)(2,1)S(1)} collective-permute-done((bf16[2,4,1,16,768]{4,3,1,0,2:T(8,128)(2,1)S(1)}, bf16[2,4,1,16,768]{4,3,1,0,2:T(8,128)(2,1)S(1)}, u32[]{:S(2)}, u32[]{:S(2)}) %collective-permute-start.6) | collective-permute-done | bytes 196640 | tf_op jit(solution)/shard_map/ppermute | solution.py:61
  186.2 3.5 %all-to-all-start.1 = ((bf16[4,4,1,16,768]{4,3,1,2,0:T(8,128)(2,1)}), bf16[4,4,1,16,768]{4,3,1,2,0:T(8,128)(2,1)S(1)}, u32[]{:S(2)}, u32[]{:S(2)}) async-start(bf16[4,4,1,16,768]{4,3,1,2,0:T(8,128)(2,1)} %maximum_bitcast_fusion), calls=%async_computation.1 | async-start | bytes 786432 | tf_op jit(solution)/shard_map/all_to_all | solution.py:78
  189.7 1.3 fusion.34
  191.0 1.1 pad_maximum_fusion
  192.1 1.0 copy.240
  193.0 2.8 %all-to-all-done.1 = bf16[4,4,1,16,768]{4,3,1,2,0:T(8,128)(2,1)S(1)} async-done(((bf16[4,4,1,16,768]{4,3,1,2,0:T(8,128)(2,1)}), bf16[4,4,1,16,768]{4,3,1,2,0:T(8,128)(2,1)S(1)}, u32[]{:S(2)}, u32[]{:S(2)}) %all-to-all-start.1) | async-done | bytes 393248 | tf_op jit(solution)/shard_map/all_to_all | solution.py:78
  195.9 4.5 %all-to-all-start.2 = ((bf16[8,4,1,16,768]{4,3,1,2,0:T(8,128)(2,1)}), bf16[8,4,1,16,768]{4,3,1,2,0:T(8,128)(2,1)}, u32[]{:S(2)}, u32[]{:S(2)}) async-start(bf16[8,4,1,16,768]{4,3,1,2,0:T(8,128)(2,1)} %copy.240), calls=%async_computation.2 | async-start | bytes 1572864 | tf_op jit(solution)/shard_map/all_to_all | solution.py:78
  201.0 1.1 slice.123
  204.3 1.2 sqrt_bitcast_fusion
  205.4 1.3 copy.217
  206.8 1.4 slice_divide_fusion.2
  210.3 5.1 %all-to-all-done.2 = bf16[8,4,1,16,768]{4,3,1,2,0:T(8,128)(2,1)} async-done(((bf16[8,4,1,16,768]{4,3,1,2,0:T(8,128)(2,1)}), bf16[8,4,1,16,768]{4,3,1,2,0:T(8,128)(2,1)}, u32[]{:S(2)}, u32[]{:S(2)}) %all-to-all-start.2) | async-done | bytes 786464 | tf_op jit(solution)/shard_map/all_to_all | solution.py:78
  215.5 1.2 reduce.16
  216.7 1.6 pad_maximum_fusion.1
  218.3 15.0 %all-to-all-start.3 = ((bf16[8,1,16,768]{3,2,1,0:T(8,128)(2,1)}), bf16[8,1,16,768]{3,2,1,0:T(8,128)(2,1)S(1)}, u32[]{:S(2)}, u32[]{:S(2)}) async-start(bf16[8,1,16,768]{3,2,1,0:T(8,128)(2,1)} %pad_maximum_fusion.1), calls=%async_computation.3 | async-start | bytes 393216 | tf_op jit(solution)/shard_map/all_to_all | solution.py:200
  233.3 5.8 %all-to-all-done.3 = bf16[8,1,16,768]{3,2,1,0:T(8,128)(2,1)S(1)} async-done(((bf16[8,1,16,768]{3,2,1,0:T(8,128)(2,1)}), bf16[8,1,16,768]{3,2,1,0:T(8,128)(2,1)S(1)}, u32[]{:S(2)}, u32[]{:S(2)}) %all-to-all-start.3) | async-done | bytes 196640 | tf_op jit(solution)/shard_map/all_to_all | solution.py:200
  239.2 0.9 fusion.72
  (132 shorter events, 20.3 us)
Async XLA Ops:
  7.2 119.4 %copy-start = (bf16[1,6144,256]{2,1,0:T(8,128)(2,1)S(1)}, bf16[1,6144,256]{2,1,0:T(8,128)(2,1)}, u32[]{:S(2)}) copy-start(bf16[1,6144,256]{2,1,0:T(8,128)(2,1)} %param.30) | copy-start | bytes 9437188
  7.2 8.4 %copy-start.12 = (bf16[16,2,128]{2,1,0:T(2,128)(2,1)S(1)}, bf16[16,2,128]{2,1,0:T(2,128)(2,1)}, u32[]{:S(2)}) copy-start(bf16[16,2,128]{2,1,0:T(2,128)(2,1)} %param.22) | copy-start | bytes 24580
  11.4 4.4 %copy-start.11 = (bf16[16,1,512,128]{3,2,1,0:T(8,128)(2,1)S(1)}, bf16[16,1,512,128]{3,2,1,0:T(8,128)(2,1)}, u32[]{:S(2)}) copy-start(bf16[16,1,512,128]{3,2,1,0:T(8,128)(2,1)} %param.24) | copy-start | bytes 6291460
  15.1 1.4 copy-start.6
  15.2 8.8 %copy-start.9 = (bf16[768]{0:T(1024)(128)(2,1)S(1)}, bf16[768]{0:T(1024)(128)(2,1)}, u32[]{:S(2)}) copy-start(bf16[768]{0:T(1024)(128)(2,1)} %param.26) | copy-start | bytes 4612
  15.2 8.9 %copy-start.7 = (f32[768,8]{0,1:T(8,128)S(1)}, f32[768,8]{0,1:T(8,128)}, u32[]{:S(2)}) copy-start(f32[768,8]{0,1:T(8,128)} %param.27) | copy-start | bytes 73732
  16.6 1.0 copy-start.5
  17.6 12.4 %all-to-all-start = ((bf16[8,16,768]{2,1,0:T(8,128)(2,1)}), bf16[8,16,768]{2,1,0:T(8,128)(2,1)S(1)}, u32[]{:S(2)}, u32[]{:S(2)}) async-start(bf16[8,16,768]{2,1,0:T(8,128)(2,1)} %bitcast.446), calls=%async_computation | async-start | bytes 393216 | tf_op jit(solution)/shard_map/all_to_all | solution.py:141
  24.1 97.0 %all-gather.4.cloned.1.call-start = ((), (), s32[]{:S(2)}) async-start(), calls=%async_computation.4 | async-start | bytes 6893568 | tf_op jit(solution)/shard_map/all_gather | solution.py:144
  122.0 4.8 %copy-start.4 = (bf16[32,130,768]{2,1,0:T(8,128)(2,1)S(1)}, bf16[32,130,768]{2,1,0:T(8,128)(2,1)}, u32[]{:S(2)}) copy-start(bf16[32,130,768]{2,1,0:T(8,128)(2,1)} %all-gather.4.cloned.1.call-done) | copy-start | bytes 19169284
  126.5 2.1 copy-start.8
  126.8 1.9 copy-start.10
  128.7 1.9 slice-start
  130.6 1.9 copy-start.1
  133.7 1.9 copy-start.2
  136.9 26.4 %copy-start.3 = (f32[4,4,16,4,768]{4,2,3,1,0:T(8,128)}, f32[4,4,16,4,768]{4,2,3,1,0:T(8,128)S(1)}, u32[]{:S(2)}) copy-start(f32[4,4,16,4,768]{4,2,3,1,0:T(8,128)S(1)} %fusion.10) | copy-start | bytes 9437188
  136.9 5.7 %collective-permute-start.7 = (bf16[2,4,1,16,768]{4,3,1,0,2:T(8,128)(2,1)S(1)}, bf16[2,4,1,16,768]{4,3,1,0,2:T(8,128)(2,1)S(1)}, u32[]{:S(2)}, u32[]{:S(2)}) collective-permute-start(bf16[2,4,1,16,768]{4,3,1,0,2:T(8,128)(2,1)S(1)} %fusion.61), channel_id=1, source_target_pairs={{0,7},{1,0},{2,1},{3,2},{4,3},{5,4},{6,5},{7,6},{8,15},{9,8},{10,9... | collective-permute-start | bytes 589832 | tf_op jit(solution)/shard_map/ppermute | solution.py:61
  138.3 6.4 %collective-permute-start = (bf16[2,4,1,16,768]{4,3,1,0,2:T(8,128)(2,1)S(1)}, bf16[2,4,1,16,768]{4,3,1,0,2:T(8,128)(2,1)S(1)}, u32[]{:S(2)}, u32[]{:S(2)}) collective-permute-start(bf16[2,4,1,16,768]{4,3,1,0,2:T(8,128)(2,1)S(1)} %fusion.62), channel_id=1, source_target_pairs={{0,1},{1,2},{2,3},{3,4},{4,5},{5,6},{6,7},{7,0},{8,9},{9,10},{10,1... | collective-permute-start | bytes 589832 | tf_op jit(solution)/shard_map/ppermute | solution.py:61
  138.8 12.2 %collective-permute-start.14 = (bf16[4,4,1,16,768]{4,3,0,1,2:T(8,128)(2,1)S(1)}, bf16[4,4,1,16,768]{4,3,0,1,2:T(8,128)(2,1)S(1)}, u32[]{:S(2)}, u32[]{:S(2)}) collective-permute-start(bf16[4,4,1,16,768]{4,3,0,1,2:T(8,128)(2,1)S(1)} %fusion.41), channel_id=1, source_target_pairs={{0,64},{64,128},{128,192},{192,0},{1,65},{65,129},{129,193},{193,1... | collective-permute-start | bytes 1179656 | tf_op jit(solution)/shard_map/ppermute | solution.py:61
  139.0 12.2 %collective-permute-start.17 = (bf16[4,4,1,16,768]{4,3,0,1,2:T(8,128)(2,1)S(1)}, bf16[4,4,1,16,768]{4,3,0,1,2:T(8,128)(2,1)S(1)}, u32[]{:S(2)}, u32[]{:S(2)}) collective-permute-start(bf16[4,4,1,16,768]{4,3,0,1,2:T(8,128)(2,1)S(1)} %fusion.42), channel_id=1, source_target_pairs={{0,192},{64,0},{128,64},{192,128},{1,193},{65,1},{129,65},{193,129... | collective-permute-start | bytes 1179656 | tf_op jit(solution)/shard_map/ppermute | solution.py:61
  142.6 4.9 %collective-permute-start.8 = (bf16[2,4,1,16,768]{4,3,1,0,2:T(8,128)(2,1)S(1)}, bf16[2,4,1,16,768]{4,3,1,0,2:T(8,128)(2,1)S(1)}, u32[]{:S(2)}, u32[]{:S(2)}) collective-permute-start(bf16[2,4,1,16,768]{4,3,1,0,2:T(8,128)(2,1)S(1)} %fusion.55), channel_id=1, source_target_pairs={{0,7},{1,0},{2,1},{3,2},{4,3},{5,4},{6,5},{7,6},{8,15},{9,8},{10,9... | collective-permute-start | bytes 589832 | tf_op jit(solution)/shard_map/ppermute | solution.py:61
  144.7 6.1 %collective-permute-start.1 = (bf16[2,4,1,16,768]{4,3,1,0,2:T(8,128)(2,1)S(1)}, bf16[2,4,1,16,768]{4,3,1,0,2:T(8,128)(2,1)S(1)}, u32[]{:S(2)}, u32[]{:S(2)}) collective-permute-start(bf16[2,4,1,16,768]{4,3,1,0,2:T(8,128)(2,1)S(1)} %fusion.48), channel_id=1, source_target_pairs={{0,1},{1,2},{2,3},{3,4},{4,5},{5,6},{6,7},{7,0},{8,9},{9,10},{10,1... | collective-permute-start | bytes 589832 | tf_op jit(solution)/shard_map/ppermute | solution.py:61
  147.5 6.5 %collective-permute-start.9 = (bf16[2,4,1,16,768]{4,3,1,0,2:T(8,128)(2,1)S(1)}, bf16[2,4,1,16,768]{4,3,1,0,2:T(8,128)(2,1)S(1)}, u32[]{:S(2)}, u32[]{:S(2)}) collective-permute-start(bf16[2,4,1,16,768]{4,3,1,0,2:T(8,128)(2,1)S(1)} %fusion.54), channel_id=1, source_target_pairs={{0,7},{1,0},{2,1},{3,2},{4,3},{5,4},{6,5},{7,6},{8,15},{9,8},{10,9... | collective-permute-start | bytes 589832 | tf_op jit(solution)/shard_map/ppermute | solution.py:61
  150.9 5.9 %collective-permute-start.2 = (bf16[2,4,1,16,768]{4,3,1,0,2:T(8,128)(2,1)S(1)}, bf16[2,4,1,16,768]{4,3,1,0,2:T(8,128)(2,1)S(1)}, u32[]{:S(2)}, u32[]{:S(2)}) collective-permute-start(bf16[2,4,1,16,768]{4,3,1,0,2:T(8,128)(2,1)S(1)} %fusion.47), channel_id=1, source_target_pairs={{0,1},{1,2},{2,3},{3,4},{4,5},{5,6},{6,7},{7,0},{8,9},{9,10},{10,1... | collective-permute-start | bytes 589832 | tf_op jit(solution)/shard_map/ppermute | solution.py:61
  151.1 12.0 %collective-permute-start.15 = (bf16[4,4,1,16,768]{4,3,0,1,2:T(8,128)(2,1)S(1)}, bf16[4,4,1,16,768]{4,3,0,1,2:T(8,128)(2,1)S(1)}, u32[]{:S(2)}, u32[]{:S(2)}) collective-permute-start(bf16[4,4,1,16,768]{4,3,0,1,2:T(8,128)(2,1)S(1)} %fusion.39), channel_id=1, source_target_pairs={{0,64},{64,128},{128,192},{192,0},{1,65},{65,129},{129,193},{193,1... | collective-permute-start | bytes 1179656 | tf_op jit(solution)/shard_map/ppermute | solution.py:61
  151.3 12.0 %collective-permute-start.18 = (bf16[4,4,1,16,768]{4,3,0,1,2:T(8,128)(2,1)S(1)}, bf16[4,4,1,16,768]{4,3,0,1,2:T(8,128)(2,1)S(1)}, u32[]{:S(2)}, u32[]{:S(2)}) collective-permute-start(bf16[4,4,1,16,768]{4,3,0,1,2:T(8,128)(2,1)S(1)} %fusion.36), channel_id=1, source_target_pairs={{0,192},{64,0},{128,64},{192,128},{1,193},{65,1},{129,65},{193,129... | collective-permute-start | bytes 1179656 | tf_op jit(solution)/shard_map/ppermute | solution.py:61
  154.0 5.3 %collective-permute-start.10 = (bf16[2,4,1,16,768]{4,3,1,0,2:T(8,128)(2,1)S(1)}, bf16[2,4,1,16,768]{4,3,1,0,2:T(8,128)(2,1)S(1)}, u32[]{:S(2)}, u32[]{:S(2)}) collective-permute-start(bf16[2,4,1,16,768]{4,3,1,0,2:T(8,128)(2,1)S(1)} %fusion.53), channel_id=1, source_target_pairs={{0,7},{1,0},{2,1},{3,2},{4,3},{5,4},{6,5},{7,6},{8,15},{9,8},{10,9... | collective-permute-start | bytes 589832 | tf_op jit(solution)/shard_map/ppermute | solution.py:61
  156.8 6.1 %collective-permute-start.3 = (bf16[2,4,1,16,768]{4,3,1,0,2:T(8,128)(2,1)S(1)}, bf16[2,4,1,16,768]{4,3,1,0,2:T(8,128)(2,1)S(1)}, u32[]{:S(2)}, u32[]{:S(2)}) collective-permute-start(bf16[2,4,1,16,768]{4,3,1,0,2:T(8,128)(2,1)S(1)} %fusion.46), channel_id=1, source_target_pairs={{0,1},{1,2},{2,3},{3,4},{4,5},{5,6},{6,7},{7,0},{8,9},{9,10},{10,1... | collective-permute-start | bytes 589832 | tf_op jit(solution)/shard_map/ppermute | solution.py:61
  159.4 7.4 %collective-permute-start.11 = (bf16[2,4,1,16,768]{4,3,1,0,2:T(8,128)(2,1)S(1)}, bf16[2,4,1,16,768]{4,3,1,0,2:T(8,128)(2,1)S(1)}, u32[]{:S(2)}, u32[]{:S(2)}) collective-permute-start(bf16[2,4,1,16,768]{4,3,1,0,2:T(8,128)(2,1)S(1)} %fusion.52), channel_id=1, source_target_pairs={{0,7},{1,0},{2,1},{3,2},{4,3},{5,4},{6,5},{7,6},{8,15},{9,8},{10,9... | collective-permute-start | bytes 589832 | tf_op jit(solution)/shard_map/ppermute | solution.py:61
  163.0 6.7 %collective-permute-start.4 = (bf16[2,4,1,16,768]{4,3,1,0,2:T(8,128)(2,1)S(1)}, bf16[2,4,1,16,768]{4,3,1,0,2:T(8,128)(2,1)S(1)}, u32[]{:S(2)}, u32[]{:S(2)}) collective-permute-start(bf16[2,4,1,16,768]{4,3,1,0,2:T(8,128)(2,1)S(1)} %fusion.45), channel_id=1, source_target_pairs={{0,1},{1,2},{2,3},{3,4},{4,5},{5,6},{6,7},{7,0},{8,9},{9,10},{10,1... | collective-permute-start | bytes 589832 | tf_op jit(solution)/shard_map/ppermute | solution.py:61
  163.2 14.9 %collective-permute-start.16 = (bf16[4,4,1,16,768]{4,3,0,1,2:T(8,128)(2,1)S(1)}, bf16[4,4,1,16,768]{4,3,0,1,2:T(8,128)(2,1)S(1)}, u32[]{:S(2)}, u32[]{:S(2)}) collective-permute-start(bf16[4,4,1,16,768]{4,3,0,1,2:T(8,128)(2,1)S(1)} %fusion.38), channel_id=1, source_target_pairs={{0,64},{64,128},{128,192},{192,0},{1,65},{65,129},{129,193},{193,1... | collective-permute-start | bytes 1179656 | tf_op jit(solution)/shard_map/ppermute | solution.py:61
  164.1 25.5 %collective-permute-start.19 = (bf16[4,4,1,16,768]{4,3,0,1,2:T(8,128)(2,1)}, bf16[4,4,1,16,768]{4,3,0,1,2:T(8,128)(2,1)}, u32[]{:S(2)}, u32[]{:S(2)}) collective-permute-start(bf16[4,4,1,16,768]{4,3,0,1,2:T(8,128)(2,1)} %fusion.35), channel_id=1, source_target_pairs={{0,192},{64,0},{128,64},{192,128},{1,193},{65,1},{129,65},{193,129... | collective-permute-start | bytes 1179656 | tf_op jit(solution)/shard_map/ppermute | solution.py:61
  166.8 7.0 %collective-permute-start.12 = (bf16[2,4,1,16,768]{4,3,1,0,2:T(8,128)(2,1)S(1)}, bf16[2,4,1,16,768]{4,3,1,0,2:T(8,128)(2,1)S(1)}, u32[]{:S(2)}, u32[]{:S(2)}) collective-permute-start(bf16[2,4,1,16,768]{4,3,1,0,2:T(8,128)(2,1)S(1)} %fusion.51), channel_id=1, source_target_pairs={{0,7},{1,0},{2,1},{3,2},{4,3},{5,4},{6,5},{7,6},{8,15},{9,8},{10,9... | collective-permute-start | bytes 589832 | tf_op jit(solution)/shard_map/ppermute | solution.py:61
  169.8 8.2 %collective-permute-start.5 = (bf16[2,4,1,16,768]{4,3,1,0,2:T(8,128)(2,1)S(1)}, bf16[2,4,1,16,768]{4,3,1,0,2:T(8,128)(2,1)S(1)}, u32[]{:S(2)}, u32[]{:S(2)}) collective-permute-start(bf16[2,4,1,16,768]{4,3,1,0,2:T(8,128)(2,1)S(1)} %fusion.44), channel_id=1, source_target_pairs={{0,1},{1,2},{2,3},{3,4},{4,5},{5,6},{6,7},{7,0},{8,9},{9,10},{10,1... | collective-permute-start | bytes 589832 | tf_op jit(solution)/shard_map/ppermute | solution.py:61
  173.9 7.8 %collective-permute-start.13 = (bf16[2,4,1,16,768]{4,3,1,0,2:T(8,128)(2,1)S(1)}, bf16[2,4,1,16,768]{4,3,1,0,2:T(8,128)(2,1)S(1)}, u32[]{:S(2)}, u32[]{:S(2)}) collective-permute-start(bf16[2,4,1,16,768]{4,3,1,0,2:T(8,128)(2,1)S(1)} %fusion.50), channel_id=1, source_target_pairs={{0,7},{1,0},{2,1},{3,2},{4,3},{5,4},{6,5},{7,6},{8,15},{9,8},{10,9... | collective-permute-start | bytes 589832 | tf_op jit(solution)/shard_map/ppermute | solution.py:61
  178.0 7.4 %collective-permute-start.6 = (bf16[2,4,1,16,768]{4,3,1,0,2:T(8,128)(2,1)S(1)}, bf16[2,4,1,16,768]{4,3,1,0,2:T(8,128)(2,1)S(1)}, u32[]{:S(2)}, u32[]{:S(2)}) collective-permute-start(bf16[2,4,1,16,768]{4,3,1,0,2:T(8,128)(2,1)S(1)} %fusion.43), channel_id=1, source_target_pairs={{0,1},{1,2},{2,3},{3,4},{4,5},{5,6},{6,7},{7,0},{8,9},{9,10},{10,1... | collective-permute-start | bytes 589832 | tf_op jit(solution)/shard_map/ppermute | solution.py:61
  186.2 9.7 %all-to-all-start.1 = ((bf16[4,4,1,16,768]{4,3,1,2,0:T(8,128)(2,1)}), bf16[4,4,1,16,768]{4,3,1,2,0:T(8,128)(2,1)S(1)}, u32[]{:S(2)}, u32[]{:S(2)}) async-start(bf16[4,4,1,16,768]{4,3,1,2,0:T(8,128)(2,1)} %maximum_bitcast_fusion), calls=%async_computation.1 | async-start | bytes 786432 | tf_op jit(solution)/shard_map/all_to_all | solution.py:78
  195.9 19.6 %all-to-all-start.2 = ((bf16[8,4,1,16,768]{4,3,1,2,0:T(8,128)(2,1)}), bf16[8,4,1,16,768]{4,3,1,2,0:T(8,128)(2,1)}, u32[]{:S(2)}, u32[]{:S(2)}) async-start(bf16[8,4,1,16,768]{4,3,1,2,0:T(8,128)(2,1)} %copy.240), calls=%async_computation.2 | async-start | bytes 1572864 | tf_op jit(solution)/shard_map/all_to_all | solution.py:78
  218.3 20.9 %all-to-all-start.3 = ((bf16[8,1,16,768]{3,2,1,0:T(8,128)(2,1)}), bf16[8,1,16,768]{3,2,1,0:T(8,128)(2,1)S(1)}, u32[]{:S(2)}, u32[]{:S(2)}) async-start(bf16[8,1,16,768]{3,2,1,0:T(8,128)(2,1)} %pad_maximum_fusion.1), calls=%async_computation.3 | async-start | bytes 393216 | tf_op jit(solution)/shard_map/all_to_all | solution.py:200
Sparse Core Ops, SparseCore 0:
  30.8 90.1 all-gather.3

commit v5 on v4

--- a/solution.py
+++ b/solution.py
@@ -141,7 +141,8 @@
     received = lax.all_to_all(outgoing, "ex", split_axis=0, concat_axis=0, tiled=True)
     block_rows = owner_count * local_experts * CAP
     payload = jnp.concatenate([received.reshape(block_rows, slice_width), extras], axis=0)
-    gathered = lax.all_gather(payload[None], ("grp", "tp"), axis=0, tiled=True)
+    gathered = lax.all_gather(payload[None], "tp", axis=0, tiled=True)
+    gathered = lax.all_gather(gathered, "grp", axis=0, tiled=True)
     stat_rows = gathered[:, block_rows + 1].reshape(group_count, tensor_count, slice_width)
     stat_rows = lax.dynamic_index_in_dim(stat_rows, lax.axis_index("grp"), 0, keepdims=False)
     stat_rows = stat_rows.astype(jnp.float32)

time: 249 us -> 288 us (1.16); the launches traced: 248 us -> 283 us
  waiting for transfers between devices: 116 us -> 133 us
  matrix products: 14.2 us -> 28.1 us
  starting transfers between devices: 57.9 us -> 60.8 us
    all_gather x1 -> x2, waiting for transfers between devices: 80.8 us -> 98.5 us  [the longest x1 62.1 us: per_device(): gathered = lax.all_gather(gathered, 'grp', axis=0, tiled=True)]
    dot_general x2, matrix products: 3.77 us -> 17.7 us  [expert_in(): jnp.einsum('gtrd,tdf->grf', scaled_rows, split, preferred_element_type=jn...]
    ppermute x20, starting transfers between devices: 28.5 us -> 31.7 us  [ring_reduce_scatter(): arrived = lax.ppermute(total.astype(jnp.bfloat16), axis, pairs)]
    all_gather x0 -> x1, local copies, waits for them, and re-layouts: none -> 2.93 us  [per_device(): gathered = lax.all_gather(payload[None], 'tp', axis=0, tiled=True)]
    unnamed x34 -> x32, local copies, waits for them, and re-layouts: 13.8 us -> 13.8 us
  transfers between devices with their start and end apart: 25 -> 26, of which waited for: 13 -> 13; matrix products, arithmetic and copies ran while one was open for 11% -> 10% of each run, Pallas kernels for 0% -> 0%
where the time goes in v5:
time: 288 us; the launch traced here: 283 us
  waiting for transfers between devices  133 us (46%)
  starting transfers between devices  60.8 us (21%)
  matrix products  28.1 us (10%)
  local copies, waits for them, and re-layouts  24.4 us (8%)
  other arithmetic  21.8 us (8%)
  between operations  15.2 us (5%)
    all_gather x1, waiting for transfers between devices, per_device(): gathered = lax.all_gather(gathered, 'grp', axis=0, tiled=True)  62.1 us
    all_gather x1, waiting for transfers between devices, per_device(): gathered = lax.all_gather(payload[None], 'tp', axis=0, tiled=True)  36.4 us
    ppermute x20, starting transfers between devices, ring_reduce_scatter(): arrived = lax.ppermute(total.astype(jnp.bfloat16), axis, pairs)  31.7 us
    dot_general x2, matrix products, expert_in(): jnp.einsum('gtrd,tdf->grf', scaled_rows, split, preferred_element_type=jn...  17.7 us
    ppermute x20, waiting for transfers between devices, ring_reduce_scatter(): arrived = lax.ppermute(total.astype(jnp.bfloat16), axis, pairs)  15.9 us
    all_to_all x1, starting transfers between devices, per_device(): lax.all_to_all(summed.astype(jnp.bfloat16), 'ex', split_axis=0, concat_ax...  14.9 us
    unnamed x32, local copies, waits for them, and re-layouts  13.8 us
    all_to_all x2, waiting for transfers between devices, exchange_sum(): moved = lax.all_to_all(parts.astype(jnp.bfloat16), axis, 0, 0, tiled=True)  8.17 us
  transfers between devices with their start and end apart: 26, of which 13 were waited for; matrix products, arithmetic and copies ran while one was open for 10% of the time, Pallas kernels for 0%

profile of v5, /device:TPU:1, one launch (start us, length us, event | category | flops | bytes accessed | tf_op | source)
XLA Modules:
  0.0 283.5 jit_solution(4295222163559957622)
XLA Ops:
  8.0 0.9 copy.300
  11.4 1.3 fusion.88
  12.7 2.3 fusion.87
  16.6 0.9 convolution_convert_fusion
  17.6 6.5 %all-to-all-start = ((bf16[8,16,768]{2,1,0:T(8,128)(2,1)}), bf16[8,16,768]{2,1,0:T(8,128)(2,1)S(1)}, u32[]{:S(2)}, u32[]{:S(2)}) async-start(bf16[8,16,768]{2,1,0:T(8,128)(2,1)} %bitcast.447), calls=%async_computation | async-start | bytes 393216 | tf_op jit(solution)/shard_map/all_to_all | solution.py:141
  25.4 4.6 %all-to-all-done = bf16[8,16,768]{2,1,0:T(8,128)(2,1)S(1)} async-done(((bf16[8,16,768]{2,1,0:T(8,128)(2,1)}), bf16[8,16,768]{2,1,0:T(8,128)(2,1)S(1)}, u32[]{:S(2)}, u32[]{:S(2)}) %all-to-all-start) | async-done | bytes 196640 | tf_op jit(solution)/shard_map/all_to_all | solution.py:141
  30.7 36.4 %all-gather.7.cloned.1.call-done = bf16[8,130,768]{2,1,0:T(8,128)(2,1)} async-done(((bf16[1,130,768]{2,1,0:T(8,128)(2,1)}), bf16[8,130,768]{2,1,0:T(8,128)(2,1)}) %all-gather.7.cloned.1.call-update) | async-done | bytes 1597456 | tf_op jit(solution)/shard_map/all_gather | solution.py:144
  67.2 2.9 %copy.305 = bf16[8,130,768]{2,0,1:T(8,128)(2,1)} copy(bf16[8,130,768]{2,1,0:T(8,128)(2,1)} %all-gather.7.cloned.1.call-done) | data formatting | bytes 3194880 | tf_op jit(solution)/shard_map/all_gather | solution.py:144
  70.5 4.9 %copy.329 = bf16[1,256,6144]{1,2,0:T(8,128)(2,1)} copy(bf16[1,256,6144]{2,1,0:T(8,128)(2,1)} %param.31) | data formatting | bytes 6291456 | tf_op args[12]
  75.4 4.5 %copy.368 = bf16[32,8,8,768]{3,2,1,0:T(8,128)(2,1)} copy(bf16[32,8,8,768]{3,1,2,0:T(8,128)(2,1)} %bitcast.435) | data formatting | bytes 6291456
  79.8 62.1 %all-gather.5.cloned.1.call-done = bf16[32,130,768]{2,0,1:T(8,128)(2,1)} async-done(((bf16[8,130,768]{2,0,1:T(8,128)(2,1)}), bf16[32,130,768]{2,0,1:T(8,128)(2,1)}) %all-gather.5.cloned.1.call-update) | async-done | bytes 6389776 | tf_op jit(solution)/shard_map/all_gather | solution.py:145
  142.7 4.1 %multiply_reduce_fusion = f32[32,130]{0,1:T(8,128)S(1)} fusion(bf16[32,130,768]{2,0,1:T(8,128)(2,1)} %all-gather.5.cloned.1.call-done), kind=kLoop, calls=%fused_computation.1 | loop fusion | flops 9580480 | bytes 6406400 | tf_op jit(solution)/shard_map/reduce_sum | solution.py:164
  147.0 10.1 %fusion.13 = f32[4,130,256]{2,1,0:T(8,128)S(1)} fusion(bf16[8,768,256,1]{2,1,0,3:T(8,128)(2,1)S(1)} %bitcast.434, bf16[4,8,130,768]{3,1,0,2:T(8,128)(2,1)} %bitcast.441, f32[8,768]{1,0:T(8,128)S(1)} %fusion.79), kind=kOutput, calls=%fused_computation.17 | convolution fusion | flops 1645363200 | bytes 10092544 | tf_op jit(solution)/shard_map/gtrd,tdf->grf/dot_general | solution.py:169
  157.2 7.6 %fusion.12 = f32[4,130,256]{2,1,0:T(8,128)S(1)} fusion(bf16[8,768,256,1]{2,1,0,3:T(8,128)(2,1)S(1)} %bitcast.454, bf16[4,8,130,768]{3,1,0,2:T(8,128)(2,1)S(1)} %bitcast.442, f32[8,768]{1,0:T(8,128)S(1)} %fusion.79), kind=kOutput, calls=%fused_computation.16 | convolution fusion | flops 1645363200 | bytes 10092544 | tf_op jit(solution)/shard_map/gtrd,tdf->grf/dot_general | solution.py:169
  165.1 1.6 copy-done.1
  166.6 1.3 fusion.2
  167.9 1.3 fusion.4
  171.1 3.1 %collective-permute-start.7 = (bf16[2,4,1,16,768]{4,3,1,0,2:T(8,128)(2,1)S(1)}, bf16[2,4,1,16,768]{4,3,1,0,2:T(8,128)(2,1)S(1)}, u32[]{:S(2)}, u32[]{:S(2)}) collective-permute-start(bf16[2,4,1,16,768]{4,3,1,0,2:T(8,128)(2,1)S(1)} %fusion.61), channel_id=1, source_target_pairs={{0,7},{1,0},{2,1},{3,2},{4,3},{5,4},{6,5},{7,6},{8,15},{9,8},{10,9... | collective-permute-start | bytes 589832 | tf_op jit(solution)/shard_map/ppermute | solution.py:61
  174.3 1.0 collective-permute-start.14
  175.3 1.9 collective-permute-start.17
  177.6 3.7 %collective-permute-start.8 = (bf16[2,4,1,16,768]{4,3,1,0,2:T(8,128)(2,1)S(1)}, bf16[2,4,1,16,768]{4,3,1,0,2:T(8,128)(2,1)S(1)}, u32[]{:S(2)}, u32[]{:S(2)}) collective-permute-start(bf16[2,4,1,16,768]{4,3,1,0,2:T(8,128)(2,1)S(1)} %fusion.55), channel_id=1, source_target_pairs={{0,7},{1,0},{2,1},{3,2},{4,3},{5,4},{6,5},{7,6},{8,15},{9,8},{10,9... | collective-permute-start | bytes 589832 | tf_op jit(solution)/shard_map/ppermute | solution.py:61
  181.4 2.5 collective-permute-done.8
  184.0 3.5 %collective-permute-start.9 = (bf16[2,4,1,16,768]{4,3,1,0,2:T(8,128)(2,1)S(1)}, bf16[2,4,1,16,768]{4,3,1,0,2:T(8,128)(2,1)S(1)}, u32[]{:S(2)}, u32[]{:S(2)}) collective-permute-start(bf16[2,4,1,16,768]{4,3,1,0,2:T(8,128)(2,1)S(1)} %fusion.54), channel_id=1, source_target_pairs={{0,7},{1,0},{2,1},{3,2},{4,3},{5,4},{6,5},{7,6},{8,15},{9,8},{10,9... | collective-permute-start | bytes 589832 | tf_op jit(solution)/shard_map/ppermute | solution.py:61
  188.4 2.2 collective-permute-start.18
  190.7 2.7 collective-permute-start.10
  193.5 2.5 collective-permute-done.10
  196.1 3.5 %collective-permute-start.11 = (bf16[2,4,1,16,768]{4,3,1,0,2:T(8,128)(2,1)S(1)}, bf16[2,4,1,16,768]{4,3,1,0,2:T(8,128)(2,1)S(1)}, u32[]{:S(2)}, u32[]{:S(2)}) collective-permute-start(bf16[2,4,1,16,768]{4,3,1,0,2:T(8,128)(2,1)S(1)} %fusion.52), channel_id=1, source_target_pairs={{0,7},{1,0},{2,1},{3,2},{4,3},{5,4},{6,5},{7,6},{8,15},{9,8},{10,9... | collective-permute-start | bytes 589832 | tf_op jit(solution)/shard_map/ppermute | solution.py:61
  200.9 2.5 collective-permute-start.19
  203.4 2.7 collective-permute-start.12
  206.3 3.0 %collective-permute-done.12 = bf16[2,4,1,16,768]{4,3,1,0,2:T(8,128)(2,1)S(1)} collective-permute-done((bf16[2,4,1,16,768]{4,3,1,0,2:T(8,128)(2,1)S(1)}, bf16[2,4,1,16,768]{4,3,1,0,2:T(8,128)(2,1)S(1)}, u32[]{:S(2)}, u32[]{:S(2)}) %collective-permute-start.12) | collective-permute-done | bytes 196640 | tf_op jit(solution)/shard_map/ppermute | solution.py:61
  209.4 3.5 %collective-permute-start.13 = (bf16[2,4,1,16,768]{4,3,1,0,2:T(8,128)(2,1)S(1)}, bf16[2,4,1,16,768]{4,3,1,0,2:T(8,128)(2,1)S(1)}, u32[]{:S(2)}, u32[]{:S(2)}) collective-permute-start(bf16[2,4,1,16,768]{4,3,1,0,2:T(8,128)(2,1)S(1)} %fusion.50), channel_id=1, source_target_pairs={{0,7},{1,0},{2,1},{3,2},{4,3},{5,4},{6,5},{7,6},{8,15},{9,8},{10,9... | collective-permute-start | bytes 589832 | tf_op jit(solution)/shard_map/ppermute | solution.py:61
  214.4 2.9 %collective-permute-done.13 = bf16[2,4,1,16,768]{4,3,1,0,2:T(8,128)(2,1)S(1)} collective-permute-done((bf16[2,4,1,16,768]{4,3,1,0,2:T(8,128)(2,1)S(1)}, bf16[2,4,1,16,768]{4,3,1,0,2:T(8,128)(2,1)S(1)}, u32[]{:S(2)}, u32[]{:S(2)}) %collective-permute-start.13) | collective-permute-done | bytes 196640 | tf_op jit(solution)/shard_map/ppermute | solution.py:61
  217.4 4.0 %collective-permute-done.6 = bf16[2,4,1,16,768]{4,3,1,0,2:T(8,128)(2,1)S(1)} collective-permute-done((bf16[2,4,1,16,768]{4,3,1,0,2:T(8,128)(2,1)S(1)}, bf16[2,4,1,16,768]{4,3,1,0,2:T(8,128)(2,1)S(1)}, u32[]{:S(2)}, u32[]{:S(2)}) %collective-permute-start.6) | collective-permute-done | bytes 196640 | tf_op jit(solution)/shard_map/ppermute | solution.py:61
  222.3 3.5 %all-to-all-start.1 = ((bf16[4,4,1,16,768]{4,3,1,2,0:T(8,128)(2,1)}), bf16[4,4,1,16,768]{4,3,1,2,0:T(8,128)(2,1)S(1)}, u32[]{:S(2)}, u32[]{:S(2)}) async-start(bf16[4,4,1,16,768]{4,3,1,2,0:T(8,128)(2,1)} %maximum_bitcast_fusion), calls=%async_computation.1 | async-start | bytes 786432 | tf_op jit(solution)/shard_map/all_to_all | solution.py:78
  225.8 1.3 fusion.34
  227.1 1.1 pad_maximum_fusion
  228.2 1.0 copy.332
  229.2 2.8 all-to-all-done.1
  232.0 4.2 %all-to-all-start.2 = ((bf16[8,4,1,16,768]{4,3,1,2,0:T(8,128)(2,1)}), bf16[8,4,1,16,768]{4,3,1,2,0:T(8,128)(2,1)}, u32[]{:S(2)}, u32[]{:S(2)}) async-start(bf16[8,4,1,16,768]{4,3,1,2,0:T(8,128)(2,1)} %copy.332), calls=%async_computation.2 | async-start | bytes 1572864 | tf_op jit(solution)/shard_map/all_to_all | solution.py:78
  239.7 1.2 sqrt_bitcast_fusion
  240.9 1.3 copy.307
  242.2 1.4 slice_divide_fusion.2
  245.8 5.4 %all-to-all-done.2 = bf16[8,4,1,16,768]{4,3,1,2,0:T(8,128)(2,1)} async-done(((bf16[8,4,1,16,768]{4,3,1,2,0:T(8,128)(2,1)}), bf16[8,4,1,16,768]{4,3,1,2,0:T(8,128)(2,1)}, u32[]{:S(2)}, u32[]{:S(2)}) %all-to-all-start.2) | async-done | bytes 786464 | tf_op jit(solution)/shard_map/all_to_all | solution.py:78
  251.2 1.2 reduce.16
  252.4 1.6 pad_maximum_fusion.1
  254.0 14.9 %all-to-all-start.3 = ((bf16[8,1,16,768]{3,2,1,0:T(8,128)(2,1)}), bf16[8,1,16,768]{3,2,1,0:T(8,128)(2,1)S(1)}, u32[]{:S(2)}, u32[]{:S(2)}) async-start(bf16[8,1,16,768]{3,2,1,0:T(8,128)(2,1)} %pad_maximum_fusion.1), calls=%async_computation.3 | async-start | bytes 393216 | tf_op jit(solution)/shard_map/all_to_all | solution.py:201
  269.0 5.8 %all-to-all-done.3 = bf16[8,1,16,768]{3,2,1,0:T(8,128)(2,1)S(1)} async-done(((bf16[8,1,16,768]{3,2,1,0:T(8,128)(2,1)}), bf16[8,1,16,768]{3,2,1,0:T(8,128)(2,1)S(1)}, u32[]{:S(2)}, u32[]{:S(2)}) %all-to-all-start.3) | async-done | bytes 196640 | tf_op jit(solution)/shard_map/all_to_all | solution.py:201
  274.8 0.9 fusion.72
  (135 shorter events, 22.3 us)
Async XLA Ops:
  7.2 139.8 %copy-start = (bf16[1,6144,256]{2,1,0:T(8,128)(2,1)S(1)}, bf16[1,6144,256]{2,1,0:T(8,128)(2,1)}, u32[]{:S(2)}) copy-start(bf16[1,6144,256]{2,1,0:T(8,128)(2,1)} %param.30) | copy-start | bytes 9437188
  7.2 8.4 %copy-start.12 = (bf16[16,2,128]{2,1,0:T(2,128)(2,1)S(1)}, bf16[16,2,128]{2,1,0:T(2,128)(2,1)}, u32[]{:S(2)}) copy-start(bf16[16,2,128]{2,1,0:T(2,128)(2,1)} %param.22) | copy-start | bytes 24580
  11.4 4.4 %copy-start.11 = (bf16[16,1,512,128]{3,2,1,0:T(8,128)(2,1)S(1)}, bf16[16,1,512,128]{3,2,1,0:T(8,128)(2,1)}, u32[]{:S(2)}) copy-start(bf16[16,1,512,128]{3,2,1,0:T(8,128)(2,1)} %param.24) | copy-start | bytes 6291460
  15.1 1.4 copy-start.6
  15.2 8.8 %copy-start.9 = (bf16[768]{0:T(1024)(128)(2,1)S(1)}, bf16[768]{0:T(1024)(128)(2,1)}, u32[]{:S(2)}) copy-start(bf16[768]{0:T(1024)(128)(2,1)} %param.26) | copy-start | bytes 4612
  15.2 8.9 %copy-start.7 = (f32[768,8]{0,1:T(8,128)S(1)}, f32[768,8]{0,1:T(8,128)}, u32[]{:S(2)}) copy-start(f32[768,8]{0,1:T(8,128)} %param.27) | copy-start | bytes 73732
  16.6 1.0 copy-start.5
  17.6 12.4 %all-to-all-start = ((bf16[8,16,768]{2,1,0:T(8,128)(2,1)}), bf16[8,16,768]{2,1,0:T(8,128)(2,1)S(1)}, u32[]{:S(2)}, u32[]{:S(2)}) async-start(bf16[8,16,768]{2,1,0:T(8,128)(2,1)} %bitcast.447), calls=%async_computation | async-start | bytes 393216 | tf_op jit(solution)/shard_map/all_to_all | solution.py:141
  24.1 43.1 %all-gather.7.cloned.1.call-start = ((), (), s32[]{:S(2)}) async-start(), calls=%async_computation.5 | async-start | bytes 1880064 | tf_op jit(solution)/shard_map/all_gather | solution.py:144
  30.7 111.3 %all-gather.5.cloned.1.call-start = ((), (), s32[]{:S(2)}) async-start(), calls=%async_computation.4 | async-start | bytes 7987200 | tf_op jit(solution)/shard_map/all_gather | solution.py:145
  146.9 10.2 %copy-start.8 = (f32[4,130]{1,0:T(4,128)}, f32[4,130]{1,0:T(4,128)S(1)}, u32[]{:S(2)}) copy-start(f32[4,130]{1,0:T(4,128)S(1)} %add_sqrt_fusion) | copy-start | bytes 6244
  146.9 10.2 %copy-start.4 = (bf16[32,130,768]{2,0,1:T(8,128)(2,1)S(1)}, bf16[32,130,768]{2,0,1:T(8,128)(2,1)}, u32[]{:S(2)}) copy-start(bf16[32,130,768]{2,0,1:T(8,128)(2,1)} %all-gather.5.cloned.1.call-done) | copy-start | bytes 19169284
  147.0 10.2 %copy-start.10 = (bf16[1,6144,256]{2,1,0:T(8,128)(2,1)S(1)}, bf16[1,6144,256]{2,1,0:T(8,128)(2,1)}, u32[]{:S(2)}) copy-start(bf16[1,6144,256]{2,1,0:T(8,128)(2,1)} %param.29) | copy-start | bytes 9437188
  157.1 7.6 %slice-start = ((f32[4,130]{1,0:T(4,128)}), f32[4,128]{1,0:T(4,128)S(1)}, s32[]{:S(2)}) async-start(f32[4,130]{1,0:T(4,128)} %copy-done.8), calls=%async_computation.6 | async-start | bytes 4096 | tf_op jit(solution)/shard_map/slice | solution.py:170
  164.8 1.9 copy-start.1
  167.9 1.9 copy-start.2
  171.0 29.0 %copy-start.3 = (f32[4,4,16,4,768]{4,2,3,1,0:T(8,128)}, f32[4,4,16,4,768]{4,2,3,1,0:T(8,128)S(1)}, u32[]{:S(2)}) copy-start(f32[4,4,16,4,768]{4,2,3,1,0:T(8,128)S(1)} %fusion.10) | copy-start | bytes 9437188
  171.1 6.5 %collective-permute-start.7 = (bf16[2,4,1,16,768]{4,3,1,0,2:T(8,128)(2,1)S(1)}, bf16[2,4,1,16,768]{4,3,1,0,2:T(8,128)(2,1)S(1)}, u32[]{:S(2)}, u32[]{:S(2)}) collective-permute-start(bf16[2,4,1,16,768]{4,3,1,0,2:T(8,128)(2,1)S(1)} %fusion.61), channel_id=1, source_target_pairs={{0,7},{1,0},{2,1},{3,2},{4,3},{5,4},{6,5},{7,6},{8,15},{9,8},{10,9... | collective-permute-start | bytes 589832 | tf_op jit(solution)/shard_map/ppermute | solution.py:61
  174.2 7.1 %collective-permute-start = (bf16[2,4,1,16,768]{4,3,1,0,2:T(8,128)(2,1)S(1)}, bf16[2,4,1,16,768]{4,3,1,0,2:T(8,128)(2,1)S(1)}, u32[]{:S(2)}, u32[]{:S(2)}) collective-permute-start(bf16[2,4,1,16,768]{4,3,1,0,2:T(8,128)(2,1)S(1)} %fusion.62), channel_id=1, source_target_pairs={{0,1},{1,2},{2,3},{3,4},{4,5},{5,6},{6,7},{7,0},{8,9},{9,10},{10,1... | collective-permute-start | bytes 589832 | tf_op jit(solution)/shard_map/ppermute | solution.py:61
  174.3 13.2 %collective-permute-start.14 = (bf16[4,4,1,16,768]{4,3,0,1,2:T(8,128)(2,1)S(1)}, bf16[4,4,1,16,768]{4,3,0,1,2:T(8,128)(2,1)S(1)}, u32[]{:S(2)}, u32[]{:S(2)}) collective-permute-start(bf16[4,4,1,16,768]{4,3,0,1,2:T(8,128)(2,1)S(1)} %fusion.41), channel_id=1, source_target_pairs={{0,64},{64,128},{128,192},{192,0},{1,65},{65,129},{129,193},{193,1... | collective-permute-start | bytes 1179656 | tf_op jit(solution)/shard_map/ppermute | solution.py:61
  175.3 13.0 %collective-permute-start.17 = (bf16[4,4,1,16,768]{4,3,0,1,2:T(8,128)(2,1)S(1)}, bf16[4,4,1,16,768]{4,3,0,1,2:T(8,128)(2,1)S(1)}, u32[]{:S(2)}, u32[]{:S(2)}) collective-permute-start(bf16[4,4,1,16,768]{4,3,0,1,2:T(8,128)(2,1)S(1)} %fusion.42), channel_id=1, source_target_pairs={{0,192},{64,0},{128,64},{192,128},{1,193},{65,1},{129,65},{193,129... | collective-permute-start | bytes 1179656 | tf_op jit(solution)/shard_map/ppermute | solution.py:61
  177.6 6.3 %collective-permute-start.8 = (bf16[2,4,1,16,768]{4,3,1,0,2:T(8,128)(2,1)S(1)}, bf16[2,4,1,16,768]{4,3,1,0,2:T(8,128)(2,1)S(1)}, u32[]{:S(2)}, u32[]{:S(2)}) collective-permute-start(bf16[2,4,1,16,768]{4,3,1,0,2:T(8,128)(2,1)S(1)} %fusion.55), channel_id=1, source_target_pairs={{0,7},{1,0},{2,1},{3,2},{4,3},{5,4},{6,5},{7,6},{8,15},{9,8},{10,9... | collective-permute-start | bytes 589832 | tf_op jit(solution)/shard_map/ppermute | solution.py:61
  181.3 6.1 %collective-permute-start.1 = (bf16[2,4,1,16,768]{4,3,1,0,2:T(8,128)(2,1)S(1)}, bf16[2,4,1,16,768]{4,3,1,0,2:T(8,128)(2,1)S(1)}, u32[]{:S(2)}, u32[]{:S(2)}) collective-permute-start(bf16[2,4,1,16,768]{4,3,1,0,2:T(8,128)(2,1)S(1)} %fusion.48), channel_id=1, source_target_pairs={{0,1},{1,2},{2,3},{3,4},{4,5},{5,6},{6,7},{7,0},{8,9},{9,10},{10,1... | collective-permute-start | bytes 589832 | tf_op jit(solution)/shard_map/ppermute | solution.py:61
  184.0 6.7 %collective-permute-start.9 = (bf16[2,4,1,16,768]{4,3,1,0,2:T(8,128)(2,1)S(1)}, bf16[2,4,1,16,768]{4,3,1,0,2:T(8,128)(2,1)S(1)}, u32[]{:S(2)}, u32[]{:S(2)}) collective-permute-start(bf16[2,4,1,16,768]{4,3,1,0,2:T(8,128)(2,1)S(1)} %fusion.54), channel_id=1, source_target_pairs={{0,7},{1,0},{2,1},{3,2},{4,3},{5,4},{6,5},{7,6},{8,15},{9,8},{10,9... | collective-permute-start | bytes 589832 | tf_op jit(solution)/shard_map/ppermute | solution.py:61
  187.5 5.9 %collective-permute-start.2 = (bf16[2,4,1,16,768]{4,3,1,0,2:T(8,128)(2,1)S(1)}, bf16[2,4,1,16,768]{4,3,1,0,2:T(8,128)(2,1)S(1)}, u32[]{:S(2)}, u32[]{:S(2)}) collective-permute-start(bf16[2,4,1,16,768]{4,3,1,0,2:T(8,128)(2,1)S(1)} %fusion.47), channel_id=1, source_target_pairs={{0,1},{1,2},{2,3},{3,4},{4,5},{5,6},{6,7},{7,0},{8,9},{9,10},{10,1... | collective-permute-start | bytes 589832 | tf_op jit(solution)/shard_map/ppermute | solution.py:61
  187.7 12.0 %collective-permute-start.15 = (bf16[4,4,1,16,768]{4,3,0,1,2:T(8,128)(2,1)S(1)}, bf16[4,4,1,16,768]{4,3,0,1,2:T(8,128)(2,1)S(1)}, u32[]{:S(2)}, u32[]{:S(2)}) collective-permute-start(bf16[4,4,1,16,768]{4,3,0,1,2:T(8,128)(2,1)S(1)} %fusion.39), channel_id=1, source_target_pairs={{0,64},{64,128},{128,192},{192,0},{1,65},{65,129},{129,193},{193,1... | collective-permute-start | bytes 1179656 | tf_op jit(solution)/shard_map/ppermute | solution.py:61
  188.4 11.6 %collective-permute-start.18 = (bf16[4,4,1,16,768]{4,3,0,1,2:T(8,128)(2,1)S(1)}, bf16[4,4,1,16,768]{4,3,0,1,2:T(8,128)(2,1)S(1)}, u32[]{:S(2)}, u32[]{:S(2)}) collective-permute-start(bf16[4,4,1,16,768]{4,3,0,1,2:T(8,128)(2,1)S(1)} %fusion.36), channel_id=1, source_target_pairs={{0,192},{64,0},{128,64},{192,128},{1,193},{65,1},{129,65},{193,129... | collective-permute-start | bytes 1179656 | tf_op jit(solution)/shard_map/ppermute | solution.py:61
  190.7 5.3 %collective-permute-start.10 = (bf16[2,4,1,16,768]{4,3,1,0,2:T(8,128)(2,1)S(1)}, bf16[2,4,1,16,768]{4,3,1,0,2:T(8,128)(2,1)S(1)}, u32[]{:S(2)}, u32[]{:S(2)}) collective-permute-start(bf16[2,4,1,16,768]{4,3,1,0,2:T(8,128)(2,1)S(1)} %fusion.53), channel_id=1, source_target_pairs={{0,7},{1,0},{2,1},{3,2},{4,3},{5,4},{6,5},{7,6},{8,15},{9,8},{10,9... | collective-permute-start | bytes 589832 | tf_op jit(solution)/shard_map/ppermute | solution.py:61
  193.4 6.1 %collective-permute-start.3 = (bf16[2,4,1,16,768]{4,3,1,0,2:T(8,128)(2,1)S(1)}, bf16[2,4,1,16,768]{4,3,1,0,2:T(8,128)(2,1)S(1)}, u32[]{:S(2)}, u32[]{:S(2)}) collective-permute-start(bf16[2,4,1,16,768]{4,3,1,0,2:T(8,128)(2,1)S(1)} %fusion.46), channel_id=1, source_target_pairs={{0,1},{1,2},{2,3},{3,4},{4,5},{5,6},{6,7},{7,0},{8,9},{9,10},{10,1... | collective-permute-start | bytes 589832 | tf_op jit(solution)/shard_map/ppermute | solution.py:61
  196.1 7.3 %collective-permute-start.11 = (bf16[2,4,1,16,768]{4,3,1,0,2:T(8,128)(2,1)S(1)}, bf16[2,4,1,16,768]{4,3,1,0,2:T(8,128)(2,1)S(1)}, u32[]{:S(2)}, u32[]{:S(2)}) collective-permute-start(bf16[2,4,1,16,768]{4,3,1,0,2:T(8,128)(2,1)S(1)} %fusion.52), channel_id=1, source_target_pairs={{0,7},{1,0},{2,1},{3,2},{4,3},{5,4},{6,5},{7,6},{8,15},{9,8},{10,9... | collective-permute-start | bytes 589832 | tf_op jit(solution)/shard_map/ppermute | solution.py:61
  199.6 6.6 %collective-permute-start.4 = (bf16[2,4,1,16,768]{4,3,1,0,2:T(8,128)(2,1)S(1)}, bf16[2,4,1,16,768]{4,3,1,0,2:T(8,128)(2,1)S(1)}, u32[]{:S(2)}, u32[]{:S(2)}) collective-permute-start(bf16[2,4,1,16,768]{4,3,1,0,2:T(8,128)(2,1)S(1)} %fusion.45), channel_id=1, source_target_pairs={{0,1},{1,2},{2,3},{3,4},{4,5},{5,6},{6,7},{7,0},{8,9},{9,10},{10,1... | collective-permute-start | bytes 589832 | tf_op jit(solution)/shard_map/ppermute | solution.py:61
  199.8 13.8 %collective-permute-start.16 = (bf16[4,4,1,16,768]{4,3,0,1,2:T(8,128)(2,1)S(1)}, bf16[4,4,1,16,768]{4,3,0,1,2:T(8,128)(2,1)S(1)}, u32[]{:S(2)}, u32[]{:S(2)}) collective-permute-start(bf16[4,4,1,16,768]{4,3,0,1,2:T(8,128)(2,1)S(1)} %fusion.38), channel_id=1, source_target_pairs={{0,64},{64,128},{128,192},{192,0},{1,65},{65,129},{129,193},{193,1... | collective-permute-start | bytes 1179656 | tf_op jit(solution)/shard_map/ppermute | solution.py:61
  200.9 24.9 %collective-permute-start.19 = (bf16[4,4,1,16,768]{4,3,0,1,2:T(8,128)(2,1)}, bf16[4,4,1,16,768]{4,3,0,1,2:T(8,128)(2,1)}, u32[]{:S(2)}, u32[]{:S(2)}) collective-permute-start(bf16[4,4,1,16,768]{4,3,0,1,2:T(8,128)(2,1)} %fusion.35), channel_id=1, source_target_pairs={{0,192},{64,0},{128,64},{192,128},{1,193},{65,1},{129,65},{193,129... | collective-permute-start | bytes 1179656 | tf_op jit(solution)/shard_map/ppermute | solution.py:61
  203.4 5.9 %collective-permute-start.12 = (bf16[2,4,1,16,768]{4,3,1,0,2:T(8,128)(2,1)S(1)}, bf16[2,4,1,16,768]{4,3,1,0,2:T(8,128)(2,1)S(1)}, u32[]{:S(2)}, u32[]{:S(2)}) collective-permute-start(bf16[2,4,1,16,768]{4,3,1,0,2:T(8,128)(2,1)S(1)} %fusion.51), channel_id=1, source_target_pairs={{0,7},{1,0},{2,1},{3,2},{4,3},{5,4},{6,5},{7,6},{8,15},{9,8},{10,9... | collective-permute-start | bytes 589832 | tf_op jit(solution)/shard_map/ppermute | solution.py:61
  206.2 7.2 %collective-permute-start.5 = (bf16[2,4,1,16,768]{4,3,1,0,2:T(8,128)(2,1)S(1)}, bf16[2,4,1,16,768]{4,3,1,0,2:T(8,128)(2,1)S(1)}, u32[]{:S(2)}, u32[]{:S(2)}) collective-permute-start(bf16[2,4,1,16,768]{4,3,1,0,2:T(8,128)(2,1)S(1)} %fusion.44), channel_id=1, source_target_pairs={{0,1},{1,2},{2,3},{3,4},{4,5},{5,6},{6,7},{7,0},{8,9},{9,10},{10,1... | collective-permute-start | bytes 589832 | tf_op jit(solution)/shard_map/ppermute | solution.py:61
  209.4 8.0 %collective-permute-start.13 = (bf16[2,4,1,16,768]{4,3,1,0,2:T(8,128)(2,1)S(1)}, bf16[2,4,1,16,768]{4,3,1,0,2:T(8,128)(2,1)S(1)}, u32[]{:S(2)}, u32[]{:S(2)}) collective-permute-start(bf16[2,4,1,16,768]{4,3,1,0,2:T(8,128)(2,1)S(1)} %fusion.50), channel_id=1, source_target_pairs={{0,7},{1,0},{2,1},{3,2},{4,3},{5,4},{6,5},{7,6},{8,15},{9,8},{10,9... | collective-permute-start | bytes 589832 | tf_op jit(solution)/shard_map/ppermute | solution.py:61
  213.5 8.0 %collective-permute-start.6 = (bf16[2,4,1,16,768]{4,3,1,0,2:T(8,128)(2,1)S(1)}, bf16[2,4,1,16,768]{4,3,1,0,2:T(8,128)(2,1)S(1)}, u32[]{:S(2)}, u32[]{:S(2)}) collective-permute-start(bf16[2,4,1,16,768]{4,3,1,0,2:T(8,128)(2,1)S(1)} %fusion.43), channel_id=1, source_target_pairs={{0,1},{1,2},{2,3},{3,4},{4,5},{5,6},{6,7},{7,0},{8,9},{9,10},{10,1... | collective-permute-start | bytes 589832 | tf_op jit(solution)/shard_map/ppermute | solution.py:61
  222.3 9.7 %all-to-all-start.1 = ((bf16[4,4,1,16,768]{4,3,1,2,0:T(8,128)(2,1)}), bf16[4,4,1,16,768]{4,3,1,2,0:T(8,128)(2,1)S(1)}, u32[]{:S(2)}, u32[]{:S(2)}) async-start(bf16[4,4,1,16,768]{4,3,1,2,0:T(8,128)(2,1)} %maximum_bitcast_fusion), calls=%async_computation.1 | async-start | bytes 786432 | tf_op jit(solution)/shard_map/all_to_all | solution.py:78
  232.0 19.2 %all-to-all-start.2 = ((bf16[8,4,1,16,768]{4,3,1,2,0:T(8,128)(2,1)}), bf16[8,4,1,16,768]{4,3,1,2,0:T(8,128)(2,1)}, u32[]{:S(2)}, u32[]{:S(2)}) async-start(bf16[8,4,1,16,768]{4,3,1,2,0:T(8,128)(2,1)} %copy.332), calls=%async_computation.2 | async-start | bytes 1572864 | tf_op jit(solution)/shard_map/all_to_all | solution.py:78
  254.0 20.8 %all-to-all-start.3 = ((bf16[8,1,16,768]{3,2,1,0:T(8,128)(2,1)}), bf16[8,1,16,768]{3,2,1,0:T(8,128)(2,1)S(1)}, u32[]{:S(2)}, u32[]{:S(2)}) async-start(bf16[8,1,16,768]{3,2,1,0:T(8,128)(2,1)} %pad_maximum_fusion.1), calls=%async_computation.3 | async-start | bytes 393216 | tf_op jit(solution)/shard_map/all_to_all | solution.py:201
Sparse Core Ops, SparseCore 0:
  30.8 36.3 all-gather.6
  70.2 71.6 all-gather.4

commit v6 on v4

--- a/solution.py
+++ b/solution.py
@@ -194,7 +194,8 @@
         "grp",
         0,
     )
-    z_done = exchange_sum(z_first, "grp")
+    z_done = lax.psum_scatter(z_first.astype(jnp.bfloat16), "grp", scatter_dimension=0, tiled=True)
+    z_done = z_done[0].astype(jnp.float32)
     y_done = exchange_sum(y_first, "tp")
     summed = jnp.concatenate([z_done, y_done], axis=0)
     returned = lax.all_to_all(

time: 249 us -> 246 us (0.988)
  waiting for transfers between devices: 116 us -> 130 us
  starting transfers between devices: 57.9 us -> 47.6 us
  other arithmetic: 22.4 us -> 18.5 us
    reduce_scatter x0 -> x1, waiting for transfers between devices: none -> 16.5 us  [per_device(): lax.psum_scatter(z_first.astype(jnp.bfloat16), 'grp', scatter_dimension=0...]
    all_to_all x1, starting transfers between devices: 15 us -> 7.35 us  [per_device(): lax.all_to_all(summed.astype(jnp.bfloat16), 'ex', split_axis=0, concat_ax...]
    ppermute x20, waiting for transfers between devices: 17.2 us -> 12.1 us  [ring_reduce_scatter(): arrived = lax.ppermute(total.astype(jnp.bfloat16), axis, pairs)]
    all_to_all x2 -> x1, starting transfers between devices: 7.91 us -> 4.74 us  [exchange_sum(): moved = lax.all_to_all(parts.astype(jnp.bfloat16), axis, 0, 0, tiled=True)]
    all_to_all x2 -> x1, waiting for transfers between devices: 7.93 us -> 10.9 us  [exchange_sum(): moved = lax.all_to_all(parts.astype(jnp.bfloat16), axis, 0, 0, tiled=True)]
  transfers between devices with their start and end apart: 25 -> 25, of which waited for: 13 -> 12; matrix products, arithmetic and copies ran while one was open for 11% -> 8% of each run, Pallas kernels for 0% -> 0%
where the time goes in v6:
time: 246 us; the launch traced here: 245 us
  waiting for transfers between devices  130 us (53%)
  starting transfers between devices  47.6 us (19%)
  local copies, waits for them, and re-layouts  19.8 us (8%)
  other arithmetic  18.5 us (8%)
  between operations  15 us (6%)
  matrix products  14.2 us (6%)
    all_gather x1, waiting for transfers between devices, per_device(): gathered = lax.all_gather(payload[None], ('grp', 'tp'), axis=0, tiled=True)  80.8 us
    ppermute x20, starting transfers between devices, ring_reduce_scatter(): arrived = lax.ppermute(total.astype(jnp.bfloat16), axis, pairs)  29 us
    reduce_scatter x1, waiting for transfers between devices, per_device(): lax.psum_scatter(z_first.astype(jnp.bfloat16), 'grp', scatter_dimension=0...  16.5 us
    unnamed x34, local copies, waits for them, and re-layouts  16.1 us
    ppermute x20, waiting for transfers between devices, ring_reduce_scatter(): arrived = lax.ppermute(total.astype(jnp.bfloat16), axis, pairs)  12.1 us
    all_to_all x1, waiting for transfers between devices, exchange_sum(): moved = lax.all_to_all(parts.astype(jnp.bfloat16), axis, 0, 0, tiled=True)  10.9 us
    all_to_all x1, starting transfers between devices, per_device(): lax.all_to_all(summed.astype(jnp.bfloat16), 'ex', split_axis=0, concat_ax...  7.35 us
    all_to_all x1, starting transfers between devices, per_device(): lax.all_to_all(outgoing, 'ex', split_axis=0, concat_axis=0, tiled=True)  6.49 us
  transfers between devices with their start and end apart: 25, of which 12 were waited for; matrix products, arithmetic and copies ran while one was open for 8% of the time, Pallas kernels for 0%

profile of v6, /device:TPU:1, one launch (start us, length us, event | category | flops | bytes accessed | tf_op | source)
XLA Modules:
  0.0 245.0 jit_solution(7587058760096739437)
XLA Ops:
  7.2 0.8 broadcast_multiply_fusion
  8.0 0.9 copy.210
  8.9 0.7 iota_compare_fusion.3
  10.6 0.9 reshape.679
  11.4 1.3 fusion.87
  12.7 2.3 fusion.86
  16.6 0.9 convolution_convert_fusion
  17.5 6.5 %all-to-all-start = ((bf16[8,16,768]{2,1,0:T(8,128)(2,1)}), bf16[8,16,768]{2,1,0:T(8,128)(2,1)S(1)}, u32[]{:S(2)}, u32[]{:S(2)}) async-start(bf16[8,16,768]{2,1,0:T(8,128)(2,1)} %bitcast.446), calls=%async_computation | async-start | bytes 393216 | tf_op jit(solution)/shard_map/all_to_all | solution.py:141
  24.1 1.2 fusion.67
  26.1 3.9 %all-to-all-done = bf16[8,16,768]{2,1,0:T(8,128)(2,1)S(1)} async-done(((bf16[8,16,768]{2,1,0:T(8,128)(2,1)}), bf16[8,16,768]{2,1,0:T(8,128)(2,1)S(1)}, u32[]{:S(2)}, u32[]{:S(2)}) %all-to-all-start) | async-done | bytes 196640 | tf_op jit(solution)/shard_map/all_to_all | solution.py:141
  31.1 4.6 %copy.236 = bf16[1,256,6144]{1,2,0:T(8,128)(2,1)} copy(bf16[1,256,6144]{2,1,0:T(8,128)(2,1)} %param.31) | data formatting | bytes 6291456 | tf_op args[12]
  35.8 4.5 %copy.278 = bf16[32,8,8,768]{3,2,1,0:T(8,128)(2,1)} copy(bf16[32,8,8,768]{3,1,2,0:T(8,128)(2,1)} %bitcast.434) | data formatting | bytes 6291456
  40.3 80.8 %all-gather.4.cloned.1.call-done = bf16[32,130,768]{2,1,0:T(8,128)(2,1)} async-done(((bf16[1,130,768]{2,1,0:T(8,128)(2,1)}), bf16[32,130,768]{2,1,0:T(8,128)(2,1)}) %all-gather.4.cloned.1.call-update) | async-done | bytes 6389776 | tf_op jit(solution)/shard_map/all_gather | solution.py:144
  121.0 0.9 slice_convert_fusion
  122.0 4.5 %multiply_reduce_fusion = f32[32,130]{1,0:T(8,128)S(1)} fusion(bf16[32,130,768]{2,1,0:T(8,128)(2,1)} %all-gather.4.cloned.1.call-done), kind=kLoop, calls=%fused_computation | loop fusion | flops 9580480 | bytes 6406400 | tf_op jit(solution)/shard_map/reduce_sum | solution.py:163
  126.8 1.9 fusion.13
  128.7 1.9 fusion.12
  130.9 1.6 copy-done.1
  132.5 1.3 fusion.2
  133.8 1.3 fusion.4
  135.0 2.9 %copy-done.2 = bf16[1,256,6144]{1,2,0:T(8,128)(2,1)S(1)} copy-done((bf16[1,256,6144]{1,2,0:T(8,128)(2,1)S(1)}, bf16[1,256,6144]{1,2,0:T(8,128)(2,1)}, u32[]{:S(2)}) %copy-start.2) | copy-done | bytes 3145752
  139.9 1.4 collective-permute-start.7
  142.0 2.7 %collective-permute-start.17 = (bf16[4,4,1,16,768]{4,3,0,1,2:T(8,128)(2,1)S(1)}, bf16[4,4,1,16,768]{4,3,0,1,2:T(8,128)(2,1)S(1)}, u32[]{:S(2)}, u32[]{:S(2)}) collective-permute-start(bf16[4,4,1,16,768]{4,3,0,1,2:T(8,128)(2,1)S(1)} %fusion.42), channel_id=1, source_target_pairs={{0,192},{64,0},{128,64},{192,128},{1,193},{65,1},{129,65},{193,129... | collective-permute-start | bytes 1179656 | tf_op jit(solution)/shard_map/ppermute | solution.py:61
  144.7 0.9 collective-permute-done.7
  145.6 2.1 collective-permute-start.8
  147.8 2.7 %collective-permute-done.8 = bf16[2,4,1,16,768]{4,3,1,0,2:T(8,128)(2,1)S(1)} collective-permute-done((bf16[2,4,1,16,768]{4,3,1,0,2:T(8,128)(2,1)S(1)}, bf16[2,4,1,16,768]{4,3,1,0,2:T(8,128)(2,1)S(1)}, u32[]{:S(2)}, u32[]{:S(2)}) %collective-permute-start.8) | collective-permute-done | bytes 196640 | tf_op jit(solution)/shard_map/ppermute | solution.py:61
  150.5 3.3 %collective-permute-start.9 = (bf16[2,4,1,16,768]{4,3,1,0,2:T(8,128)(2,1)S(1)}, bf16[2,4,1,16,768]{4,3,1,0,2:T(8,128)(2,1)S(1)}, u32[]{:S(2)}, u32[]{:S(2)}) collective-permute-start(bf16[2,4,1,16,768]{4,3,1,0,2:T(8,128)(2,1)S(1)} %fusion.54), channel_id=1, source_target_pairs={{0,7},{1,0},{2,1},{3,2},{4,3},{5,4},{6,5},{7,6},{8,15},{9,8},{10,9... | collective-permute-start | bytes 589832 | tf_op jit(solution)/shard_map/ppermute | solution.py:61
  154.3 2.7 %collective-permute-start.18 = (bf16[4,4,1,16,768]{4,3,0,1,2:T(8,128)(2,1)S(1)}, bf16[4,4,1,16,768]{4,3,0,1,2:T(8,128)(2,1)S(1)}, u32[]{:S(2)}, u32[]{:S(2)}) collective-permute-start(bf16[4,4,1,16,768]{4,3,0,1,2:T(8,128)(2,1)S(1)} %fusion.36), channel_id=1, source_target_pairs={{0,192},{64,0},{128,64},{192,128},{1,193},{65,1},{129,65},{193,129... | collective-permute-start | bytes 1179656 | tf_op jit(solution)/shard_map/ppermute | solution.py:61
  157.0 2.7 %collective-permute-start.10 = (bf16[2,4,1,16,768]{4,3,1,0,2:T(8,128)(2,1)S(1)}, bf16[2,4,1,16,768]{4,3,1,0,2:T(8,128)(2,1)S(1)}, u32[]{:S(2)}, u32[]{:S(2)}) collective-permute-start(bf16[2,4,1,16,768]{4,3,1,0,2:T(8,128)(2,1)S(1)} %fusion.53), channel_id=1, source_target_pairs={{0,7},{1,0},{2,1},{3,2},{4,3},{5,4},{6,5},{7,6},{8,15},{9,8},{10,9... | collective-permute-start | bytes 589832 | tf_op jit(solution)/shard_map/ppermute | solution.py:61
  159.9 2.5 %collective-permute-done.10 = bf16[2,4,1,16,768]{4,3,1,0,2:T(8,128)(2,1)S(1)} collective-permute-done((bf16[2,4,1,16,768]{4,3,1,0,2:T(8,128)(2,1)S(1)}, bf16[2,4,1,16,768]{4,3,1,0,2:T(8,128)(2,1)S(1)}, u32[]{:S(2)}, u32[]{:S(2)}) %collective-permute-start.10) | collective-permute-done | bytes 196640 | tf_op jit(solution)/shard_map/ppermute | solution.py:61
  162.4 3.5 %collective-permute-start.11 = (bf16[2,4,1,16,768]{4,3,1,0,2:T(8,128)(2,1)S(1)}, bf16[2,4,1,16,768]{4,3,1,0,2:T(8,128)(2,1)S(1)}, u32[]{:S(2)}, u32[]{:S(2)}) collective-permute-start(bf16[2,4,1,16,768]{4,3,1,0,2:T(8,128)(2,1)S(1)} %fusion.52), channel_id=1, source_target_pairs={{0,7},{1,0},{2,1},{3,2},{4,3},{5,4},{6,5},{7,6},{8,15},{9,8},{10,9... | collective-permute-start | bytes 589832 | tf_op jit(solution)/shard_map/ppermute | solution.py:61
  166.4 3.0 %collective-permute-start.19 = (bf16[4,4,1,16,768]{4,3,0,1,2:T(8,128)(2,1)S(1)}, bf16[4,4,1,16,768]{4,3,0,1,2:T(8,128)(2,1)S(1)}, u32[]{:S(2)}, u32[]{:S(2)}) collective-permute-start(bf16[4,4,1,16,768]{4,3,0,1,2:T(8,128)(2,1)S(1)} %fusion.35), channel_id=1, source_target_pairs={{0,192},{64,0},{128,64},{192,128},{1,193},{65,1},{129,65},{193,129... | collective-permute-start | bytes 1179656 | tf_op jit(solution)/shard_map/ppermute | solution.py:61
  169.4 3.0 %collective-permute-start.12 = (bf16[2,4,1,16,768]{4,3,1,0,2:T(8,128)(2,1)S(1)}, bf16[2,4,1,16,768]{4,3,1,0,2:T(8,128)(2,1)S(1)}, u32[]{:S(2)}, u32[]{:S(2)}) collective-permute-start(bf16[2,4,1,16,768]{4,3,1,0,2:T(8,128)(2,1)S(1)} %fusion.51), channel_id=1, source_target_pairs={{0,7},{1,0},{2,1},{3,2},{4,3},{5,4},{6,5},{7,6},{8,15},{9,8},{10,9... | collective-permute-start | bytes 589832 | tf_op jit(solution)/shard_map/ppermute | solution.py:61
  172.9 4.0 %collective-permute-done.12 = bf16[2,4,1,16,768]{4,3,1,0,2:T(8,128)(2,1)S(1)} collective-permute-done((bf16[2,4,1,16,768]{4,3,1,0,2:T(8,128)(2,1)S(1)}, bf16[2,4,1,16,768]{4,3,1,0,2:T(8,128)(2,1)S(1)}, u32[]{:S(2)}, u32[]{:S(2)}) %collective-permute-start.12) | collective-permute-done | bytes 196640 | tf_op jit(solution)/shard_map/ppermute | solution.py:61
  176.9 3.5 %collective-permute-start.13 = (bf16[2,4,1,16,768]{4,3,1,0,2:T(8,128)(2,1)S(1)}, bf16[2,4,1,16,768]{4,3,1,0,2:T(8,128)(2,1)S(1)}, u32[]{:S(2)}, u32[]{:S(2)}) collective-permute-start(bf16[2,4,1,16,768]{4,3,1,0,2:T(8,128)(2,1)S(1)} %fusion.50), channel_id=1, source_target_pairs={{0,7},{1,0},{2,1},{3,2},{4,3},{5,4},{6,5},{7,6},{8,15},{9,8},{10,9... | collective-permute-start | bytes 589832 | tf_op jit(solution)/shard_map/ppermute | solution.py:61
  181.0 0.8 fusion.43
  182.0 1.0 copy.239
  183.0 4.7 %all-to-all-start.1 = ((bf16[8,4,1,16,768]{4,3,1,2,0:T(8,128)(2,1)}), bf16[8,4,1,16,768]{4,3,1,2,0:T(8,128)(2,1)}, u32[]{:S(2)}, u32[]{:S(2)}) async-start(bf16[8,4,1,16,768]{4,3,1,2,0:T(8,128)(2,1)} %copy.239), calls=%async_computation.2 | async-start | bytes 1572864 | tf_op jit(solution)/shard_map/all_to_all | solution.py:78
  187.8 1.0 fusion.49
  188.8 1.2 collective-permute-done.6
  190.0 1.1 fusion.56
  191.1 0.8 pad_maximum_fusion.1
  193.9 10.9 %all-to-all-done.1 = bf16[8,4,1,16,768]{4,3,1,2,0:T(8,128)(2,1)} async-done(((bf16[8,4,1,16,768]{4,3,1,2,0:T(8,128)(2,1)}), bf16[8,4,1,16,768]{4,3,1,2,0:T(8,128)(2,1)}, u32[]{:S(2)}, u32[]{:S(2)}) %all-to-all-start.1) | async-done | bytes 786464 | tf_op jit(solution)/shard_map/all_to_all | solution.py:78
  204.7 1.2 reduce.14
  206.0 16.5 %reduce-scatter.2.cloned.1.call-done = bf16[1,4,1,16,768]{4,3,1,0,2:T(8,128)(2,1)} async-done(((bf16[4,4,1,16,768]{4,3,1,0,2:T(8,128)(2,1)}), bf16[1,4,1,16,768]{4,3,1,0,2:T(8,128)(2,1)}) %reduce-scatter.2.cloned.1.call-update) | async-done | bytes 98320 | tf_op jit(solution)/shard_map/reduce_scatter | solution.py:197
  222.5 1.6 maximum_bitcast_fusion.1
  224.0 7.4 %all-to-all-start.2 = ((bf16[8,1,16,768]{3,2,1,0:T(8,128)(2,1)}), bf16[8,1,16,768]{3,2,1,0:T(8,128)(2,1)S(1)}, u32[]{:S(2)}, u32[]{:S(2)}) async-start(bf16[8,1,16,768]{3,2,1,0:T(8,128)(2,1)} %maximum_bitcast_fusion.1), calls=%async_computation.3 | async-start | bytes 393216 | tf_op jit(solution)/shard_map/all_to_all | solution.py:201
  231.4 5.8 %all-to-all-done.2 = bf16[8,1,16,768]{3,2,1,0:T(8,128)(2,1)S(1)} async-done(((bf16[8,1,16,768]{3,2,1,0:T(8,128)(2,1)}), bf16[8,1,16,768]{3,2,1,0:T(8,128)(2,1)S(1)}, u32[]{:S(2)}, u32[]{:S(2)}) %all-to-all-start.2) | async-done | bytes 196640 | tf_op jit(solution)/shard_map/all_to_all | solution.py:201
  (132 shorter events, 12.8 us)
Async XLA Ops:
  7.2 119.4 %copy-start = (bf16[1,6144,256]{2,1,0:T(8,128)(2,1)S(1)}, bf16[1,6144,256]{2,1,0:T(8,128)(2,1)}, u32[]{:S(2)}) copy-start(bf16[1,6144,256]{2,1,0:T(8,128)(2,1)} %param.30) | copy-start | bytes 9437188
  7.2 8.4 %copy-start.12 = (bf16[16,2,128]{2,1,0:T(2,128)(2,1)S(1)}, bf16[16,2,128]{2,1,0:T(2,128)(2,1)}, u32[]{:S(2)}) copy-start(bf16[16,2,128]{2,1,0:T(2,128)(2,1)} %param.22) | copy-start | bytes 24580
  11.4 4.4 %copy-start.11 = (bf16[16,1,512,128]{3,2,1,0:T(8,128)(2,1)S(1)}, bf16[16,1,512,128]{3,2,1,0:T(8,128)(2,1)}, u32[]{:S(2)}) copy-start(bf16[16,1,512,128]{3,2,1,0:T(8,128)(2,1)} %param.24) | copy-start | bytes 6291460
  15.1 1.4 copy-start.7
  15.2 8.8 %copy-start.9 = (bf16[768]{0:T(1024)(128)(2,1)S(1)}, bf16[768]{0:T(1024)(128)(2,1)}, u32[]{:S(2)}) copy-start(bf16[768]{0:T(1024)(128)(2,1)} %param.26) | copy-start | bytes 4612
  16.6 19.2 %copy-start.6 = (bf16[16,2,768]{2,1,0:T(2,128)(2,1)}, bf16[16,2,768]{2,1,0:T(2,128)(2,1)S(1)}, u32[]{:S(2)}) copy-start(bf16[16,2,768]{2,1,0:T(2,128)(2,1)S(1)} %copy.243) | copy-start | bytes 147460
  17.5 12.4 %all-to-all-start = ((bf16[8,16,768]{2,1,0:T(8,128)(2,1)}), bf16[8,16,768]{2,1,0:T(8,128)(2,1)S(1)}, u32[]{:S(2)}, u32[]{:S(2)}) async-start(bf16[8,16,768]{2,1,0:T(8,128)(2,1)} %bitcast.446), calls=%async_computation | async-start | bytes 393216 | tf_op jit(solution)/shard_map/all_to_all | solution.py:141
  24.0 97.0 %all-gather.4.cloned.1.call-start = ((), (), s32[]{:S(2)}) async-start(), calls=%async_computation.5 | async-start | bytes 6893568 | tf_op jit(solution)/shard_map/all_gather | solution.py:144
  121.9 4.8 %copy-start.4 = (bf16[32,130,768]{2,1,0:T(8,128)(2,1)S(1)}, bf16[32,130,768]{2,1,0:T(8,128)(2,1)}, u32[]{:S(2)}) copy-start(bf16[32,130,768]{2,1,0:T(8,128)(2,1)} %all-gather.4.cloned.1.call-done) | copy-start | bytes 19169284
  126.5 2.1 copy-start.8
  126.8 1.9 copy-start.10
  128.7 1.9 slice-start
  130.6 1.9 copy-start.1
  133.7 43.1 %copy-start.3 = (f32[2,4,16,8,768]{4,2,1,0,3:T(8,128)}, f32[2,4,16,8,768]{4,2,1,0,3:T(8,128)S(1)}, u32[]{:S(2)}) copy-start(f32[2,4,16,8,768]{4,2,1,0,3:T(8,128)S(1)} %fusion.2) | copy-start | bytes 9437188
  133.8 4.2 %copy-start.2 = (bf16[1,256,6144]{1,2,0:T(8,128)(2,1)S(1)}, bf16[1,256,6144]{1,2,0:T(8,128)(2,1)}, u32[]{:S(2)}) copy-start(bf16[1,256,6144]{1,2,0:T(8,128)(2,1)} %copy.236) | copy-start | bytes 9437188
  135.0 45.9 %copy-start.5 = (f32[2,4,16,8,768]{4,2,3,1,0:T(8,128)}, f32[2,4,16,8,768]{4,2,3,1,0:T(8,128)S(1)}, u32[]{:S(2)}) copy-start(f32[2,4,16,8,768]{4,2,3,1,0:T(8,128)S(1)} %fusion.4) | copy-start | bytes 9437188
  139.9 5.7 %collective-permute-start.7 = (bf16[2,4,1,16,768]{4,3,1,0,2:T(8,128)(2,1)S(1)}, bf16[2,4,1,16,768]{4,3,1,0,2:T(8,128)(2,1)S(1)}, u32[]{:S(2)}, u32[]{:S(2)}) collective-permute-start(bf16[2,4,1,16,768]{4,3,1,0,2:T(8,128)(2,1)S(1)} %fusion.61), channel_id=1, source_target_pairs={{0,7},{1,0},{2,1},{3,2},{4,3},{5,4},{6,5},{7,6},{8,15},{9,8},{10,9... | collective-permute-start | bytes 589832 | tf_op jit(solution)/shard_map/ppermute | solution.py:61
  141.3 6.4 %collective-permute-start = (bf16[2,4,1,16,768]{4,3,1,0,2:T(8,128)(2,1)S(1)}, bf16[2,4,1,16,768]{4,3,1,0,2:T(8,128)(2,1)S(1)}, u32[]{:S(2)}, u32[]{:S(2)}) collective-permute-start(bf16[2,4,1,16,768]{4,3,1,0,2:T(8,128)(2,1)S(1)} %fusion.62), channel_id=1, source_target_pairs={{0,1},{1,2},{2,3},{3,4},{4,5},{5,6},{6,7},{7,0},{8,9},{9,10},{10,1... | collective-permute-start | bytes 589832 | tf_op jit(solution)/shard_map/ppermute | solution.py:61
  141.8 12.1 %collective-permute-start.14 = (bf16[4,4,1,16,768]{4,3,0,1,2:T(8,128)(2,1)S(1)}, bf16[4,4,1,16,768]{4,3,0,1,2:T(8,128)(2,1)S(1)}, u32[]{:S(2)}, u32[]{:S(2)}) collective-permute-start(bf16[4,4,1,16,768]{4,3,0,1,2:T(8,128)(2,1)S(1)} %fusion.41), channel_id=1, source_target_pairs={{0,64},{64,128},{128,192},{192,0},{1,65},{65,129},{129,193},{193,1... | collective-permute-start | bytes 1179656 | tf_op jit(solution)/shard_map/ppermute | solution.py:61
  142.0 12.2 %collective-permute-start.17 = (bf16[4,4,1,16,768]{4,3,0,1,2:T(8,128)(2,1)S(1)}, bf16[4,4,1,16,768]{4,3,0,1,2:T(8,128)(2,1)S(1)}, u32[]{:S(2)}, u32[]{:S(2)}) collective-permute-start(bf16[4,4,1,16,768]{4,3,0,1,2:T(8,128)(2,1)S(1)} %fusion.42), channel_id=1, source_target_pairs={{0,192},{64,0},{128,64},{192,128},{1,193},{65,1},{129,65},{193,129... | collective-permute-start | bytes 1179656 | tf_op jit(solution)/shard_map/ppermute | solution.py:61
  145.6 4.9 %collective-permute-start.8 = (bf16[2,4,1,16,768]{4,3,1,0,2:T(8,128)(2,1)S(1)}, bf16[2,4,1,16,768]{4,3,1,0,2:T(8,128)(2,1)S(1)}, u32[]{:S(2)}, u32[]{:S(2)}) collective-permute-start(bf16[2,4,1,16,768]{4,3,1,0,2:T(8,128)(2,1)S(1)} %fusion.55), channel_id=1, source_target_pairs={{0,7},{1,0},{2,1},{3,2},{4,3},{5,4},{6,5},{7,6},{8,15},{9,8},{10,9... | collective-permute-start | bytes 589832 | tf_op jit(solution)/shard_map/ppermute | solution.py:61
  147.7 6.1 %collective-permute-start.1 = (bf16[2,4,1,16,768]{4,3,1,0,2:T(8,128)(2,1)S(1)}, bf16[2,4,1,16,768]{4,3,1,0,2:T(8,128)(2,1)S(1)}, u32[]{:S(2)}, u32[]{:S(2)}) collective-permute-start(bf16[2,4,1,16,768]{4,3,1,0,2:T(8,128)(2,1)S(1)} %fusion.48), channel_id=1, source_target_pairs={{0,1},{1,2},{2,3},{3,4},{4,5},{5,6},{6,7},{7,0},{8,9},{9,10},{10,1... | collective-permute-start | bytes 589832 | tf_op jit(solution)/shard_map/ppermute | solution.py:61
  150.5 6.5 %collective-permute-start.9 = (bf16[2,4,1,16,768]{4,3,1,0,2:T(8,128)(2,1)S(1)}, bf16[2,4,1,16,768]{4,3,1,0,2:T(8,128)(2,1)S(1)}, u32[]{:S(2)}, u32[]{:S(2)}) collective-permute-start(bf16[2,4,1,16,768]{4,3,1,0,2:T(8,128)(2,1)S(1)} %fusion.54), channel_id=1, source_target_pairs={{0,7},{1,0},{2,1},{3,2},{4,3},{5,4},{6,5},{7,6},{8,15},{9,8},{10,9... | collective-permute-start | bytes 589832 | tf_op jit(solution)/shard_map/ppermute | solution.py:61
  153.9 5.9 %collective-permute-start.2 = (bf16[2,4,1,16,768]{4,3,1,0,2:T(8,128)(2,1)S(1)}, bf16[2,4,1,16,768]{4,3,1,0,2:T(8,128)(2,1)S(1)}, u32[]{:S(2)}, u32[]{:S(2)}) collective-permute-start(bf16[2,4,1,16,768]{4,3,1,0,2:T(8,128)(2,1)S(1)} %fusion.47), channel_id=1, source_target_pairs={{0,1},{1,2},{2,3},{3,4},{4,5},{5,6},{6,7},{7,0},{8,9},{9,10},{10,1... | collective-permute-start | bytes 589832 | tf_op jit(solution)/shard_map/ppermute | solution.py:61
  154.1 12.0 %collective-permute-start.15 = (bf16[4,4,1,16,768]{4,3,0,1,2:T(8,128)(2,1)S(1)}, bf16[4,4,1,16,768]{4,3,0,1,2:T(8,128)(2,1)S(1)}, u32[]{:S(2)}, u32[]{:S(2)}) collective-permute-start(bf16[4,4,1,16,768]{4,3,0,1,2:T(8,128)(2,1)S(1)} %fusion.39), channel_id=1, source_target_pairs={{0,64},{64,128},{128,192},{192,0},{1,65},{65,129},{129,193},{193,1... | collective-permute-start | bytes 1179656 | tf_op jit(solution)/shard_map/ppermute | solution.py:61
  154.3 12.0 %collective-permute-start.18 = (bf16[4,4,1,16,768]{4,3,0,1,2:T(8,128)(2,1)S(1)}, bf16[4,4,1,16,768]{4,3,0,1,2:T(8,128)(2,1)S(1)}, u32[]{:S(2)}, u32[]{:S(2)}) collective-permute-start(bf16[4,4,1,16,768]{4,3,0,1,2:T(8,128)(2,1)S(1)} %fusion.36), channel_id=1, source_target_pairs={{0,192},{64,0},{128,64},{192,128},{1,193},{65,1},{129,65},{193,129... | collective-permute-start | bytes 1179656 | tf_op jit(solution)/shard_map/ppermute | solution.py:61
  157.0 5.3 %collective-permute-start.10 = (bf16[2,4,1,16,768]{4,3,1,0,2:T(8,128)(2,1)S(1)}, bf16[2,4,1,16,768]{4,3,1,0,2:T(8,128)(2,1)S(1)}, u32[]{:S(2)}, u32[]{:S(2)}) collective-permute-start(bf16[2,4,1,16,768]{4,3,1,0,2:T(8,128)(2,1)S(1)} %fusion.53), channel_id=1, source_target_pairs={{0,7},{1,0},{2,1},{3,2},{4,3},{5,4},{6,5},{7,6},{8,15},{9,8},{10,9... | collective-permute-start | bytes 589832 | tf_op jit(solution)/shard_map/ppermute | solution.py:61
  159.8 6.1 %collective-permute-start.3 = (bf16[2,4,1,16,768]{4,3,1,0,2:T(8,128)(2,1)S(1)}, bf16[2,4,1,16,768]{4,3,1,0,2:T(8,128)(2,1)S(1)}, u32[]{:S(2)}, u32[]{:S(2)}) collective-permute-start(bf16[2,4,1,16,768]{4,3,1,0,2:T(8,128)(2,1)S(1)} %fusion.46), channel_id=1, source_target_pairs={{0,1},{1,2},{2,3},{3,4},{4,5},{5,6},{6,7},{7,0},{8,9},{9,10},{10,1... | collective-permute-start | bytes 589832 | tf_op jit(solution)/shard_map/ppermute | solution.py:61
  162.4 6.9 %collective-permute-start.11 = (bf16[2,4,1,16,768]{4,3,1,0,2:T(8,128)(2,1)S(1)}, bf16[2,4,1,16,768]{4,3,1,0,2:T(8,128)(2,1)S(1)}, u32[]{:S(2)}, u32[]{:S(2)}) collective-permute-start(bf16[2,4,1,16,768]{4,3,1,0,2:T(8,128)(2,1)S(1)} %fusion.52), channel_id=1, source_target_pairs={{0,7},{1,0},{2,1},{3,2},{4,3},{5,4},{6,5},{7,6},{8,15},{9,8},{10,9... | collective-permute-start | bytes 589832 | tf_op jit(solution)/shard_map/ppermute | solution.py:61
  166.0 6.7 %collective-permute-start.4 = (bf16[2,4,1,16,768]{4,3,1,0,2:T(8,128)(2,1)S(1)}, bf16[2,4,1,16,768]{4,3,1,0,2:T(8,128)(2,1)S(1)}, u32[]{:S(2)}, u32[]{:S(2)}) collective-permute-start(bf16[2,4,1,16,768]{4,3,1,0,2:T(8,128)(2,1)S(1)} %fusion.45), channel_id=1, source_target_pairs={{0,1},{1,2},{2,3},{3,4},{4,5},{5,6},{6,7},{7,0},{8,9},{9,10},{10,1... | collective-permute-start | bytes 589832 | tf_op jit(solution)/shard_map/ppermute | solution.py:61
  166.2 15.5 %collective-permute-start.16 = (bf16[4,4,1,16,768]{4,3,0,1,2:T(8,128)(2,1)S(1)}, bf16[4,4,1,16,768]{4,3,0,1,2:T(8,128)(2,1)S(1)}, u32[]{:S(2)}, u32[]{:S(2)}) collective-permute-start(bf16[4,4,1,16,768]{4,3,0,1,2:T(8,128)(2,1)S(1)} %fusion.38), channel_id=1, source_target_pairs={{0,64},{64,128},{128,192},{192,0},{1,65},{65,129},{129,193},{193,1... | collective-permute-start | bytes 1179656 | tf_op jit(solution)/shard_map/ppermute | solution.py:61
  166.4 15.5 %collective-permute-start.19 = (bf16[4,4,1,16,768]{4,3,0,1,2:T(8,128)(2,1)S(1)}, bf16[4,4,1,16,768]{4,3,0,1,2:T(8,128)(2,1)S(1)}, u32[]{:S(2)}, u32[]{:S(2)}) collective-permute-start(bf16[4,4,1,16,768]{4,3,0,1,2:T(8,128)(2,1)S(1)} %fusion.35), channel_id=1, source_target_pairs={{0,192},{64,0},{128,64},{192,128},{1,193},{65,1},{129,65},{193,129... | collective-permute-start | bytes 1179656 | tf_op jit(solution)/shard_map/ppermute | solution.py:61
  169.4 7.4 %collective-permute-start.12 = (bf16[2,4,1,16,768]{4,3,1,0,2:T(8,128)(2,1)S(1)}, bf16[2,4,1,16,768]{4,3,1,0,2:T(8,128)(2,1)S(1)}, u32[]{:S(2)}, u32[]{:S(2)}) collective-permute-start(bf16[2,4,1,16,768]{4,3,1,0,2:T(8,128)(2,1)S(1)} %fusion.51), channel_id=1, source_target_pairs={{0,7},{1,0},{2,1},{3,2},{4,3},{5,4},{6,5},{7,6},{8,15},{9,8},{10,9... | collective-permute-start | bytes 589832 | tf_op jit(solution)/shard_map/ppermute | solution.py:61
  172.8 8.2 %collective-permute-start.5 = (bf16[2,4,1,16,768]{4,3,1,0,2:T(8,128)(2,1)S(1)}, bf16[2,4,1,16,768]{4,3,1,0,2:T(8,128)(2,1)S(1)}, u32[]{:S(2)}, u32[]{:S(2)}) collective-permute-start(bf16[2,4,1,16,768]{4,3,1,0,2:T(8,128)(2,1)S(1)} %fusion.44), channel_id=1, source_target_pairs={{0,1},{1,2},{2,3},{3,4},{4,5},{5,6},{6,7},{7,0},{8,9},{9,10},{10,1... | collective-permute-start | bytes 589832 | tf_op jit(solution)/shard_map/ppermute | solution.py:61
  176.9 10.8 %collective-permute-start.13 = (bf16[2,4,1,16,768]{4,3,1,0,2:T(8,128)(2,1)S(1)}, bf16[2,4,1,16,768]{4,3,1,0,2:T(8,128)(2,1)S(1)}, u32[]{:S(2)}, u32[]{:S(2)}) collective-permute-start(bf16[2,4,1,16,768]{4,3,1,0,2:T(8,128)(2,1)S(1)} %fusion.50), channel_id=1, source_target_pairs={{0,7},{1,0},{2,1},{3,2},{4,3},{5,4},{6,5},{7,6},{8,15},{9,8},{10,9... | collective-permute-start | bytes 589832 | tf_op jit(solution)/shard_map/ppermute | solution.py:61
  181.7 8.3 %collective-permute-start.6 = (bf16[2,4,1,16,768]{4,3,1,0,2:T(8,128)(2,1)}, bf16[2,4,1,16,768]{4,3,1,0,2:T(8,128)(2,1)}, u32[]{:S(2)}, u32[]{:S(2)}) collective-permute-start(bf16[2,4,1,16,768]{4,3,1,0,2:T(8,128)(2,1)} %fusion.43), channel_id=1, source_target_pairs={{0,1},{1,2},{2,3},{3,4},{4,5},{5,6},{6,7},{7,0},{8,9},{9,10},{10,1... | collective-permute-start | bytes 589832 | tf_op jit(solution)/shard_map/ppermute | solution.py:61
  183.0 21.8 %all-to-all-start.1 = ((bf16[8,4,1,16,768]{4,3,1,2,0:T(8,128)(2,1)}), bf16[8,4,1,16,768]{4,3,1,2,0:T(8,128)(2,1)}, u32[]{:S(2)}, u32[]{:S(2)}) async-start(bf16[8,4,1,16,768]{4,3,1,2,0:T(8,128)(2,1)} %copy.239), calls=%async_computation.2 | async-start | bytes 1572864 | tf_op jit(solution)/shard_map/all_to_all | solution.py:78
  187.7 34.7 %reduce-scatter.2.cloned.1.call-start = ((), (), s32[]{:S(2)}) async-start(), calls=%async_computation.4 | async-start | bytes 491520 | tf_op jit(solution)/shard_map/reduce_scatter | solution.py:197
  224.0 13.2 %all-to-all-start.2 = ((bf16[8,1,16,768]{3,2,1,0:T(8,128)(2,1)}), bf16[8,1,16,768]{3,2,1,0:T(8,128)(2,1)S(1)}, u32[]{:S(2)}, u32[]{:S(2)}) async-start(bf16[8,1,16,768]{3,2,1,0:T(8,128)(2,1)} %maximum_bitcast_fusion.1), calls=%async_computation.3 | async-start | bytes 393216 | tf_op jit(solution)/shard_map/all_to_all | solution.py:201
Sparse Core Ops, SparseCore 0:
  30.8 90.1 all-gather.3
  192.0 30.4 reduce-scatter.1

commit v7 on v6

--- a/solution.py
+++ b/solution.py
@@ -175,7 +175,6 @@
     down_split = w_down.reshape(local_experts, hidden_local, tensor_count, slice_width)
     owner_half = owner_count // 2
     group_half = group_count // 2
-    tensor_half = tensor_count // 2
 
     def down(rows, columns, spec):
         return jnp.einsum(spec, rows, columns, preferred_element_type=jnp.float32)
@@ -188,12 +187,13 @@
         "tp",
         0,
     )
-    y_first = both_ways(
-        down(y_rows, down_split[:, :, :tensor_half], "jgacf,jftd->gtajcd"),
-        down(y_rows, down_split[:, :, tensor_half:], "jgacf,jftd->gtajcd"),
+    y_first = lax.psum_scatter(
+        down(y_rows, down_split, "jgacf,jftd->gtajcd").astype(jnp.bfloat16),
         "grp",
-        0,
-    )
+        scatter_dimension=0,
+        tiled=True,
+    )
+    y_first = y_first[0].astype(jnp.float32)
     z_done = lax.psum_scatter(z_first.astype(jnp.bfloat16), "grp", scatter_dimension=0, tiled=True)
     z_done = z_done[0].astype(jnp.float32)
     y_done = exchange_sum(y_first, "tp")

time: 246 us -> 249 us (1.012)
  waiting for transfers between devices: 130 us -> 145 us
  starting transfers between devices: 47.6 us -> 37.7 us
  local copies, waits for them, and re-layouts: 19.8 us -> 14.6 us
  matrix products: 14.2 us -> 18.1 us
    ppermute x20 -> x14, starting transfers between devices: 29 us -> 18.5 us  [ring_reduce_scatter(): arrived = lax.ppermute(total.astype(jnp.bfloat16), axis, pairs)]
    ppermute x20 -> x14, waiting for transfers between devices: 12.1 us -> 20.6 us  [ring_reduce_scatter(): arrived = lax.ppermute(total.astype(jnp.bfloat16), axis, pairs)]
    unnamed x34 -> x33, local copies, waits for them, and re-layouts: 16.1 us -> 8.6 us
    all_gather x1, waiting for transfers between devices: 80.8 us -> 85.7 us  [per_device(): gathered = lax.all_gather(payload[None], ('grp', 'tp'), axis=0, tiled=True)]
    dot_general x4 -> x3, matrix products: 3.73 us -> 7.61 us  [down(): return jnp.einsum(spec, rows, columns, preferred_element_type=jnp.float32)]
  transfers between devices with their start and end apart: 25 -> 20, of which waited for: 12 -> 13; matrix products, arithmetic and copies ran while one was open for 8% -> 9% of each run, Pallas kernels for 0% -> 0%
where the time goes in v7:
time: 249 us; the launch traced here: 248 us
  waiting for transfers between devices  145 us (58%)
  starting transfers between devices  37.7 us (15%)
  matrix products  18.1 us (7%)
  other arithmetic  17.8 us (7%)
  between operations  14.7 us (6%)
  local copies, waits for them, and re-layouts  14.6 us (6%)
    all_gather x1, waiting for transfers between devices, per_device(): gathered = lax.all_gather(payload[None], ('grp', 'tp'), axis=0, tiled=True)  85.7 us
    ppermute x14, waiting for transfers between devices, ring_reduce_scatter(): arrived = lax.ppermute(total.astype(jnp.bfloat16), axis, pairs)  20.6 us
    ppermute x14, starting transfers between devices, ring_reduce_scatter(): arrived = lax.ppermute(total.astype(jnp.bfloat16), axis, pairs)  18.5 us
    reduce_scatter x1, waiting for transfers between devices, per_device(): lax.psum_scatter(z_first.astype(jnp.bfloat16), 'grp', scatter_dimension=0...  17.8 us
    all_to_all x1, waiting for transfers between devices, exchange_sum(): moved = lax.all_to_all(parts.astype(jnp.bfloat16), axis, 0, 0, tiled=True)  11.3 us
    unnamed x33, local copies, waits for them, and re-layouts  8.6 us
    dot_general x3, matrix products, down(): return jnp.einsum(spec, rows, columns, preferred_element_type=jnp.float32)  7.61 us
    all_to_all x1, starting transfers between devices, per_device(): lax.all_to_all(summed.astype(jnp.bfloat16), 'ex', split_axis=0, concat_ax...  7.33 us
  transfers between devices with their start and end apart: 20, of which 13 were waited for; matrix products, arithmetic and copies ran while one was open for 9% of the time, Pallas kernels for 0%

profile of v7, /device:TPU:1, one launch (start us, length us, event | category | flops | bytes accessed | tf_op | source)
XLA Modules:
  0.0 248.0 jit_solution(12182791272602477108)
XLA Ops:
  7.2 0.8 broadcast_multiply_fusion
  8.0 0.9 copy.203
  8.9 0.7 iota_compare_fusion.3
  10.6 0.9 reshape.586
  11.4 1.3 fusion.81
  12.7 2.3 fusion.80
  16.6 0.9 convolution_convert_fusion
  17.5 6.5 %all-to-all-start = ((bf16[8,16,768]{2,1,0:T(8,128)(2,1)}), bf16[8,16,768]{2,1,0:T(8,128)(2,1)S(1)}, u32[]{:S(2)}, u32[]{:S(2)}) async-start(bf16[8,16,768]{2,1,0:T(8,128)(2,1)} %bitcast.360), calls=%async_computation | async-start | bytes 393216 | tf_op jit(solution)/shard_map/all_to_all | solution.py:141
  24.1 1.2 fusion.61
  26.1 3.9 %all-to-all-done = bf16[8,16,768]{2,1,0:T(8,128)(2,1)S(1)} async-done(((bf16[8,16,768]{2,1,0:T(8,128)(2,1)}), bf16[8,16,768]{2,1,0:T(8,128)(2,1)S(1)}, u32[]{:S(2)}, u32[]{:S(2)}) %all-to-all-start) | async-done | bytes 196640 | tf_op jit(solution)/shard_map/all_to_all | solution.py:141
  30.9 4.5 %copy.268 = bf16[32,8,8,768]{3,2,1,0:T(8,128)(2,1)} copy(bf16[32,8,8,768]{3,1,2,0:T(8,128)(2,1)} %bitcast.354) | data formatting | bytes 6291456
  35.3 85.7 %all-gather.4.cloned.1.call-done = bf16[32,130,768]{2,1,0:T(8,128)(2,1)} async-done(((bf16[1,130,768]{2,1,0:T(8,128)(2,1)}), bf16[32,130,768]{2,1,0:T(8,128)(2,1)}) %all-gather.4.cloned.1.call-update) | async-done | bytes 6389776 | tf_op jit(solution)/shard_map/all_gather | solution.py:144
  121.0 0.9 slice_convert_fusion
  121.9 4.5 %multiply_reduce_fusion = f32[32,130]{1,0:T(8,128)S(1)} fusion(bf16[32,130,768]{2,1,0:T(8,128)(2,1)} %all-gather.4.cloned.1.call-done), kind=kLoop, calls=%fused_computation | loop fusion | flops 9580480 | bytes 6406400 | tf_op jit(solution)/shard_map/reduce_sum | solution.py:163
  126.7 1.9 fusion.15
  128.7 1.9 fusion.14
  130.9 1.6 copy-done.1
  132.4 3.0 %convert_bitcast_fusion = bf16[4,8,4,1,16,768]{5,4,1,2,0,3:T(8,128)(2,1)} fusion(bf16[256,8,768,1,1]{2,1,0,4,3:T(8,128)(2,1)S(1)} %bitcast.349, bf16[1,4,8,16,256]{4,3,2,1,0:T(8,128)(2,1)S(1)} %multiply_convert_fusion.7), kind=kOutput, calls=%fused_computation.6 | convolution fusion | flops 806879232 | bytes 6422528 | tf_op jit(solution)/shard_map/jgacf,jftd->gtajcd/dot_general | solution.py:180
  136.0 3.3 %fusion.2 = f32[2,4,16,8,768]{4,2,1,0,3:T(8,128)S(1)} fusion(bf16[256,8,768,1,1]{2,1,0,4,3:T(8,128)(2,1)} %bitcast.348, bf16[1,4,8,16,256]{4,3,2,1,0:T(8,128)(2,1)S(1)} %multiply_convert_fusion.7), kind=kOutput, calls=%fused_computation.4 | convolution fusion | flops 402653184 | bytes 6356992 | tf_op jit(solution)/shard_map/jgacf,jftd->tgajcd/dot_general | solution.py:180
  139.3 1.2 collective-permute-start.7
  140.5 1.3 fusion.6
  141.8 1.4 slice.115
  144.8 2.1 collective-permute-start.8
  146.9 3.3 %collective-permute-done = bf16[2,4,1,16,768]{4,3,1,0,2:T(8,128)(2,1)S(1)} collective-permute-done((bf16[2,4,1,16,768]{4,3,1,0,2:T(8,128)(2,1)S(1)}, bf16[2,4,1,16,768]{4,3,1,0,2:T(8,128)(2,1)S(1)}, u32[]{:S(2)}, u32[]{:S(2)}) %collective-permute-start) | collective-permute-done | bytes 196640 | tf_op jit(solution)/shard_map/ppermute | solution.py:61
  150.5 2.7 %collective-permute-start.9 = (bf16[2,4,1,16,768]{4,3,1,0,2:T(8,128)(2,1)S(1)}, bf16[2,4,1,16,768]{4,3,1,0,2:T(8,128)(2,1)S(1)}, u32[]{:S(2)}, u32[]{:S(2)}) collective-permute-start(bf16[2,4,1,16,768]{4,3,1,0,2:T(8,128)(2,1)S(1)} %fusion.48), channel_id=1, source_target_pairs={{0,7},{1,0},{2,1},{3,2},{4,3},{5,4},{6,5},{7,6},{8,15},{9,8},{10,9... | collective-permute-start | bytes 589832 | tf_op jit(solution)/shard_map/ppermute | solution.py:61
  153.2 3.3 %collective-permute-done.1 = bf16[2,4,1,16,768]{4,3,1,0,2:T(8,128)(2,1)S(1)} collective-permute-done((bf16[2,4,1,16,768]{4,3,1,0,2:T(8,128)(2,1)S(1)}, bf16[2,4,1,16,768]{4,3,1,0,2:T(8,128)(2,1)S(1)}, u32[]{:S(2)}, u32[]{:S(2)}) %collective-permute-start.1) | collective-permute-done | bytes 196640 | tf_op jit(solution)/shard_map/ppermute | solution.py:61
  156.7 2.7 %collective-permute-start.10 = (bf16[2,4,1,16,768]{4,3,1,0,2:T(8,128)(2,1)S(1)}, bf16[2,4,1,16,768]{4,3,1,0,2:T(8,128)(2,1)S(1)}, u32[]{:S(2)}, u32[]{:S(2)}) collective-permute-start(bf16[2,4,1,16,768]{4,3,1,0,2:T(8,128)(2,1)S(1)} %fusion.47), channel_id=1, source_target_pairs={{0,7},{1,0},{2,1},{3,2},{4,3},{5,4},{6,5},{7,6},{8,15},{9,8},{10,9... | collective-permute-start | bytes 589832 | tf_op jit(solution)/shard_map/ppermute | solution.py:61
  159.4 3.3 %collective-permute-done.2 = bf16[2,4,1,16,768]{4,3,1,0,2:T(8,128)(2,1)S(1)} collective-permute-done((bf16[2,4,1,16,768]{4,3,1,0,2:T(8,128)(2,1)S(1)}, bf16[2,4,1,16,768]{4,3,1,0,2:T(8,128)(2,1)S(1)}, u32[]{:S(2)}, u32[]{:S(2)}) %collective-permute-start.2) | collective-permute-done | bytes 196640 | tf_op jit(solution)/shard_map/ppermute | solution.py:61
  163.0 2.7 %collective-permute-start.11 = (bf16[2,4,1,16,768]{4,3,1,0,2:T(8,128)(2,1)S(1)}, bf16[2,4,1,16,768]{4,3,1,0,2:T(8,128)(2,1)S(1)}, u32[]{:S(2)}, u32[]{:S(2)}) collective-permute-start(bf16[2,4,1,16,768]{4,3,1,0,2:T(8,128)(2,1)S(1)} %fusion.46), channel_id=1, source_target_pairs={{0,7},{1,0},{2,1},{3,2},{4,3},{5,4},{6,5},{7,6},{8,15},{9,8},{10,9... | collective-permute-start | bytes 589832 | tf_op jit(solution)/shard_map/ppermute | solution.py:61
  165.7 3.3 %collective-permute-done.3 = bf16[2,4,1,16,768]{4,3,1,0,2:T(8,128)(2,1)S(1)} collective-permute-done((bf16[2,4,1,16,768]{4,3,1,0,2:T(8,128)(2,1)S(1)}, bf16[2,4,1,16,768]{4,3,1,0,2:T(8,128)(2,1)S(1)}, u32[]{:S(2)}, u32[]{:S(2)}) %collective-permute-start.3) | collective-permute-done | bytes 196640 | tf_op jit(solution)/shard_map/ppermute | solution.py:61
  169.2 2.8 %collective-permute-start.12 = (bf16[2,4,1,16,768]{4,3,1,0,2:T(8,128)(2,1)S(1)}, bf16[2,4,1,16,768]{4,3,1,0,2:T(8,128)(2,1)S(1)}, u32[]{:S(2)}, u32[]{:S(2)}) collective-permute-start(bf16[2,4,1,16,768]{4,3,1,0,2:T(8,128)(2,1)S(1)} %fusion.45), channel_id=1, source_target_pairs={{0,7},{1,0},{2,1},{3,2},{4,3},{5,4},{6,5},{7,6},{8,15},{9,8},{10,9... | collective-permute-start | bytes 589832 | tf_op jit(solution)/shard_map/ppermute | solution.py:61
  172.0 3.1 %collective-permute-done.4 = bf16[2,4,1,16,768]{4,3,1,0,2:T(8,128)(2,1)S(1)} collective-permute-done((bf16[2,4,1,16,768]{4,3,1,0,2:T(8,128)(2,1)S(1)}, bf16[2,4,1,16,768]{4,3,1,0,2:T(8,128)(2,1)S(1)}, u32[]{:S(2)}, u32[]{:S(2)}) %collective-permute-start.4) | collective-permute-done | bytes 196640 | tf_op jit(solution)/shard_map/ppermute | solution.py:61
  175.4 3.2 %collective-permute-start.13 = (bf16[2,4,1,16,768]{4,3,1,0,2:T(8,128)(2,1)S(1)}, bf16[2,4,1,16,768]{4,3,1,0,2:T(8,128)(2,1)S(1)}, u32[]{:S(2)}, u32[]{:S(2)}) collective-permute-start(bf16[2,4,1,16,768]{4,3,1,0,2:T(8,128)(2,1)S(1)} %fusion.44), channel_id=1, source_target_pairs={{0,7},{1,0},{2,1},{3,2},{4,3},{5,4},{6,5},{7,6},{8,15},{9,8},{10,9... | collective-permute-start | bytes 589832 | tf_op jit(solution)/shard_map/ppermute | solution.py:61
  178.6 3.8 %collective-permute-done.5 = bf16[2,4,1,16,768]{4,3,1,0,2:T(8,128)(2,1)S(1)} collective-permute-done((bf16[2,4,1,16,768]{4,3,1,0,2:T(8,128)(2,1)S(1)}, bf16[2,4,1,16,768]{4,3,1,0,2:T(8,128)(2,1)S(1)}, u32[]{:S(2)}, u32[]{:S(2)}) %collective-permute-start.5) | collective-permute-done | bytes 196640 | tf_op jit(solution)/shard_map/ppermute | solution.py:61
  182.4 0.7 fusion.37
  183.1 2.2 copy.230
  185.3 5.1 %all-to-all-start.1 = ((bf16[8,4,1,16,768]{4,3,1,2,0:T(8,128)(2,1)}), bf16[8,4,1,16,768]{4,3,1,2,0:T(8,128)(2,1)}, u32[]{:S(2)}, u32[]{:S(2)}) async-start(bf16[8,4,1,16,768]{4,3,1,2,0:T(8,128)(2,1)} %copy.230), calls=%async_computation.3 | async-start | bytes 1572864 | tf_op jit(solution)/shard_map/all_to_all | solution.py:78
  190.4 1.0 fusion.43
  191.5 1.1 fusion.50
  192.6 0.8 pad_maximum_fusion
  193.4 0.7 bitcast_convert_fusion.1
  194.7 0.7 select_reduce_fusion.1
  195.4 11.3 %all-to-all-done.1 = bf16[8,4,1,16,768]{4,3,1,2,0:T(8,128)(2,1)} async-done(((bf16[8,4,1,16,768]{4,3,1,2,0:T(8,128)(2,1)}), bf16[8,4,1,16,768]{4,3,1,2,0:T(8,128)(2,1)}, u32[]{:S(2)}, u32[]{:S(2)}) %all-to-all-start.1) | async-done | bytes 786464 | tf_op jit(solution)/shard_map/all_to_all | solution.py:78
  206.7 1.2 reduce.14
  208.0 17.8 %reduce-scatter.3.cloned.1.call-done = bf16[1,4,1,16,768]{4,3,1,0,2:T(8,128)(2,1)} async-done(((bf16[4,4,1,16,768]{4,3,1,0,2:T(8,128)(2,1)}), bf16[1,4,1,16,768]{4,3,1,0,2:T(8,128)(2,1)}) %reduce-scatter.3.cloned.1.call-update) | async-done | bytes 98320 | tf_op jit(solution)/shard_map/reduce_scatter | solution.py:197
  225.8 1.6 maximum_bitcast_fusion.1
  227.3 7.3 %all-to-all-start.2 = ((bf16[8,1,16,768]{3,2,1,0:T(8,128)(2,1)}), bf16[8,1,16,768]{3,2,1,0:T(8,128)(2,1)S(1)}, u32[]{:S(2)}, u32[]{:S(2)}) async-start(bf16[8,1,16,768]{3,2,1,0:T(8,128)(2,1)} %maximum_bitcast_fusion.1), calls=%async_computation.4 | async-start | bytes 393216 | tf_op jit(solution)/shard_map/all_to_all | solution.py:201
  234.7 5.8 %all-to-all-done.2 = bf16[8,1,16,768]{3,2,1,0:T(8,128)(2,1)S(1)} async-done(((bf16[8,1,16,768]{3,2,1,0:T(8,128)(2,1)}), bf16[8,1,16,768]{3,2,1,0:T(8,128)(2,1)S(1)}, u32[]{:S(2)}, u32[]{:S(2)}) %all-to-all-start.2) | async-done | bytes 196640 | tf_op jit(solution)/shard_map/all_to_all | solution.py:201
  (112 shorter events, 9.0 us)
Async XLA Ops:
  7.2 119.4 %copy-start = (bf16[1,6144,256]{2,1,0:T(8,128)(2,1)S(1)}, bf16[1,6144,256]{2,1,0:T(8,128)(2,1)}, u32[]{:S(2)}) copy-start(bf16[1,6144,256]{2,1,0:T(8,128)(2,1)} %param.30) | copy-start | bytes 9437188
  7.2 8.4 %copy-start.12 = (bf16[16,2,128]{2,1,0:T(2,128)(2,1)S(1)}, bf16[16,2,128]{2,1,0:T(2,128)(2,1)}, u32[]{:S(2)}) copy-start(bf16[16,2,128]{2,1,0:T(2,128)(2,1)} %param.22) | copy-start | bytes 24580
  11.4 4.4 %copy-start.11 = (bf16[16,1,512,128]{3,2,1,0:T(8,128)(2,1)S(1)}, bf16[16,1,512,128]{3,2,1,0:T(8,128)(2,1)}, u32[]{:S(2)}) copy-start(bf16[16,1,512,128]{3,2,1,0:T(8,128)(2,1)} %param.24) | copy-start | bytes 6291460
  15.1 1.4 copy-start.7
  15.2 8.8 %copy-start.9 = (bf16[768]{0:T(1024)(128)(2,1)S(1)}, bf16[768]{0:T(1024)(128)(2,1)}, u32[]{:S(2)}) copy-start(bf16[768]{0:T(1024)(128)(2,1)} %param.26) | copy-start | bytes 4612
  16.6 18.7 %copy-start.6 = (bf16[16,2,768]{2,1,0:T(2,128)(2,1)}, bf16[16,2,768]{2,1,0:T(2,128)(2,1)S(1)}, u32[]{:S(2)}) copy-start(bf16[16,2,768]{2,1,0:T(2,128)(2,1)S(1)} %copy.234) | copy-start | bytes 147460
  17.5 12.4 %all-to-all-start = ((bf16[8,16,768]{2,1,0:T(8,128)(2,1)}), bf16[8,16,768]{2,1,0:T(8,128)(2,1)S(1)}, u32[]{:S(2)}, u32[]{:S(2)}) async-start(bf16[8,16,768]{2,1,0:T(8,128)(2,1)} %bitcast.360), calls=%async_computation | async-start | bytes 393216 | tf_op jit(solution)/shard_map/all_to_all | solution.py:141
  24.0 97.0 %all-gather.4.cloned.1.call-start = ((), (), s32[]{:S(2)}) async-start(), calls=%async_computation.7 | async-start | bytes 6893568 | tf_op jit(solution)/shard_map/all_gather | solution.py:144
  30.6 152.5 %reduce-scatter.5.cloned.1.call-start = ((), (), s32[]{:S(2)}) async-start(), calls=%async_computation.6 | async-start | bytes 3932160 | tf_op jit(solution)/shard_map/reduce_scatter | solution.py:190
  121.9 4.8 %copy-start.4 = (bf16[32,130,768]{2,1,0:T(8,128)(2,1)S(1)}, bf16[32,130,768]{2,1,0:T(8,128)(2,1)}, u32[]{:S(2)}) copy-start(bf16[32,130,768]{2,1,0:T(8,128)(2,1)} %all-gather.4.cloned.1.call-done) | copy-start | bytes 19169284
  126.5 2.1 copy-start.8
  126.7 1.9 copy-start.10
  128.6 1.9 slice-start
  130.6 1.9 copy-start.1
  136.0 4.6 %copy-start.2 = (bf16[32,8,8,768]{3,2,1,0:T(8,128)(2,1)S(1)}, bf16[32,8,8,768]{3,2,1,0:T(8,128)(2,1)}, u32[]{:S(2)}) copy-start(bf16[32,8,8,768]{3,2,1,0:T(8,128)(2,1)} %copy.268) | copy-start | bytes 9437188
  139.3 36.1 %copy-start.3 = (f32[2,4,16,8,768]{4,2,1,0,3:T(8,128)}, f32[2,4,16,8,768]{4,2,1,0,3:T(8,128)S(1)}, u32[]{:S(2)}) copy-start(f32[2,4,16,8,768]{4,2,1,0,3:T(8,128)S(1)} %fusion.2) | copy-start | bytes 9437188
  139.3 5.4 %collective-permute-start.7 = (bf16[2,4,1,16,768]{4,3,1,0,2:T(8,128)(2,1)S(1)}, bf16[2,4,1,16,768]{4,3,1,0,2:T(8,128)(2,1)S(1)}, u32[]{:S(2)}, u32[]{:S(2)}) collective-permute-start(bf16[2,4,1,16,768]{4,3,1,0,2:T(8,128)(2,1)S(1)} %fusion.55), channel_id=1, source_target_pairs={{0,7},{1,0},{2,1},{3,2},{4,3},{5,4},{6,5},{7,6},{8,15},{9,8},{10,9... | collective-permute-start | bytes 589832 | tf_op jit(solution)/shard_map/ppermute | solution.py:61
  141.8 40.6 %copy-start.5 = (f32[2,4,16,8,768]{4,2,3,1,0:T(8,128)}, f32[2,4,16,8,768]{4,2,3,1,0:T(8,128)S(1)}, u32[]{:S(2)}) copy-start(f32[2,4,16,8,768]{4,2,3,1,0:T(8,128)S(1)} %fusion.6) | copy-start | bytes 9437188
  143.8 6.4 %collective-permute-start = (bf16[2,4,1,16,768]{4,3,1,0,2:T(8,128)(2,1)S(1)}, bf16[2,4,1,16,768]{4,3,1,0,2:T(8,128)(2,1)S(1)}, u32[]{:S(2)}, u32[]{:S(2)}) collective-permute-start(bf16[2,4,1,16,768]{4,3,1,0,2:T(8,128)(2,1)S(1)} %fusion.56), channel_id=1, source_target_pairs={{0,1},{1,2},{2,3},{3,4},{4,5},{5,6},{6,7},{7,0},{8,9},{9,10},{10,1... | collective-permute-start | bytes 589832 | tf_op jit(solution)/shard_map/ppermute | solution.py:61
  144.8 5.6 %collective-permute-start.8 = (bf16[2,4,1,16,768]{4,3,1,0,2:T(8,128)(2,1)S(1)}, bf16[2,4,1,16,768]{4,3,1,0,2:T(8,128)(2,1)S(1)}, u32[]{:S(2)}, u32[]{:S(2)}) collective-permute-start(bf16[2,4,1,16,768]{4,3,1,0,2:T(8,128)(2,1)S(1)} %fusion.49), channel_id=1, source_target_pairs={{0,7},{1,0},{2,1},{3,2},{4,3},{5,4},{6,5},{7,6},{8,15},{9,8},{10,9... | collective-permute-start | bytes 589832 | tf_op jit(solution)/shard_map/ppermute | solution.py:61
  150.3 6.2 %collective-permute-start.1 = (bf16[2,4,1,16,768]{4,3,1,0,2:T(8,128)(2,1)S(1)}, bf16[2,4,1,16,768]{4,3,1,0,2:T(8,128)(2,1)S(1)}, u32[]{:S(2)}, u32[]{:S(2)}) collective-permute-start(bf16[2,4,1,16,768]{4,3,1,0,2:T(8,128)(2,1)S(1)} %fusion.42), channel_id=1, source_target_pairs={{0,1},{1,2},{2,3},{3,4},{4,5},{5,6},{6,7},{7,0},{8,9},{9,10},{10,1... | collective-permute-start | bytes 589832 | tf_op jit(solution)/shard_map/ppermute | solution.py:61
  150.5 6.2 %collective-permute-start.9 = (bf16[2,4,1,16,768]{4,3,1,0,2:T(8,128)(2,1)S(1)}, bf16[2,4,1,16,768]{4,3,1,0,2:T(8,128)(2,1)S(1)}, u32[]{:S(2)}, u32[]{:S(2)}) collective-permute-start(bf16[2,4,1,16,768]{4,3,1,0,2:T(8,128)(2,1)S(1)} %fusion.48), channel_id=1, source_target_pairs={{0,7},{1,0},{2,1},{3,2},{4,3},{5,4},{6,5},{7,6},{8,15},{9,8},{10,9... | collective-permute-start | bytes 589832 | tf_op jit(solution)/shard_map/ppermute | solution.py:61
  156.6 6.2 %collective-permute-start.2 = (bf16[2,4,1,16,768]{4,3,1,0,2:T(8,128)(2,1)S(1)}, bf16[2,4,1,16,768]{4,3,1,0,2:T(8,128)(2,1)S(1)}, u32[]{:S(2)}, u32[]{:S(2)}) collective-permute-start(bf16[2,4,1,16,768]{4,3,1,0,2:T(8,128)(2,1)S(1)} %fusion.41), channel_id=1, source_target_pairs={{0,1},{1,2},{2,3},{3,4},{4,5},{5,6},{6,7},{7,0},{8,9},{9,10},{10,1... | collective-permute-start | bytes 589832 | tf_op jit(solution)/shard_map/ppermute | solution.py:61
  156.7 6.2 %collective-permute-start.10 = (bf16[2,4,1,16,768]{4,3,1,0,2:T(8,128)(2,1)S(1)}, bf16[2,4,1,16,768]{4,3,1,0,2:T(8,128)(2,1)S(1)}, u32[]{:S(2)}, u32[]{:S(2)}) collective-permute-start(bf16[2,4,1,16,768]{4,3,1,0,2:T(8,128)(2,1)S(1)} %fusion.47), channel_id=1, source_target_pairs={{0,7},{1,0},{2,1},{3,2},{4,3},{5,4},{6,5},{7,6},{8,15},{9,8},{10,9... | collective-permute-start | bytes 589832 | tf_op jit(solution)/shard_map/ppermute | solution.py:61
  162.8 6.2 %collective-permute-start.3 = (bf16[2,4,1,16,768]{4,3,1,0,2:T(8,128)(2,1)S(1)}, bf16[2,4,1,16,768]{4,3,1,0,2:T(8,128)(2,1)S(1)}, u32[]{:S(2)}, u32[]{:S(2)}) collective-permute-start(bf16[2,4,1,16,768]{4,3,1,0,2:T(8,128)(2,1)S(1)} %fusion.40), channel_id=1, source_target_pairs={{0,1},{1,2},{2,3},{3,4},{4,5},{5,6},{6,7},{7,0},{8,9},{9,10},{10,1... | collective-permute-start | bytes 589832 | tf_op jit(solution)/shard_map/ppermute | solution.py:61
  163.0 6.2 %collective-permute-start.11 = (bf16[2,4,1,16,768]{4,3,1,0,2:T(8,128)(2,1)S(1)}, bf16[2,4,1,16,768]{4,3,1,0,2:T(8,128)(2,1)S(1)}, u32[]{:S(2)}, u32[]{:S(2)}) collective-permute-start(bf16[2,4,1,16,768]{4,3,1,0,2:T(8,128)(2,1)S(1)} %fusion.46), channel_id=1, source_target_pairs={{0,7},{1,0},{2,1},{3,2},{4,3},{5,4},{6,5},{7,6},{8,15},{9,8},{10,9... | collective-permute-start | bytes 589832 | tf_op jit(solution)/shard_map/ppermute | solution.py:61
  169.1 6.1 %collective-permute-start.4 = (bf16[2,4,1,16,768]{4,3,1,0,2:T(8,128)(2,1)S(1)}, bf16[2,4,1,16,768]{4,3,1,0,2:T(8,128)(2,1)S(1)}, u32[]{:S(2)}, u32[]{:S(2)}) collective-permute-start(bf16[2,4,1,16,768]{4,3,1,0,2:T(8,128)(2,1)S(1)} %fusion.39), channel_id=1, source_target_pairs={{0,1},{1,2},{2,3},{3,4},{4,5},{5,6},{6,7},{7,0},{8,9},{9,10},{10,1... | collective-permute-start | bytes 589832 | tf_op jit(solution)/shard_map/ppermute | solution.py:61
  169.2 6.2 %collective-permute-start.12 = (bf16[2,4,1,16,768]{4,3,1,0,2:T(8,128)(2,1)S(1)}, bf16[2,4,1,16,768]{4,3,1,0,2:T(8,128)(2,1)S(1)}, u32[]{:S(2)}, u32[]{:S(2)}) collective-permute-start(bf16[2,4,1,16,768]{4,3,1,0,2:T(8,128)(2,1)S(1)} %fusion.45), channel_id=1, source_target_pairs={{0,7},{1,0},{2,1},{3,2},{4,3},{5,4},{6,5},{7,6},{8,15},{9,8},{10,9... | collective-permute-start | bytes 589832 | tf_op jit(solution)/shard_map/ppermute | solution.py:61
  175.2 7.2 %collective-permute-start.5 = (bf16[2,4,1,16,768]{4,3,1,0,2:T(8,128)(2,1)S(1)}, bf16[2,4,1,16,768]{4,3,1,0,2:T(8,128)(2,1)S(1)}, u32[]{:S(2)}, u32[]{:S(2)}) collective-permute-start(bf16[2,4,1,16,768]{4,3,1,0,2:T(8,128)(2,1)S(1)} %fusion.38), channel_id=1, source_target_pairs={{0,1},{1,2},{2,3},{3,4},{4,5},{5,6},{6,7},{7,0},{8,9},{9,10},{10,1... | collective-permute-start | bytes 589832 | tf_op jit(solution)/shard_map/ppermute | solution.py:61
  175.4 15.0 %collective-permute-start.13 = (bf16[2,4,1,16,768]{4,3,1,0,2:T(8,128)(2,1)S(1)}, bf16[2,4,1,16,768]{4,3,1,0,2:T(8,128)(2,1)S(1)}, u32[]{:S(2)}, u32[]{:S(2)}) collective-permute-start(bf16[2,4,1,16,768]{4,3,1,0,2:T(8,128)(2,1)S(1)} %fusion.44), channel_id=1, source_target_pairs={{0,7},{1,0},{2,1},{3,2},{4,3},{5,4},{6,5},{7,6},{8,15},{9,8},{10,9... | collective-permute-start | bytes 589832 | tf_op jit(solution)/shard_map/ppermute | solution.py:61
  183.1 8.4 %collective-permute-start.6 = (bf16[2,4,1,16,768]{4,3,1,0,2:T(8,128)(2,1)}, bf16[2,4,1,16,768]{4,3,1,0,2:T(8,128)(2,1)}, u32[]{:S(2)}, u32[]{:S(2)}) collective-permute-start(bf16[2,4,1,16,768]{4,3,1,0,2:T(8,128)(2,1)} %fusion.37), channel_id=1, source_target_pairs={{0,1},{1,2},{2,3},{3,4},{4,5},{5,6},{6,7},{7,0},{8,9},{9,10},{10,1... | collective-permute-start | bytes 589832 | tf_op jit(solution)/shard_map/ppermute | solution.py:61
  185.3 21.5 %all-to-all-start.1 = ((bf16[8,4,1,16,768]{4,3,1,2,0:T(8,128)(2,1)}), bf16[8,4,1,16,768]{4,3,1,2,0:T(8,128)(2,1)}, u32[]{:S(2)}, u32[]{:S(2)}) async-start(bf16[8,4,1,16,768]{4,3,1,2,0:T(8,128)(2,1)} %copy.230), calls=%async_computation.3 | async-start | bytes 1572864 | tf_op jit(solution)/shard_map/all_to_all | solution.py:78
  190.4 35.4 %reduce-scatter.3.cloned.1.call-start = ((), (), s32[]{:S(2)}) async-start(), calls=%async_computation.5 | async-start | bytes 491520 | tf_op jit(solution)/shard_map/reduce_scatter | solution.py:197
  227.3 13.2 %all-to-all-start.2 = ((bf16[8,1,16,768]{3,2,1,0:T(8,128)(2,1)}), bf16[8,1,16,768]{3,2,1,0:T(8,128)(2,1)S(1)}, u32[]{:S(2)}, u32[]{:S(2)}) async-start(bf16[8,1,16,768]{3,2,1,0:T(8,128)(2,1)} %maximum_bitcast_fusion.1), calls=%async_computation.4 | async-start | bytes 393216 | tf_op jit(solution)/shard_map/all_to_all | solution.py:201
Sparse Core Ops, SparseCore 0:
  30.8 90.1 all-gather.3
  135.6 38.2 reduce-scatter.4
  193.7 32.0 reduce-scatter.2

commit v8 on v6

--- a/solution.py
+++ b/solution.py
@@ -173,7 +173,7 @@
     up_sums = expert_in(w_up)
     hidden = (jax.nn.silu(gate_sums) * up_sums).astype(jnp.bfloat16)
     down_split = w_down.reshape(local_experts, hidden_local, tensor_count, slice_width)
-    owner_half = owner_count // 2
+    owner_half = (owner_count * 3) // 8
     group_half = group_count // 2
     tensor_half = tensor_count // 2
 

time: 246 us -> 258 us (1.049)
  waiting for transfers between devices: 130 us -> 144 us
    ppermute x20, waiting for transfers between devices: 12.1 us -> 27.8 us  [ring_reduce_scatter(): arrived = lax.ppermute(total.astype(jnp.bfloat16), axis, pairs)]
    all_to_all x1, waiting for transfers between devices: 10.9 us -> 0.01 us  [exchange_sum(): moved = lax.all_to_all(parts.astype(jnp.bfloat16), axis, 0, 0, tiled=True)]
    reduce_scatter x1, waiting for transfers between devices: 16.5 us -> 25.2 us  [per_device(): lax.psum_scatter(z_first.astype(jnp.bfloat16), 'grp', scatter_dimension=0...]
    unnamed x34 -> x36, local copies, waits for them, and re-layouts: 16.1 us -> 15 us
  transfers between devices with their start and end apart: 25 -> 25, of which waited for: 12 -> 10; matrix products, arithmetic and copies ran while one was open for 8% -> 8% of each run, Pallas kernels for 0% -> 0%
where the time goes in v8:
time: 258 us; the launch traced here: 257 us
  waiting for transfers between devices  144 us (56%)
  starting transfers between devices  46.6 us (18%)
  other arithmetic  19 us (7%)
  local copies, waits for them, and re-layouts  18.8 us (7%)
  between operations  15.1 us (6%)
  matrix products  14.3 us (6%)
    all_gather x1, waiting for transfers between devices, per_device(): gathered = lax.all_gather(payload[None], ('grp', 'tp'), axis=0, tiled=True)  80.8 us
    ppermute x20, starting transfers between devices, ring_reduce_scatter(): arrived = lax.ppermute(total.astype(jnp.bfloat16), axis, pairs)  27.9 us
    ppermute x20, waiting for transfers between devices, ring_reduce_scatter(): arrived = lax.ppermute(total.astype(jnp.bfloat16), axis, pairs)  27.8 us
    reduce_scatter x1, waiting for transfers between devices, per_device(): lax.psum_scatter(z_first.astype(jnp.bfloat16), 'grp', scatter_dimension=0...  25.2 us
    unnamed x36, local copies, waits for them, and re-layouts  15 us
    all_to_all x1, starting transfers between devices, per_device(): lax.all_to_all(summed.astype(jnp.bfloat16), 'ex', split_axis=0, concat_ax...  7.24 us
    all_to_all x1, starting transfers between devices, per_device(): lax.all_to_all(outgoing, 'ex', split_axis=0, concat_axis=0, tiled=True)  6.49 us
    all_to_all x1, waiting for transfers between devices, per_device(): lax.all_to_all(summed.astype(jnp.bfloat16), 'ex', split_axis=0, concat_ax...  5.84 us
  transfers between devices with their start and end apart: 25, of which 10 were waited for; matrix products, arithmetic and copies ran while one was open for 8% of the time, Pallas kernels for 0%

profile of v8, /device:TPU:1, one launch (start us, length us, event | category | flops | bytes accessed | tf_op | source)
XLA Modules:
  0.0 257.3 jit_solution(17395344595687583236)
XLA Ops:
  7.2 0.8 broadcast_multiply_fusion
  8.0 0.9 copy.210
  10.6 0.9 reshape.679
  11.4 1.3 fusion.87
  12.7 2.3 fusion.86
  16.6 0.9 convolution_convert_fusion
  17.5 6.5 %all-to-all-start = ((bf16[8,16,768]{2,1,0:T(8,128)(2,1)}), bf16[8,16,768]{2,1,0:T(8,128)(2,1)S(1)}, u32[]{:S(2)}, u32[]{:S(2)}) async-start(bf16[8,16,768]{2,1,0:T(8,128)(2,1)} %bitcast.446), calls=%async_computation | async-start | bytes 393216 | tf_op jit(solution)/shard_map/all_to_all | solution.py:141
  24.1 1.2 fusion.67
  26.1 3.9 %all-to-all-done = bf16[8,16,768]{2,1,0:T(8,128)(2,1)S(1)} async-done(((bf16[8,16,768]{2,1,0:T(8,128)(2,1)}), bf16[8,16,768]{2,1,0:T(8,128)(2,1)S(1)}, u32[]{:S(2)}, u32[]{:S(2)}) %all-to-all-start) | async-done | bytes 196640 | tf_op jit(solution)/shard_map/all_to_all | solution.py:141
  31.1 4.6 %copy.236 = bf16[1,256,6144]{1,2,0:T(8,128)(2,1)} copy(bf16[1,256,6144]{2,1,0:T(8,128)(2,1)} %param.31) | data formatting | bytes 6291456 | tf_op args[12]
  35.8 4.5 %copy.278 = bf16[32,8,8,768]{3,2,1,0:T(8,128)(2,1)} copy(bf16[32,8,8,768]{3,1,2,0:T(8,128)(2,1)} %bitcast.434) | data formatting | bytes 6291456
  40.3 80.8 %all-gather.4.cloned.1.call-done = bf16[32,130,768]{2,1,0:T(8,128)(2,1)} async-done(((bf16[1,130,768]{2,1,0:T(8,128)(2,1)}), bf16[32,130,768]{2,1,0:T(8,128)(2,1)}) %all-gather.4.cloned.1.call-update) | async-done | bytes 6389776 | tf_op jit(solution)/shard_map/all_gather | solution.py:144
  121.0 0.9 slice_convert_fusion
  122.0 4.5 %multiply_reduce_fusion = f32[32,130]{1,0:T(8,128)S(1)} fusion(bf16[32,130,768]{2,1,0:T(8,128)(2,1)} %all-gather.4.cloned.1.call-done), kind=kLoop, calls=%fused_computation | loop fusion | flops 9580480 | bytes 6406400 | tf_op jit(solution)/shard_map/reduce_sum | solution.py:163
  126.8 1.9 fusion.13
  128.7 1.9 fusion.12
  130.9 1.6 copy-done.2
  132.5 1.2 fusion.2
  133.7 1.2 fusion.4
  134.9 2.4 copy-done.1
  138.9 1.4 collective-permute-start.7
  140.9 2.7 %collective-permute-start.17 = (bf16[4,5,1,16,768]{4,3,0,1,2:T(8,128)(2,1)S(1)}, bf16[4,5,1,16,768]{4,3,0,1,2:T(8,128)(2,1)S(1)}, u32[]{:S(2)}, u32[]{:S(2)}) collective-permute-start(bf16[4,5,1,16,768]{4,3,0,1,2:T(8,128)(2,1)S(1)} %fusion.41), channel_id=1, source_target_pairs={{0,192},{64,0},{128,64},{192,128},{1,193},{65,1},{129,65},{193,129... | collective-permute-start | bytes 1474568 | tf_op jit(solution)/shard_map/ppermute | solution.py:61
  143.7 2.4 collective-permute-start.8
  146.2 2.0 collective-permute-done.8
  148.2 3.5 %collective-permute-start.9 = (bf16[2,3,1,16,768]{4,3,1,0,2:T(8,128)(2,1)S(1)}, bf16[2,3,1,16,768]{4,3,1,0,2:T(8,128)(2,1)S(1)}, u32[]{:S(2)}, u32[]{:S(2)}) collective-permute-start(bf16[2,3,1,16,768]{4,3,1,0,2:T(8,128)(2,1)S(1)} %fusion.54), channel_id=1, source_target_pairs={{0,7},{1,0},{2,1},{3,2},{4,3},{5,4},{6,5},{7,6},{8,15},{9,8},{10,9... | collective-permute-start | bytes 442376 | tf_op jit(solution)/shard_map/ppermute | solution.py:61
  151.8 2.0 collective-permute-done.9
  153.8 3.5 %collective-permute-start.10 = (bf16[2,3,1,16,768]{4,3,1,0,2:T(8,128)(2,1)S(1)}, bf16[2,3,1,16,768]{4,3,1,0,2:T(8,128)(2,1)S(1)}, u32[]{:S(2)}, u32[]{:S(2)}) collective-permute-start(bf16[2,3,1,16,768]{4,3,1,0,2:T(8,128)(2,1)S(1)} %fusion.53), channel_id=1, source_target_pairs={{0,7},{1,0},{2,1},{3,2},{4,3},{5,4},{6,5},{7,6},{8,15},{9,8},{10,9... | collective-permute-start | bytes 442376 | tf_op jit(solution)/shard_map/ppermute | solution.py:61
  157.8 2.7 %collective-permute-start.18 = (bf16[4,5,1,16,768]{4,3,0,1,2:T(8,128)(2,1)S(1)}, bf16[4,5,1,16,768]{4,3,0,1,2:T(8,128)(2,1)S(1)}, u32[]{:S(2)}, u32[]{:S(2)}) collective-permute-start(bf16[4,5,1,16,768]{4,3,0,1,2:T(8,128)(2,1)S(1)} %fusion.36), channel_id=1, source_target_pairs={{0,192},{64,0},{128,64},{192,128},{1,193},{65,1},{129,65},{193,129... | collective-permute-start | bytes 1474568 | tf_op jit(solution)/shard_map/ppermute | solution.py:61
  160.6 2.7 %collective-permute-start.11 = (bf16[2,3,1,16,768]{4,3,1,0,2:T(8,128)(2,1)S(1)}, bf16[2,3,1,16,768]{4,3,1,0,2:T(8,128)(2,1)S(1)}, u32[]{:S(2)}, u32[]{:S(2)}) collective-permute-start(bf16[2,3,1,16,768]{4,3,1,0,2:T(8,128)(2,1)S(1)} %fusion.52), channel_id=1, source_target_pairs={{0,7},{1,0},{2,1},{3,2},{4,3},{5,4},{6,5},{7,6},{8,15},{9,8},{10,9... | collective-permute-start | bytes 442376 | tf_op jit(solution)/shard_map/ppermute | solution.py:61
  163.5 3.6 %collective-permute-done.15 = bf16[4,5,1,16,768]{4,3,0,1,2:T(8,128)(2,1)S(1)} collective-permute-done((bf16[4,5,1,16,768]{4,3,0,1,2:T(8,128)(2,1)S(1)}, bf16[4,5,1,16,768]{4,3,0,1,2:T(8,128)(2,1)S(1)}, u32[]{:S(2)}, u32[]{:S(2)}) %collective-permute-start.15) | collective-permute-done | bytes 491552 | tf_op jit(solution)/shard_map/ppermute | solution.py:61
  167.4 3.0 %collective-permute-start.19 = (bf16[4,5,1,16,768]{4,3,0,1,2:T(8,128)(2,1)S(1)}, bf16[4,5,1,16,768]{4,3,0,1,2:T(8,128)(2,1)S(1)}, u32[]{:S(2)}, u32[]{:S(2)}) collective-permute-start(bf16[4,5,1,16,768]{4,3,0,1,2:T(8,128)(2,1)S(1)} %fusion.35), channel_id=1, source_target_pairs={{0,192},{64,0},{128,64},{192,128},{1,193},{65,1},{129,65},{193,129... | collective-permute-start | bytes 1474568 | tf_op jit(solution)/shard_map/ppermute | solution.py:61
  170.5 2.2 collective-permute-start.12
  173.4 3.7 %collective-permute-done.16 = bf16[4,5,1,16,768]{4,3,0,1,2:T(8,128)(2,1)S(1)} collective-permute-done((bf16[4,5,1,16,768]{4,3,0,1,2:T(8,128)(2,1)S(1)}, bf16[4,5,1,16,768]{4,3,0,1,2:T(8,128)(2,1)S(1)}, u32[]{:S(2)}, u32[]{:S(2)}) %collective-permute-start.16) | collective-permute-done | bytes 491552 | tf_op jit(solution)/shard_map/ppermute | solution.py:61
  177.5 1.0 copy.239
  178.5 4.9 %all-to-all-start.1 = ((bf16[8,5,1,16,768]{4,3,1,2,0:T(8,128)(2,1)}), bf16[8,5,1,16,768]{4,3,1,2,0:T(8,128)(2,1)}, u32[]{:S(2)}, u32[]{:S(2)}) async-start(bf16[8,5,1,16,768]{4,3,1,2,0:T(8,128)(2,1)} %copy.239), calls=%async_computation.2 | async-start | bytes 1966080 | tf_op jit(solution)/shard_map/all_to_all | solution.py:78
  183.5 1.0 fusion.50
  184.5 2.7 %collective-permute-start.13 = (bf16[2,3,1,16,768]{4,3,1,0,2:T(8,128)(2,1)S(1)}, bf16[2,3,1,16,768]{4,3,1,0,2:T(8,128)(2,1)S(1)}, u32[]{:S(2)}, u32[]{:S(2)}) collective-permute-start(bf16[2,3,1,16,768]{4,3,1,0,2:T(8,128)(2,1)S(1)} %fusion.50), channel_id=1, source_target_pairs={{0,7},{1,0},{2,1},{3,2},{4,3},{5,4},{6,5},{7,6},{8,15},{9,8},{10,9... | collective-permute-start | bytes 442376 | tf_op jit(solution)/shard_map/ppermute | solution.py:61
  187.2 1.0 fusion.43
  188.3 14.5 %collective-permute-done.13 = bf16[2,3,1,16,768]{4,3,1,0,2:T(8,128)(2,1)S(1)} collective-permute-done((bf16[2,3,1,16,768]{4,3,1,0,2:T(8,128)(2,1)S(1)}, bf16[2,3,1,16,768]{4,3,1,0,2:T(8,128)(2,1)S(1)}, u32[]{:S(2)}, u32[]{:S(2)}) %collective-permute-start.13) | collective-permute-done | bytes 147488 | tf_op jit(solution)/shard_map/ppermute | solution.py:61
  202.9 1.0 fusion.49
  203.9 2.0 collective-permute-done.6
  205.9 1.0 fusion.56
  206.9 0.8 pad_maximum_fusion.1
  208.3 1.3 reduce.14
  209.6 25.2 %reduce-scatter.2.cloned.1.call-done = bf16[1,3,1,16,768]{4,3,1,0,2:T(8,128)(2,1)} async-done(((bf16[4,3,1,16,768]{4,3,1,0,2:T(8,128)(2,1)}), bf16[1,3,1,16,768]{4,3,1,0,2:T(8,128)(2,1)}) %reduce-scatter.2.cloned.1.call-update) | async-done | bytes 73744 | tf_op jit(solution)/shard_map/reduce_scatter | solution.py:197
  234.9 1.6 pad_maximum_fusion.2
  236.4 7.2 %all-to-all-start.2 = ((bf16[8,1,16,768]{3,2,1,0:T(8,128)(2,1)}), bf16[8,1,16,768]{3,2,1,0:T(8,128)(2,1)S(1)}, u32[]{:S(2)}, u32[]{:S(2)}) async-start(bf16[8,1,16,768]{3,2,1,0:T(8,128)(2,1)} %pad_maximum_fusion.2), calls=%async_computation.3 | async-start | bytes 393216 | tf_op jit(solution)/shard_map/all_to_all | solution.py:201
  243.7 5.8 %all-to-all-done.2 = bf16[8,1,16,768]{3,2,1,0:T(8,128)(2,1)S(1)} async-done(((bf16[8,1,16,768]{3,2,1,0:T(8,128)(2,1)}), bf16[8,1,16,768]{3,2,1,0:T(8,128)(2,1)S(1)}, u32[]{:S(2)}, u32[]{:S(2)}) %all-to-all-start.2) | async-done | bytes 196640 | tf_op jit(solution)/shard_map/all_to_all | solution.py:201
  (134 shorter events, 11.6 us)
Async XLA Ops:
  7.2 119.4 %copy-start = (bf16[1,6144,256]{2,1,0:T(8,128)(2,1)S(1)}, bf16[1,6144,256]{2,1,0:T(8,128)(2,1)}, u32[]{:S(2)}) copy-start(bf16[1,6144,256]{2,1,0:T(8,128)(2,1)} %param.30) | copy-start | bytes 9437188
  7.2 8.4 %copy-start.13 = (bf16[16,2,128]{2,1,0:T(2,128)(2,1)S(1)}, bf16[16,2,128]{2,1,0:T(2,128)(2,1)}, u32[]{:S(2)}) copy-start(bf16[16,2,128]{2,1,0:T(2,128)(2,1)} %param.22) | copy-start | bytes 24580
  11.4 4.4 %copy-start.12 = (bf16[16,1,512,128]{3,2,1,0:T(8,128)(2,1)S(1)}, bf16[16,1,512,128]{3,2,1,0:T(8,128)(2,1)}, u32[]{:S(2)}) copy-start(bf16[16,1,512,128]{3,2,1,0:T(8,128)(2,1)} %param.24) | copy-start | bytes 6291460
  15.1 1.4 copy-start.7
  15.2 8.8 %copy-start.10 = (bf16[768]{0:T(1024)(128)(2,1)S(1)}, bf16[768]{0:T(1024)(128)(2,1)}, u32[]{:S(2)}) copy-start(bf16[768]{0:T(1024)(128)(2,1)} %param.26) | copy-start | bytes 4612
  16.6 19.2 %copy-start.6 = (bf16[16,2,768]{2,1,0:T(2,128)(2,1)}, bf16[16,2,768]{2,1,0:T(2,128)(2,1)S(1)}, u32[]{:S(2)}) copy-start(bf16[16,2,768]{2,1,0:T(2,128)(2,1)S(1)} %copy.243) | copy-start | bytes 147460
  17.5 12.4 %all-to-all-start = ((bf16[8,16,768]{2,1,0:T(8,128)(2,1)}), bf16[8,16,768]{2,1,0:T(8,128)(2,1)S(1)}, u32[]{:S(2)}, u32[]{:S(2)}) async-start(bf16[8,16,768]{2,1,0:T(8,128)(2,1)} %bitcast.446), calls=%async_computation | async-start | bytes 393216 | tf_op jit(solution)/shard_map/all_to_all | solution.py:141
  24.0 97.0 %all-gather.4.cloned.1.call-start = ((), (), s32[]{:S(2)}) async-start(), calls=%async_computation.5 | async-start | bytes 6893568 | tf_op jit(solution)/shard_map/all_gather | solution.py:144
  121.9 4.8 %copy-start.4 = (bf16[32,130,768]{2,1,0:T(8,128)(2,1)S(1)}, bf16[32,130,768]{2,1,0:T(8,128)(2,1)}, u32[]{:S(2)}) copy-start(bf16[32,130,768]{2,1,0:T(8,128)(2,1)} %all-gather.4.cloned.1.call-done) | copy-start | bytes 19169284
  126.5 2.1 copy-start.9
  126.8 1.9 copy-start.11
  128.7 1.9 slice-start
  130.6 1.9 copy-start.2
  133.7 36.8 %copy-start.3 = (f32[2,3,16,8,768]{4,2,1,0,3:T(8,128)}, f32[2,3,16,8,768]{4,2,1,0,3:T(8,128)S(1)}, u32[]{:S(2)}) copy-start(f32[2,3,16,8,768]{4,2,1,0,3:T(8,128)S(1)} %fusion.2) | copy-start | bytes 7077892
  133.7 3.6 %copy-start.1 = (bf16[1,256,6144]{1,2,0:T(8,128)(2,1)S(1)}, bf16[1,256,6144]{1,2,0:T(8,128)(2,1)}, u32[]{:S(2)}) copy-start(bf16[1,256,6144]{1,2,0:T(8,128)(2,1)} %copy.236) | copy-start | bytes 9437188
  134.9 37.8 %copy-start.5 = (f32[2,3,16,8,768]{4,2,3,1,0:T(8,128)}, f32[2,3,16,8,768]{4,2,3,1,0:T(8,128)S(1)}, u32[]{:S(2)}) copy-start(f32[2,3,16,8,768]{4,2,3,1,0:T(8,128)S(1)} %fusion.4) | copy-start | bytes 7077892
  138.9 4.8 %collective-permute-start.7 = (bf16[2,3,1,16,768]{4,3,1,0,2:T(8,128)(2,1)S(1)}, bf16[2,3,1,16,768]{4,3,1,0,2:T(8,128)(2,1)S(1)}, u32[]{:S(2)}, u32[]{:S(2)}) collective-permute-start(bf16[2,3,1,16,768]{4,3,1,0,2:T(8,128)(2,1)S(1)} %fusion.61), channel_id=1, source_target_pairs={{0,7},{1,0},{2,1},{3,2},{4,3},{5,4},{6,5},{7,6},{8,15},{9,8},{10,9... | collective-permute-start | bytes 442376 | tf_op jit(solution)/shard_map/ppermute | solution.py:61
  140.3 5.8 %collective-permute-start = (bf16[2,3,1,16,768]{4,3,1,0,2:T(8,128)(2,1)S(1)}, bf16[2,3,1,16,768]{4,3,1,0,2:T(8,128)(2,1)S(1)}, u32[]{:S(2)}, u32[]{:S(2)}) collective-permute-start(bf16[2,3,1,16,768]{4,3,1,0,2:T(8,128)(2,1)S(1)} %fusion.62), channel_id=1, source_target_pairs={{0,1},{1,2},{2,3},{3,4},{4,5},{5,6},{6,7},{7,0},{8,9},{9,10},{10,1... | collective-permute-start | bytes 442376 | tf_op jit(solution)/shard_map/ppermute | solution.py:61
  140.8 16.7 %collective-permute-start.14 = (bf16[4,5,1,16,768]{4,3,0,1,2:T(8,128)(2,1)S(1)}, bf16[4,5,1,16,768]{4,3,0,1,2:T(8,128)(2,1)S(1)}, u32[]{:S(2)}, u32[]{:S(2)}) collective-permute-start(bf16[4,5,1,16,768]{4,3,0,1,2:T(8,128)(2,1)S(1)} %fusion.40), channel_id=1, source_target_pairs={{0,64},{64,128},{128,192},{192,0},{1,65},{65,129},{129,193},{193,1... | collective-permute-start | bytes 1474568 | tf_op jit(solution)/shard_map/ppermute | solution.py:61
  140.9 16.7 %collective-permute-start.17 = (bf16[4,5,1,16,768]{4,3,0,1,2:T(8,128)(2,1)S(1)}, bf16[4,5,1,16,768]{4,3,0,1,2:T(8,128)(2,1)S(1)}, u32[]{:S(2)}, u32[]{:S(2)}) collective-permute-start(bf16[4,5,1,16,768]{4,3,0,1,2:T(8,128)(2,1)S(1)} %fusion.41), channel_id=1, source_target_pairs={{0,192},{64,0},{128,64},{192,128},{1,193},{65,1},{129,65},{193,129... | collective-permute-start | bytes 1474568 | tf_op jit(solution)/shard_map/ppermute | solution.py:61
  143.7 4.5 %collective-permute-start.8 = (bf16[2,3,1,16,768]{4,3,1,0,2:T(8,128)(2,1)S(1)}, bf16[2,3,1,16,768]{4,3,1,0,2:T(8,128)(2,1)S(1)}, u32[]{:S(2)}, u32[]{:S(2)}) collective-permute-start(bf16[2,3,1,16,768]{4,3,1,0,2:T(8,128)(2,1)S(1)} %fusion.55), channel_id=1, source_target_pairs={{0,7},{1,0},{2,1},{3,2},{4,3},{5,4},{6,5},{7,6},{8,15},{9,8},{10,9... | collective-permute-start | bytes 442376 | tf_op jit(solution)/shard_map/ppermute | solution.py:61
  146.1 5.6 %collective-permute-start.1 = (bf16[2,3,1,16,768]{4,3,1,0,2:T(8,128)(2,1)S(1)}, bf16[2,3,1,16,768]{4,3,1,0,2:T(8,128)(2,1)S(1)}, u32[]{:S(2)}, u32[]{:S(2)}) collective-permute-start(bf16[2,3,1,16,768]{4,3,1,0,2:T(8,128)(2,1)S(1)} %fusion.48), channel_id=1, source_target_pairs={{0,1},{1,2},{2,3},{3,4},{4,5},{5,6},{6,7},{7,0},{8,9},{9,10},{10,1... | collective-permute-start | bytes 442376 | tf_op jit(solution)/shard_map/ppermute | solution.py:61
  148.2 5.6 %collective-permute-start.9 = (bf16[2,3,1,16,768]{4,3,1,0,2:T(8,128)(2,1)S(1)}, bf16[2,3,1,16,768]{4,3,1,0,2:T(8,128)(2,1)S(1)}, u32[]{:S(2)}, u32[]{:S(2)}) collective-permute-start(bf16[2,3,1,16,768]{4,3,1,0,2:T(8,128)(2,1)S(1)} %fusion.54), channel_id=1, source_target_pairs={{0,7},{1,0},{2,1},{3,2},{4,3},{5,4},{6,5},{7,6},{8,15},{9,8},{10,9... | collective-permute-start | bytes 442376 | tf_op jit(solution)/shard_map/ppermute | solution.py:61
  151.7 5.6 %collective-permute-start.2 = (bf16[2,3,1,16,768]{4,3,1,0,2:T(8,128)(2,1)S(1)}, bf16[2,3,1,16,768]{4,3,1,0,2:T(8,128)(2,1)S(1)}, u32[]{:S(2)}, u32[]{:S(2)}) collective-permute-start(bf16[2,3,1,16,768]{4,3,1,0,2:T(8,128)(2,1)S(1)} %fusion.47), channel_id=1, source_target_pairs={{0,1},{1,2},{2,3},{3,4},{4,5},{5,6},{6,7},{7,0},{8,9},{9,10},{10,1... | collective-permute-start | bytes 442376 | tf_op jit(solution)/shard_map/ppermute | solution.py:61
  153.8 6.7 %collective-permute-start.10 = (bf16[2,3,1,16,768]{4,3,1,0,2:T(8,128)(2,1)S(1)}, bf16[2,3,1,16,768]{4,3,1,0,2:T(8,128)(2,1)S(1)}, u32[]{:S(2)}, u32[]{:S(2)}) collective-permute-start(bf16[2,3,1,16,768]{4,3,1,0,2:T(8,128)(2,1)S(1)} %fusion.53), channel_id=1, source_target_pairs={{0,7},{1,0},{2,1},{3,2},{4,3},{5,4},{6,5},{7,6},{8,15},{9,8},{10,9... | collective-permute-start | bytes 442376 | tf_op jit(solution)/shard_map/ppermute | solution.py:61
  157.3 6.0 %collective-permute-start.3 = (bf16[2,3,1,16,768]{4,3,1,0,2:T(8,128)(2,1)S(1)}, bf16[2,3,1,16,768]{4,3,1,0,2:T(8,128)(2,1)S(1)}, u32[]{:S(2)}, u32[]{:S(2)}) collective-permute-start(bf16[2,3,1,16,768]{4,3,1,0,2:T(8,128)(2,1)S(1)} %fusion.46), channel_id=1, source_target_pairs={{0,1},{1,2},{2,3},{3,4},{4,5},{5,6},{6,7},{7,0},{8,9},{9,10},{10,1... | collective-permute-start | bytes 442376 | tf_op jit(solution)/shard_map/ppermute | solution.py:61
  157.6 9.5 %collective-permute-start.15 = (bf16[4,5,1,16,768]{4,3,0,1,2:T(8,128)(2,1)S(1)}, bf16[4,5,1,16,768]{4,3,0,1,2:T(8,128)(2,1)S(1)}, u32[]{:S(2)}, u32[]{:S(2)}) collective-permute-start(bf16[4,5,1,16,768]{4,3,0,1,2:T(8,128)(2,1)S(1)} %fusion.39), channel_id=1, source_target_pairs={{0,64},{64,128},{128,192},{192,0},{1,65},{65,129},{129,193},{193,1... | collective-permute-start | bytes 1474568 | tf_op jit(solution)/shard_map/ppermute | solution.py:61
  157.8 9.4 %collective-permute-start.18 = (bf16[4,5,1,16,768]{4,3,0,1,2:T(8,128)(2,1)S(1)}, bf16[4,5,1,16,768]{4,3,0,1,2:T(8,128)(2,1)S(1)}, u32[]{:S(2)}, u32[]{:S(2)}) collective-permute-start(bf16[4,5,1,16,768]{4,3,0,1,2:T(8,128)(2,1)S(1)} %fusion.36), channel_id=1, source_target_pairs={{0,192},{64,0},{128,64},{192,128},{1,193},{65,1},{129,65},{193,129... | collective-permute-start | bytes 1474568 | tf_op jit(solution)/shard_map/ppermute | solution.py:61
  160.6 9.8 %collective-permute-start.11 = (bf16[2,3,1,16,768]{4,3,1,0,2:T(8,128)(2,1)S(1)}, bf16[2,3,1,16,768]{4,3,1,0,2:T(8,128)(2,1)S(1)}, u32[]{:S(2)}, u32[]{:S(2)}) collective-permute-start(bf16[2,3,1,16,768]{4,3,1,0,2:T(8,128)(2,1)S(1)} %fusion.52), channel_id=1, source_target_pairs={{0,7},{1,0},{2,1},{3,2},{4,3},{5,4},{6,5},{7,6},{8,15},{9,8},{10,9... | collective-permute-start | bytes 442376 | tf_op jit(solution)/shard_map/ppermute | solution.py:61
  163.4 9.3 %collective-permute-start.4 = (bf16[2,3,1,16,768]{4,3,1,0,2:T(8,128)(2,1)S(1)}, bf16[2,3,1,16,768]{4,3,1,0,2:T(8,128)(2,1)S(1)}, u32[]{:S(2)}, u32[]{:S(2)}) collective-permute-start(bf16[2,3,1,16,768]{4,3,1,0,2:T(8,128)(2,1)S(1)} %fusion.45), channel_id=1, source_target_pairs={{0,1},{1,2},{2,3},{3,4},{4,5},{5,6},{6,7},{7,0},{8,9},{9,10},{10,1... | collective-permute-start | bytes 442376 | tf_op jit(solution)/shard_map/ppermute | solution.py:61
  167.2 9.9 %collective-permute-start.16 = (bf16[4,5,1,16,768]{4,3,0,1,2:T(8,128)(2,1)S(1)}, bf16[4,5,1,16,768]{4,3,0,1,2:T(8,128)(2,1)S(1)}, u32[]{:S(2)}, u32[]{:S(2)}) collective-permute-start(bf16[4,5,1,16,768]{4,3,0,1,2:T(8,128)(2,1)S(1)} %fusion.38), channel_id=1, source_target_pairs={{0,64},{64,128},{128,192},{192,0},{1,65},{65,129},{129,193},{193,1... | collective-permute-start | bytes 1474568 | tf_op jit(solution)/shard_map/ppermute | solution.py:61
  167.4 9.8 %collective-permute-start.19 = (bf16[4,5,1,16,768]{4,3,0,1,2:T(8,128)(2,1)S(1)}, bf16[4,5,1,16,768]{4,3,0,1,2:T(8,128)(2,1)S(1)}, u32[]{:S(2)}, u32[]{:S(2)}) collective-permute-start(bf16[4,5,1,16,768]{4,3,0,1,2:T(8,128)(2,1)S(1)} %fusion.35), channel_id=1, source_target_pairs={{0,192},{64,0},{128,64},{192,128},{1,193},{65,1},{129,65},{193,129... | collective-permute-start | bytes 1474568 | tf_op jit(solution)/shard_map/ppermute | solution.py:61
  170.5 13.0 %collective-permute-start.12 = (bf16[2,3,1,16,768]{4,3,1,0,2:T(8,128)(2,1)S(1)}, bf16[2,3,1,16,768]{4,3,1,0,2:T(8,128)(2,1)S(1)}, u32[]{:S(2)}, u32[]{:S(2)}) collective-permute-start(bf16[2,3,1,16,768]{4,3,1,0,2:T(8,128)(2,1)S(1)} %fusion.51), channel_id=1, source_target_pairs={{0,7},{1,0},{2,1},{3,2},{4,3},{5,4},{6,5},{7,6},{8,15},{9,8},{10,9... | collective-permute-start | bytes 442376 | tf_op jit(solution)/shard_map/ppermute | solution.py:61
  173.4 13.8 %collective-permute-start.5 = (bf16[2,3,1,16,768]{4,3,1,0,2:T(8,128)(2,1)}, bf16[2,3,1,16,768]{4,3,1,0,2:T(8,128)(2,1)}, u32[]{:S(2)}, u32[]{:S(2)}) collective-permute-start(bf16[2,3,1,16,768]{4,3,1,0,2:T(8,128)(2,1)} %fusion.44), channel_id=1, source_target_pairs={{0,1},{1,2},{2,3},{3,4},{4,5},{5,6},{6,7},{7,0},{8,9},{9,10},{10,1... | collective-permute-start | bytes 442376 | tf_op jit(solution)/shard_map/ppermute | solution.py:61
  178.5 29.7 %copy-start.8 = (s32[16,2,2]{0,2,1:T(2,128)S(1)}, s32[16,2,2]{0,2,1:T(2,128)}, u32[]{:S(2)}) copy-start(s32[16,2,2]{0,2,1:T(2,128)} %param.28) | copy-start | bytes 772
  178.5 29.7 %all-to-all-start.1 = ((bf16[8,5,1,16,768]{4,3,1,2,0:T(8,128)(2,1)}), bf16[8,5,1,16,768]{4,3,1,2,0:T(8,128)(2,1)}, u32[]{:S(2)}, u32[]{:S(2)}) async-start(bf16[8,5,1,16,768]{4,3,1,2,0:T(8,128)(2,1)} %copy.239), calls=%async_computation.2 | async-start | bytes 1966080 | tf_op jit(solution)/shard_map/all_to_all | solution.py:78
  183.4 51.4 %reduce-scatter.2.cloned.1.call-start = ((), (), s32[]{:S(2)}) async-start(), calls=%async_computation.4 | async-start | bytes 368640 | tf_op jit(solution)/shard_map/reduce_scatter | solution.py:197
  184.5 18.4 %collective-permute-start.13 = (bf16[2,3,1,16,768]{4,3,1,0,2:T(8,128)(2,1)S(1)}, bf16[2,3,1,16,768]{4,3,1,0,2:T(8,128)(2,1)S(1)}, u32[]{:S(2)}, u32[]{:S(2)}) collective-permute-start(bf16[2,3,1,16,768]{4,3,1,0,2:T(8,128)(2,1)S(1)} %fusion.50), channel_id=1, source_target_pairs={{0,7},{1,0},{2,1},{3,2},{4,3},{5,4},{6,5},{7,6},{8,15},{9,8},{10,9... | collective-permute-start | bytes 442376 | tf_op jit(solution)/shard_map/ppermute | solution.py:61
  188.2 17.6 %collective-permute-start.6 = (bf16[2,3,1,16,768]{4,3,1,0,2:T(8,128)(2,1)S(1)}, bf16[2,3,1,16,768]{4,3,1,0,2:T(8,128)(2,1)S(1)}, u32[]{:S(2)}, u32[]{:S(2)}) collective-permute-start(bf16[2,3,1,16,768]{4,3,1,0,2:T(8,128)(2,1)S(1)} %fusion.43), channel_id=1, source_target_pairs={{0,1},{1,2},{2,3},{3,4},{4,5},{5,6},{6,7},{7,0},{8,9},{9,10},{10,1... | collective-permute-start | bytes 442376 | tf_op jit(solution)/shard_map/ppermute | solution.py:61
  236.4 13.1 %all-to-all-start.2 = ((bf16[8,1,16,768]{3,2,1,0:T(8,128)(2,1)}), bf16[8,1,16,768]{3,2,1,0:T(8,128)(2,1)S(1)}, u32[]{:S(2)}, u32[]{:S(2)}) async-start(bf16[8,1,16,768]{3,2,1,0:T(8,128)(2,1)} %pad_maximum_fusion.2), calls=%async_computation.3 | async-start | bytes 393216 | tf_op jit(solution)/shard_map/all_to_all | solution.py:201
Sparse Core Ops, SparseCore 0:
  30.8 90.1 all-gather.3
  207.8 27.0 reduce-scatter.1

commit v9 on v8

--- a/solution.py
+++ b/solution.py
@@ -173,7 +173,7 @@
     up_sums = expert_in(w_up)
     hidden = (jax.nn.silu(gate_sums) * up_sums).astype(jnp.bfloat16)
     down_split = w_down.reshape(local_experts, hidden_local, tensor_count, slice_width)
-    owner_half = (owner_count * 3) // 8
+    owner_half = (owner_count * 5) // 8
     group_half = group_count // 2
     tensor_half = tensor_count // 2
 

time: 258 us -> 249 us (0.965)
  waiting for transfers between devices: 144 us -> 137 us
    ppermute x20, waiting for transfers between devices: 27.8 us -> 17 us  [ring_reduce_scatter(): arrived = lax.ppermute(total.astype(jnp.bfloat16), axis, pairs)]
    all_to_all x1, waiting for transfers between devices: 0.01 us -> 7.42 us  [exchange_sum(): moved = lax.all_to_all(parts.astype(jnp.bfloat16), axis, 0, 0, tiled=True)]
    reduce_scatter x1, waiting for transfers between devices: 25.2 us -> 21.8 us  [per_device(): lax.psum_scatter(z_first.astype(jnp.bfloat16), 'grp', scatter_dimension=0...]
  transfers between devices with their start and end apart: 25 -> 25, of which waited for: 10 -> 15; matrix products, arithmetic and copies ran while one was open for 8% -> 8% of each run, Pallas kernels for 0% -> 0%
where the time goes in v9:
time: 249 us; the launch traced here: 248 us
  waiting for transfers between devices  137 us (55%)
  starting transfers between devices  46.7 us (19%)
  local copies, waits for them, and re-layouts  17.7 us (7%)
  other arithmetic  17.7 us (7%)
  between operations  15.1 us (6%)
  matrix products  14.4 us (6%)
    all_gather x1, waiting for transfers between devices, per_device(): gathered = lax.all_gather(payload[None], ('grp', 'tp'), axis=0, tiled=True)  80.9 us
    ppermute x20, starting transfers between devices, ring_reduce_scatter(): arrived = lax.ppermute(total.astype(jnp.bfloat16), axis, pairs)  28.2 us
    reduce_scatter x1, waiting for transfers between devices, per_device(): lax.psum_scatter(z_first.astype(jnp.bfloat16), 'grp', scatter_dimension=0...  21.8 us
    ppermute x20, waiting for transfers between devices, ring_reduce_scatter(): arrived = lax.ppermute(total.astype(jnp.bfloat16), axis, pairs)  17 us
    unnamed x36, local copies, waits for them, and re-layouts  13.2 us
    all_to_all x1, waiting for transfers between devices, exchange_sum(): moved = lax.all_to_all(parts.astype(jnp.bfloat16), axis, 0, 0, tiled=True)  7.42 us
    all_to_all x1, starting transfers between devices, per_device(): lax.all_to_all(summed.astype(jnp.bfloat16), 'ex', split_axis=0, concat_ax...  7.29 us
    all_to_all x1, starting transfers between devices, per_device(): lax.all_to_all(outgoing, 'ex', split_axis=0, concat_axis=0, tiled=True)  6.49 us
  transfers between devices with their start and end apart: 25, of which 15 were waited for; matrix products, arithmetic and copies ran while one was open for 8% of the time, Pallas kernels for 0%

profile of v9, /device:TPU:1, one launch (start us, length us, event | category | flops | bytes accessed | tf_op | source)
XLA Modules:
  0.0 248.4 jit_solution(16018808455822926272)
XLA Ops:
  7.2 0.8 broadcast_multiply_fusion
  8.0 0.9 copy.210
  10.6 0.9 reshape.679
  11.4 1.3 fusion.87
  12.7 2.3 fusion.86
  16.6 0.9 convolution_convert_fusion
  17.5 6.5 %all-to-all-start = ((bf16[8,16,768]{2,1,0:T(8,128)(2,1)}), bf16[8,16,768]{2,1,0:T(8,128)(2,1)S(1)}, u32[]{:S(2)}, u32[]{:S(2)}) async-start(bf16[8,16,768]{2,1,0:T(8,128)(2,1)} %bitcast.446), calls=%async_computation | async-start | bytes 393216 | tf_op jit(solution)/shard_map/all_to_all | solution.py:141
  24.1 1.2 fusion.67
  26.1 3.9 %all-to-all-done = bf16[8,16,768]{2,1,0:T(8,128)(2,1)S(1)} async-done(((bf16[8,16,768]{2,1,0:T(8,128)(2,1)}), bf16[8,16,768]{2,1,0:T(8,128)(2,1)S(1)}, u32[]{:S(2)}, u32[]{:S(2)}) %all-to-all-start) | async-done | bytes 196640 | tf_op jit(solution)/shard_map/all_to_all | solution.py:141
  31.0 4.6 %copy.236 = bf16[1,256,6144]{1,2,0:T(8,128)(2,1)} copy(bf16[1,256,6144]{2,1,0:T(8,128)(2,1)} %param.31) | data formatting | bytes 6291456 | tf_op args[12]
  35.7 4.5 %copy.278 = bf16[32,8,8,768]{3,2,1,0:T(8,128)(2,1)} copy(bf16[32,8,8,768]{3,1,2,0:T(8,128)(2,1)} %bitcast.436) | data formatting | bytes 6291456
  40.2 80.9 %all-gather.4.cloned.1.call-done = bf16[32,130,768]{2,1,0:T(8,128)(2,1)} async-done(((bf16[1,130,768]{2,1,0:T(8,128)(2,1)}), bf16[32,130,768]{2,1,0:T(8,128)(2,1)}) %all-gather.4.cloned.1.call-update) | async-done | bytes 6389776 | tf_op jit(solution)/shard_map/all_gather | solution.py:144
  121.0 0.9 slice_convert_fusion
  122.0 4.5 %multiply_reduce_fusion = f32[32,130]{1,0:T(8,128)S(1)} fusion(bf16[32,130,768]{2,1,0:T(8,128)(2,1)} %all-gather.4.cloned.1.call-done), kind=kLoop, calls=%fused_computation | loop fusion | flops 9580480 | bytes 6406400 | tf_op jit(solution)/shard_map/reduce_sum | solution.py:163
  126.8 1.9 fusion.13
  128.7 1.9 fusion.12
  130.9 1.6 copy-done.3
  134.4 1.3 fusion.2
  135.7 1.3 fusion.4
  137.1 1.4 collective-permute-start.7
  139.1 2.7 %collective-permute-start.17 = (bf16[4,3,1,16,768]{4,3,0,1,2:T(8,128)(2,1)S(1)}, bf16[4,3,1,16,768]{4,3,0,1,2:T(8,128)(2,1)S(1)}, u32[]{:S(2)}, u32[]{:S(2)}) collective-permute-start(bf16[4,3,1,16,768]{4,3,0,1,2:T(8,128)(2,1)S(1)} %fusion.56), channel_id=1, source_target_pairs={{0,192},{64,0},{128,64},{192,128},{1,193},{65,1},{129,65},{193,129... | collective-permute-start | bytes 884744 | tf_op jit(solution)/shard_map/ppermute | solution.py:61
  141.8 1.9 collective-permute-done.7
  143.8 2.1 collective-permute-start.8
  146.9 2.9 %collective-permute-start.18 = (bf16[4,3,1,16,768]{4,3,0,1,2:T(8,128)(2,1)S(1)}, bf16[4,3,1,16,768]{4,3,0,1,2:T(8,128)(2,1)S(1)}, u32[]{:S(2)}, u32[]{:S(2)}) collective-permute-start(bf16[4,3,1,16,768]{4,3,0,1,2:T(8,128)(2,1)S(1)} %fusion.36), channel_id=1, source_target_pairs={{0,192},{64,0},{128,64},{192,128},{1,193},{65,1},{129,65},{193,129... | collective-permute-start | bytes 884744 | tf_op jit(solution)/shard_map/ppermute | solution.py:61
  149.9 2.4 collective-permute-start.9
  152.4 1.6 collective-permute-done.15
  154.2 1.2 collective-permute-done.9
  155.5 3.5 %collective-permute-start.10 = (bf16[2,5,1,16,768]{4,3,1,0,2:T(8,128)(2,1)S(1)}, bf16[2,5,1,16,768]{4,3,1,0,2:T(8,128)(2,1)S(1)}, u32[]{:S(2)}, u32[]{:S(2)}) collective-permute-start(bf16[2,5,1,16,768]{4,3,1,0,2:T(8,128)(2,1)S(1)} %fusion.50), channel_id=1, source_target_pairs={{0,7},{1,0},{2,1},{3,2},{4,3},{5,4},{6,5},{7,6},{8,15},{9,8},{10,9... | collective-permute-start | bytes 737288 | tf_op jit(solution)/shard_map/ppermute | solution.py:61
  159.2 2.0 collective-permute-start.19
  161.2 0.9 collective-permute-done.10
  162.2 3.5 %collective-permute-start.11 = (bf16[2,5,1,16,768]{4,3,1,0,2:T(8,128)(2,1)S(1)}, bf16[2,5,1,16,768]{4,3,1,0,2:T(8,128)(2,1)S(1)}, u32[]{:S(2)}, u32[]{:S(2)}) collective-permute-start(bf16[2,5,1,16,768]{4,3,1,0,2:T(8,128)(2,1)S(1)} %fusion.49), channel_id=1, source_target_pairs={{0,7},{1,0},{2,1},{3,2},{4,3},{5,4},{6,5},{7,6},{8,15},{9,8},{10,9... | collective-permute-start | bytes 737288 | tf_op jit(solution)/shard_map/ppermute | solution.py:61
  166.1 3.3 %collective-permute-done.11 = bf16[2,5,1,16,768]{4,3,1,0,2:T(8,128)(2,1)S(1)} collective-permute-done((bf16[2,5,1,16,768]{4,3,1,0,2:T(8,128)(2,1)S(1)}, bf16[2,5,1,16,768]{4,3,1,0,2:T(8,128)(2,1)S(1)}, u32[]{:S(2)}, u32[]{:S(2)}) %collective-permute-start.11) | collective-permute-done | bytes 245792 | tf_op jit(solution)/shard_map/ppermute | solution.py:61
  169.5 3.2 %collective-permute-start.12 = (bf16[2,5,1,16,768]{4,3,1,0,2:T(8,128)(2,1)S(1)}, bf16[2,5,1,16,768]{4,3,1,0,2:T(8,128)(2,1)S(1)}, u32[]{:S(2)}, u32[]{:S(2)}) collective-permute-start(bf16[2,5,1,16,768]{4,3,1,0,2:T(8,128)(2,1)S(1)} %fusion.48), channel_id=1, source_target_pairs={{0,7},{1,0},{2,1},{3,2},{4,3},{5,4},{6,5},{7,6},{8,15},{9,8},{10,9... | collective-permute-start | bytes 737288 | tf_op jit(solution)/shard_map/ppermute | solution.py:61
  173.3 4.3 %collective-permute-done.12 = bf16[2,5,1,16,768]{4,3,1,0,2:T(8,128)(2,1)S(1)} collective-permute-done((bf16[2,5,1,16,768]{4,3,1,0,2:T(8,128)(2,1)S(1)}, bf16[2,5,1,16,768]{4,3,1,0,2:T(8,128)(2,1)S(1)}, u32[]{:S(2)}, u32[]{:S(2)}) %collective-permute-start.12) | collective-permute-done | bytes 245792 | tf_op jit(solution)/shard_map/ppermute | solution.py:61
  178.4 3.1 %collective-permute-start.13 = (bf16[2,5,1,16,768]{4,3,1,0,2:T(8,128)(2,1)}, bf16[2,5,1,16,768]{4,3,1,0,2:T(8,128)(2,1)S(1)}, u32[]{:S(2)}, u32[]{:S(2)}) collective-permute-start(bf16[2,5,1,16,768]{4,3,1,0,2:T(8,128)(2,1)} %fusion.47), channel_id=1, source_target_pairs={{0,7},{1,0},{2,1},{3,2},{4,3},{5,4},{6,5},{7,6},{8,15},{9,8},{10,9... | collective-permute-start | bytes 737288 | tf_op jit(solution)/shard_map/ppermute | solution.py:61
  182.5 0.9 copy.239
  183.4 4.7 %all-to-all-start.1 = ((bf16[8,3,1,16,768]{4,3,1,2,0:T(8,128)(2,1)}), bf16[8,3,1,16,768]{4,3,1,2,0:T(8,128)(2,1)}, u32[]{:S(2)}, u32[]{:S(2)}) async-start(bf16[8,3,1,16,768]{4,3,1,2,0:T(8,128)(2,1)} %copy.239), calls=%async_computation.2 | async-start | bytes 1179648 | tf_op jit(solution)/shard_map/all_to_all | solution.py:78
  188.2 1.1 fusion.46
  189.3 2.4 collective-permute-done.6
  191.6 1.1 fusion.53
  192.8 0.8 pad_maximum_fusion.1
  193.7 1.1 slice.123
  195.5 7.4 %all-to-all-done.1 = bf16[8,3,1,16,768]{4,3,1,2,0:T(8,128)(2,1)} async-done(((bf16[8,3,1,16,768]{4,3,1,2,0:T(8,128)(2,1)}), bf16[8,3,1,16,768]{4,3,1,2,0:T(8,128)(2,1)}, u32[]{:S(2)}, u32[]{:S(2)}) %all-to-all-start.1) | async-done | bytes 589856 | tf_op jit(solution)/shard_map/all_to_all | solution.py:78
  202.9 1.1 reduce.14
  204.1 21.8 %reduce-scatter.2.cloned.1.call-done = bf16[1,5,1,16,768]{4,3,1,0,2:T(8,128)(2,1)} async-done(((bf16[4,5,1,16,768]{4,3,1,0,2:T(8,128)(2,1)}), bf16[1,5,1,16,768]{4,3,1,0,2:T(8,128)(2,1)}) %reduce-scatter.2.cloned.1.call-update) | async-done | bytes 122896 | tf_op jit(solution)/shard_map/reduce_scatter | solution.py:197
  225.9 1.6 maximum_bitcast_fusion.1
  227.5 7.3 %all-to-all-start.2 = ((bf16[8,1,16,768]{3,2,1,0:T(8,128)(2,1)}), bf16[8,1,16,768]{3,2,1,0:T(8,128)(2,1)S(1)}, u32[]{:S(2)}, u32[]{:S(2)}) async-start(bf16[8,1,16,768]{3,2,1,0:T(8,128)(2,1)} %maximum_bitcast_fusion.1), calls=%async_computation.3 | async-start | bytes 393216 | tf_op jit(solution)/shard_map/all_to_all | solution.py:201
  234.8 5.8 %all-to-all-done.2 = bf16[8,1,16,768]{3,2,1,0:T(8,128)(2,1)S(1)} async-done(((bf16[8,1,16,768]{3,2,1,0:T(8,128)(2,1)}), bf16[8,1,16,768]{3,2,1,0:T(8,128)(2,1)S(1)}, u32[]{:S(2)}, u32[]{:S(2)}) %all-to-all-start.2) | async-done | bytes 196640 | tf_op jit(solution)/shard_map/all_to_all | solution.py:201
  (134 shorter events, 13.9 us)
Async XLA Ops:
  7.2 119.4 %copy-start = (bf16[1,6144,256]{2,1,0:T(8,128)(2,1)S(1)}, bf16[1,6144,256]{2,1,0:T(8,128)(2,1)}, u32[]{:S(2)}) copy-start(bf16[1,6144,256]{2,1,0:T(8,128)(2,1)} %param.30) | copy-start | bytes 9437188
  7.2 8.4 %copy-start.13 = (bf16[16,2,128]{2,1,0:T(2,128)(2,1)S(1)}, bf16[16,2,128]{2,1,0:T(2,128)(2,1)}, u32[]{:S(2)}) copy-start(bf16[16,2,128]{2,1,0:T(2,128)(2,1)} %param.22) | copy-start | bytes 24580
  11.4 4.4 %copy-start.12 = (bf16[16,1,512,128]{3,2,1,0:T(8,128)(2,1)S(1)}, bf16[16,1,512,128]{3,2,1,0:T(8,128)(2,1)}, u32[]{:S(2)}) copy-start(bf16[16,1,512,128]{3,2,1,0:T(8,128)(2,1)} %param.24) | copy-start | bytes 6291460
  15.1 1.4 copy-start.7
  15.2 8.8 %copy-start.10 = (bf16[768]{0:T(1024)(128)(2,1)S(1)}, bf16[768]{0:T(1024)(128)(2,1)}, u32[]{:S(2)}) copy-start(bf16[768]{0:T(1024)(128)(2,1)} %param.26) | copy-start | bytes 4612
  16.6 19.1 %copy-start.6 = (bf16[16,2,768]{2,1,0:T(2,128)(2,1)}, bf16[16,2,768]{2,1,0:T(2,128)(2,1)S(1)}, u32[]{:S(2)}) copy-start(bf16[16,2,768]{2,1,0:T(2,128)(2,1)S(1)} %copy.243) | copy-start | bytes 147460
  17.5 12.4 %all-to-all-start = ((bf16[8,16,768]{2,1,0:T(8,128)(2,1)}), bf16[8,16,768]{2,1,0:T(8,128)(2,1)S(1)}, u32[]{:S(2)}, u32[]{:S(2)}) async-start(bf16[8,16,768]{2,1,0:T(8,128)(2,1)} %bitcast.446), calls=%async_computation | async-start | bytes 393216 | tf_op jit(solution)/shard_map/all_to_all | solution.py:141
  24.0 97.0 %all-gather.4.cloned.1.call-start = ((), (), s32[]{:S(2)}) async-start(), calls=%async_computation.5 | async-start | bytes 6893568 | tf_op jit(solution)/shard_map/all_gather | solution.py:144
  121.9 4.8 %copy-start.4 = (bf16[32,130,768]{2,1,0:T(8,128)(2,1)S(1)}, bf16[32,130,768]{2,1,0:T(8,128)(2,1)}, u32[]{:S(2)}) copy-start(bf16[32,130,768]{2,1,0:T(8,128)(2,1)} %all-gather.4.cloned.1.call-done) | copy-start | bytes 19169284
  126.5 2.1 copy-start.9
  126.8 1.9 copy-start.11
  128.7 1.9 slice-start
  130.6 1.9 copy-start.3
  132.5 1.9 copy-start.2
  135.7 42.0 %copy-start.1 = (f32[2,5,16,8,768]{4,2,1,0,3:T(8,128)}, f32[2,5,16,8,768]{4,2,1,0,3:T(8,128)S(1)}, u32[]{:S(2)}) copy-start(f32[2,5,16,8,768]{4,2,1,0,3:T(8,128)S(1)} %fusion.2) | copy-start | bytes 11796484
  137.0 44.7 %copy-start.5 = (f32[2,5,16,8,768]{4,2,3,1,0:T(8,128)}, f32[2,5,16,8,768]{4,2,3,1,0:T(8,128)S(1)}, u32[]{:S(2)}) copy-start(f32[2,5,16,8,768]{4,2,3,1,0:T(8,128)S(1)} %fusion.4) | copy-start | bytes 11796484
  137.1 6.7 %collective-permute-start.7 = (bf16[2,5,1,16,768]{4,3,1,0,2:T(8,128)(2,1)S(1)}, bf16[2,5,1,16,768]{4,3,1,0,2:T(8,128)(2,1)S(1)}, u32[]{:S(2)}, u32[]{:S(2)}) collective-permute-start(bf16[2,5,1,16,768]{4,3,1,0,2:T(8,128)(2,1)S(1)} %fusion.61), channel_id=1, source_target_pairs={{0,7},{1,0},{2,1},{3,2},{4,3},{5,4},{6,5},{7,6},{8,15},{9,8},{10,9... | collective-permute-start | bytes 737288 | tf_op jit(solution)/shard_map/ppermute | solution.py:61
  138.5 8.2 %collective-permute-start.14 = (bf16[4,3,1,16,768]{4,3,0,1,2:T(8,128)(2,1)S(1)}, bf16[4,3,1,16,768]{4,3,0,1,2:T(8,128)(2,1)S(1)}, u32[]{:S(2)}, u32[]{:S(2)}) collective-permute-start(bf16[4,3,1,16,768]{4,3,0,1,2:T(8,128)(2,1)S(1)} %fusion.55), channel_id=1, source_target_pairs={{0,64},{64,128},{128,192},{192,0},{1,65},{65,129},{129,193},{193,1... | collective-permute-start | bytes 884744 | tf_op jit(solution)/shard_map/ppermute | solution.py:61
  138.6 7.3 %collective-permute-start = (bf16[2,5,1,16,768]{4,3,1,0,2:T(8,128)(2,1)S(1)}, bf16[2,5,1,16,768]{4,3,1,0,2:T(8,128)(2,1)S(1)}, u32[]{:S(2)}, u32[]{:S(2)}) collective-permute-start(bf16[2,5,1,16,768]{4,3,1,0,2:T(8,128)(2,1)S(1)} %fusion.62), channel_id=1, source_target_pairs={{0,1},{1,2},{2,3},{3,4},{4,5},{5,6},{6,7},{7,0},{8,9},{9,10},{10,1... | collective-permute-start | bytes 737288 | tf_op jit(solution)/shard_map/ppermute | solution.py:61
  139.1 7.7 %collective-permute-start.17 = (bf16[4,3,1,16,768]{4,3,0,1,2:T(8,128)(2,1)S(1)}, bf16[4,3,1,16,768]{4,3,0,1,2:T(8,128)(2,1)S(1)}, u32[]{:S(2)}, u32[]{:S(2)}) collective-permute-start(bf16[4,3,1,16,768]{4,3,0,1,2:T(8,128)(2,1)S(1)} %fusion.56), channel_id=1, source_target_pairs={{0,192},{64,0},{128,64},{192,128},{1,193},{65,1},{129,65},{193,129... | collective-permute-start | bytes 884744 | tf_op jit(solution)/shard_map/ppermute | solution.py:61
  143.8 6.0 %collective-permute-start.8 = (bf16[2,5,1,16,768]{4,3,1,0,2:T(8,128)(2,1)S(1)}, bf16[2,5,1,16,768]{4,3,1,0,2:T(8,128)(2,1)S(1)}, u32[]{:S(2)}, u32[]{:S(2)}) collective-permute-start(bf16[2,5,1,16,768]{4,3,1,0,2:T(8,128)(2,1)S(1)} %fusion.52), channel_id=1, source_target_pairs={{0,7},{1,0},{2,1},{3,2},{4,3},{5,4},{6,5},{7,6},{8,15},{9,8},{10,9... | collective-permute-start | bytes 737288 | tf_op jit(solution)/shard_map/ppermute | solution.py:61
  145.9 6.3 %collective-permute-start.1 = (bf16[2,5,1,16,768]{4,3,1,0,2:T(8,128)(2,1)S(1)}, bf16[2,5,1,16,768]{4,3,1,0,2:T(8,128)(2,1)S(1)}, u32[]{:S(2)}, u32[]{:S(2)}) collective-permute-start(bf16[2,5,1,16,768]{4,3,1,0,2:T(8,128)(2,1)S(1)} %fusion.45), channel_id=1, source_target_pairs={{0,1},{1,2},{2,3},{3,4},{4,5},{5,6},{6,7},{7,0},{8,9},{9,10},{10,1... | collective-permute-start | bytes 737288 | tf_op jit(solution)/shard_map/ppermute | solution.py:61
  146.7 7.3 %collective-permute-start.15 = (bf16[4,3,1,16,768]{4,3,0,1,2:T(8,128)(2,1)S(1)}, bf16[4,3,1,16,768]{4,3,0,1,2:T(8,128)(2,1)S(1)}, u32[]{:S(2)}, u32[]{:S(2)}) collective-permute-start(bf16[4,3,1,16,768]{4,3,0,1,2:T(8,128)(2,1)S(1)} %fusion.39), channel_id=1, source_target_pairs={{0,64},{64,128},{128,192},{192,0},{1,65},{65,129},{129,193},{193,1... | collective-permute-start | bytes 884744 | tf_op jit(solution)/shard_map/ppermute | solution.py:61
  146.9 12.2 %collective-permute-start.18 = (bf16[4,3,1,16,768]{4,3,0,1,2:T(8,128)(2,1)S(1)}, bf16[4,3,1,16,768]{4,3,0,1,2:T(8,128)(2,1)S(1)}, u32[]{:S(2)}, u32[]{:S(2)}) collective-permute-start(bf16[4,3,1,16,768]{4,3,0,1,2:T(8,128)(2,1)S(1)} %fusion.36), channel_id=1, source_target_pairs={{0,192},{64,0},{128,64},{192,128},{1,193},{65,1},{129,65},{193,129... | collective-permute-start | bytes 884744 | tf_op jit(solution)/shard_map/ppermute | solution.py:61
  149.9 5.6 %collective-permute-start.9 = (bf16[2,5,1,16,768]{4,3,1,0,2:T(8,128)(2,1)S(1)}, bf16[2,5,1,16,768]{4,3,1,0,2:T(8,128)(2,1)S(1)}, u32[]{:S(2)}, u32[]{:S(2)}) collective-permute-start(bf16[2,5,1,16,768]{4,3,1,0,2:T(8,128)(2,1)S(1)} %fusion.51), channel_id=1, source_target_pairs={{0,7},{1,0},{2,1},{3,2},{4,3},{5,4},{6,5},{7,6},{8,15},{9,8},{10,9... | collective-permute-start | bytes 737288 | tf_op jit(solution)/shard_map/ppermute | solution.py:61
  152.3 6.6 %collective-permute-start.2 = (bf16[2,5,1,16,768]{4,3,1,0,2:T(8,128)(2,1)S(1)}, bf16[2,5,1,16,768]{4,3,1,0,2:T(8,128)(2,1)S(1)}, u32[]{:S(2)}, u32[]{:S(2)}) collective-permute-start(bf16[2,5,1,16,768]{4,3,1,0,2:T(8,128)(2,1)S(1)} %fusion.44), channel_id=1, source_target_pairs={{0,1},{1,2},{2,3},{3,4},{4,5},{5,6},{6,7},{7,0},{8,9},{9,10},{10,1... | collective-permute-start | bytes 737288 | tf_op jit(solution)/shard_map/ppermute | solution.py:61
  154.1 12.0 %collective-permute-start.16 = (bf16[4,3,1,16,768]{4,3,0,1,2:T(8,128)(2,1)S(1)}, bf16[4,3,1,16,768]{4,3,0,1,2:T(8,128)(2,1)S(1)}, u32[]{:S(2)}, u32[]{:S(2)}) collective-permute-start(bf16[4,3,1,16,768]{4,3,0,1,2:T(8,128)(2,1)S(1)} %fusion.38), channel_id=1, source_target_pairs={{0,64},{64,128},{128,192},{192,0},{1,65},{65,129},{129,193},{193,1... | collective-permute-start | bytes 884744 | tf_op jit(solution)/shard_map/ppermute | solution.py:61
  155.5 6.6 %collective-permute-start.10 = (bf16[2,5,1,16,768]{4,3,1,0,2:T(8,128)(2,1)S(1)}, bf16[2,5,1,16,768]{4,3,1,0,2:T(8,128)(2,1)S(1)}, u32[]{:S(2)}, u32[]{:S(2)}) collective-permute-start(bf16[2,5,1,16,768]{4,3,1,0,2:T(8,128)(2,1)S(1)} %fusion.50), channel_id=1, source_target_pairs={{0,7},{1,0},{2,1},{3,2},{4,3},{5,4},{6,5},{7,6},{8,15},{9,8},{10,9... | collective-permute-start | bytes 737288 | tf_op jit(solution)/shard_map/ppermute | solution.py:61
  159.0 6.6 %collective-permute-start.3 = (bf16[2,5,1,16,768]{4,3,1,0,2:T(8,128)(2,1)S(1)}, bf16[2,5,1,16,768]{4,3,1,0,2:T(8,128)(2,1)S(1)}, u32[]{:S(2)}, u32[]{:S(2)}) collective-permute-start(bf16[2,5,1,16,768]{4,3,1,0,2:T(8,128)(2,1)S(1)} %fusion.43), channel_id=1, source_target_pairs={{0,1},{1,2},{2,3},{3,4},{4,5},{5,6},{6,7},{7,0},{8,9},{9,10},{10,1... | collective-permute-start | bytes 737288 | tf_op jit(solution)/shard_map/ppermute | solution.py:61
  159.2 14.1 %collective-permute-start.19 = (bf16[4,3,1,16,768]{4,3,0,1,2:T(8,128)(2,1)S(1)}, bf16[4,3,1,16,768]{4,3,0,1,2:T(8,128)(2,1)S(1)}, u32[]{:S(2)}, u32[]{:S(2)}) collective-permute-start(bf16[4,3,1,16,768]{4,3,0,1,2:T(8,128)(2,1)S(1)} %fusion.35), channel_id=1, source_target_pairs={{0,192},{64,0},{128,64},{192,128},{1,193},{65,1},{129,65},{193,129... | collective-permute-start | bytes 884744 | tf_op jit(solution)/shard_map/ppermute | solution.py:61
  162.2 7.3 %collective-permute-start.11 = (bf16[2,5,1,16,768]{4,3,1,0,2:T(8,128)(2,1)S(1)}, bf16[2,5,1,16,768]{4,3,1,0,2:T(8,128)(2,1)S(1)}, u32[]{:S(2)}, u32[]{:S(2)}) collective-permute-start(bf16[2,5,1,16,768]{4,3,1,0,2:T(8,128)(2,1)S(1)} %fusion.49), channel_id=1, source_target_pairs={{0,7},{1,0},{2,1},{3,2},{4,3},{5,4},{6,5},{7,6},{8,15},{9,8},{10,9... | collective-permute-start | bytes 737288 | tf_op jit(solution)/shard_map/ppermute | solution.py:61
  165.7 7.4 %collective-permute-start.4 = (bf16[2,5,1,16,768]{4,3,1,0,2:T(8,128)(2,1)S(1)}, bf16[2,5,1,16,768]{4,3,1,0,2:T(8,128)(2,1)S(1)}, u32[]{:S(2)}, u32[]{:S(2)}) collective-permute-start(bf16[2,5,1,16,768]{4,3,1,0,2:T(8,128)(2,1)S(1)} %fusion.42), channel_id=1, source_target_pairs={{0,1},{1,2},{2,3},{3,4},{4,5},{5,6},{6,7},{7,0},{8,9},{9,10},{10,1... | collective-permute-start | bytes 737288 | tf_op jit(solution)/shard_map/ppermute | solution.py:61
  169.5 8.2 %collective-permute-start.12 = (bf16[2,5,1,16,768]{4,3,1,0,2:T(8,128)(2,1)S(1)}, bf16[2,5,1,16,768]{4,3,1,0,2:T(8,128)(2,1)S(1)}, u32[]{:S(2)}, u32[]{:S(2)}) collective-permute-start(bf16[2,5,1,16,768]{4,3,1,0,2:T(8,128)(2,1)S(1)} %fusion.48), channel_id=1, source_target_pairs={{0,7},{1,0},{2,1},{3,2},{4,3},{5,4},{6,5},{7,6},{8,15},{9,8},{10,9... | collective-permute-start | bytes 737288 | tf_op jit(solution)/shard_map/ppermute | solution.py:61
  173.2 8.5 %collective-permute-start.5 = (bf16[2,5,1,16,768]{4,3,1,0,2:T(8,128)(2,1)S(1)}, bf16[2,5,1,16,768]{4,3,1,0,2:T(8,128)(2,1)S(1)}, u32[]{:S(2)}, u32[]{:S(2)}) collective-permute-start(bf16[2,5,1,16,768]{4,3,1,0,2:T(8,128)(2,1)S(1)} %fusion.41), channel_id=1, source_target_pairs={{0,1},{1,2},{2,3},{3,4},{4,5},{5,6},{6,7},{7,0},{8,9},{9,10},{10,1... | collective-permute-start | bytes 737288 | tf_op jit(solution)/shard_map/ppermute | solution.py:61
  178.4 9.8 %collective-permute-start.13 = (bf16[2,5,1,16,768]{4,3,1,0,2:T(8,128)(2,1)}, bf16[2,5,1,16,768]{4,3,1,0,2:T(8,128)(2,1)S(1)}, u32[]{:S(2)}, u32[]{:S(2)}) collective-permute-start(bf16[2,5,1,16,768]{4,3,1,0,2:T(8,128)(2,1)} %fusion.47), channel_id=1, source_target_pairs={{0,7},{1,0},{2,1},{3,2},{4,3},{5,4},{6,5},{7,6},{8,15},{9,8},{10,9... | collective-permute-start | bytes 737288 | tf_op jit(solution)/shard_map/ppermute | solution.py:61
  182.5 9.2 %collective-permute-start.6 = (bf16[2,5,1,16,768]{4,3,1,0,2:T(8,128)(2,1)}, bf16[2,5,1,16,768]{4,3,1,0,2:T(8,128)(2,1)}, u32[]{:S(2)}, u32[]{:S(2)}) collective-permute-start(bf16[2,5,1,16,768]{4,3,1,0,2:T(8,128)(2,1)} %fusion.40), channel_id=1, source_target_pairs={{0,1},{1,2},{2,3},{3,4},{4,5},{5,6},{6,7},{7,0},{8,9},{9,10},{10,1... | collective-permute-start | bytes 737288 | tf_op jit(solution)/shard_map/ppermute | solution.py:61
  182.5 13.0 %copy-start.8 = (s32[16,2,2]{0,2,1:T(2,128)S(1)}, s32[16,2,2]{0,2,1:T(2,128)}, u32[]{:S(2)}) copy-start(s32[16,2,2]{0,2,1:T(2,128)} %param.28) | copy-start | bytes 772
  183.4 19.5 %all-to-all-start.1 = ((bf16[8,3,1,16,768]{4,3,1,2,0:T(8,128)(2,1)}), bf16[8,3,1,16,768]{4,3,1,2,0:T(8,128)(2,1)}, u32[]{:S(2)}, u32[]{:S(2)}) async-start(bf16[8,3,1,16,768]{4,3,1,2,0:T(8,128)(2,1)} %copy.239), calls=%async_computation.2 | async-start | bytes 1179648 | tf_op jit(solution)/shard_map/all_to_all | solution.py:78
  188.1 37.7 %reduce-scatter.2.cloned.1.call-start = ((), (), s32[]{:S(2)}) async-start(), calls=%async_computation.4 | async-start | bytes 614400 | tf_op jit(solution)/shard_map/reduce_scatter | solution.py:197
  227.5 13.1 %all-to-all-start.2 = ((bf16[8,1,16,768]{3,2,1,0:T(8,128)(2,1)}), bf16[8,1,16,768]{3,2,1,0:T(8,128)(2,1)S(1)}, u32[]{:S(2)}, u32[]{:S(2)}) async-start(bf16[8,1,16,768]{3,2,1,0:T(8,128)(2,1)} %maximum_bitcast_fusion.1), calls=%async_computation.3 | async-start | bytes 393216 | tf_op jit(solution)/shard_map/all_to_all | solution.py:201
Sparse Core Ops, SparseCore 0:
  30.8 90.1 all-gather.3
  193.8 32.0 reduce-scatter.1
